TPU v7x, 128 devices: a whole 4x4x4 slice. The times are simulated.
128 devices in a mesh: guid: 2 (over x_hi), req: 4 (over x_lo, core), seq: 16 (over y, z).
Axes of the slice: x: 4 (x_hi: 2, x_lo: 2; x = x_hi * 2 + x_lo), y: 4, z: 4, core: 2. Of those that a mesh axis runs over, the one named last changes fastest.
Arguments:
- img_hidden: bfloat16 [2, 24, 1024, 1536], P('guid', 'req', 'seq'), may hold values from -6 to 6
- txt_hidden: bfloat16 [2, 24, 192, 1536], P('guid', 'req', 'seq'), may hold values from -6 to 6
- img_mod: float32 [2, 24, 5, 1536], P('guid', 'req')
- txt_mod: float32 [2, 24, 2, 1536], P('guid', 'req'), may hold values from -3 to 3
- w_img_qkv: bfloat16 [1536, 3072], P(('guid', 'req', 'seq')), may hold values from -0.15625 to 0.15625
- w_txt_qkv: bfloat16 [1536, 3072], P(('guid', 'req', 'seq')), may hold values from -0.15625 to 0.15625
- w_out: bfloat16 [1024, 1536], P(('guid', 'req', 'seq')), may hold values from -0.1875 to 0.1875
- w_head: bfloat16 [1536, 64], P(('guid', 'req', 'seq')), may hold values from -0.15625 to 0.15625
- text_lengths: int32 [2, 24], P('guid', 'req'), may hold values from 1 to 154, as said below
- latent: float32 [24, 1024, 64], P('req', 'seq', 'guid'), may hold values from -6 to 6
- step: int32 [1], replicated, may hold values from 0 to 27
Outputs:
- advanced: float32 [24, 1024, 64], P('req', 'seq', 'guid')
- guided: float32 [24, 1024, 64], P('req', 'seq', 'guid')
Inputs may be any that keep to these rules, and one draw needn't show every extreme that they name: `text_lengths`: in each half one prompt has 154 text tokens and another has 1.
All inputs are finite; a program needn't handle non-finite values.
Results may differ from a plain program's by a relative error of at most 0.012.
The roundings to bfloat16 on the way count: a program that leaves them out, or rounds other values in their place, can miss the bound.
Values may be sent and summed in bfloat16 or wider, within the bound.
No kernel may reach another device: no remote copies, remote signals or barrier semaphores. Data moves between devices by JAX's collectives and lax.ppermute only.
A program may use at most 192 MiB of HBM per device.

v0:
```python
import jax
import jax.numpy as jnp
from jax import lax
from jax.sharding import PartitionSpec as P

HD = 64
STEPS = 28


norm_epsilon = 1e-06
flow_shift = 3.0
guide_scale = 4.5


def partner(value, axis, bit):
    mask = 2**bit
    pairs = [(source, source ^ mask) for source in range(lax.axis_size(axis))]
    return lax.ppermute(value, axis, pairs)


def modulate(values_in, shift_vec, scale_vec):
    values_in = values_in.astype(jnp.float32)
    average = jnp.mean(values_in, axis=-1, keepdims=True)
    variance = jnp.mean((values_in - average) ** 2, axis=-1, keepdims=True)
    normed = (values_in - average) * lax.rsqrt(variance + norm_epsilon)
    return (normed * (1.0 + scale_vec[..., None, :]) + shift_vec[..., None, :]).astype(jnp.bfloat16)


def sigma_level(step_value):
    remaining = 1.0 - step_value / STEPS
    return flow_shift * remaining / (1.0 + (flow_shift - 1.0) * remaining)


def local(
    img_hidden,
    txt_hidden,
    img_mod,
    txt_mod,
    w_img_qkv,
    w_txt_qkv,
    w_out,
    w_head,
    text_lengths,
    latent,
    step,
):
    prompts = img_hidden.shape[1]
    img_rows = img_hidden.shape[2]
    txt_rows = txt_hidden.shape[2]
    dev_rows = img_rows + txt_rows
    model_width = img_hidden.shape[3]
    image_in = modulate(img_hidden[0], img_mod[0, :, 0], img_mod[0, :, 1])
    text_in = modulate(txt_hidden[0], txt_mod[0, :, 0], txt_mod[0, :, 1])
    full_img, full_txt, full_head = (
        lax.all_gather(w_img_qkv, ("guid", "req", "seq"), axis=0, tiled=True),
        lax.all_gather(w_txt_qkv, ("guid", "req", "seq"), axis=0, tiled=True),
        lax.all_gather(w_head, ("guid", "req", "seq"), axis=0, tiled=True),
    )
    attn_width = full_img.shape[1] // 3
    head_count = attn_width // HD
    qkv_image = jnp.einsum(
        "prd,de->pre", image_in, full_img, preferred_element_type=jnp.float32
    ).astype(jnp.bfloat16)
    qkv_text = jnp.einsum(
        "prd,de->pre", text_in, full_txt, preferred_element_type=jnp.float32
    ).astype(jnp.bfloat16)
    query_rows = qkv_image[..., :attn_width]
    key_rows = jnp.concatenate(
        [qkv_image[..., attn_width : 2 * attn_width], qkv_text[..., attn_width : 2 * attn_width]],
        axis=1,
    )
    value_rows = jnp.concatenate(
        [qkv_image[..., 2 * attn_width :], qkv_text[..., 2 * attn_width :]], axis=1
    )
    lengths = text_lengths[0]
    query_heads = query_rows.reshape(prompts, img_rows, head_count, HD)
    running = jnp.full((prompts, head_count, img_rows), -1e30, jnp.float32)
    key_piece = lax.all_gather(key_rows, "seq", axis=1, tiled=True)
    value_piece = lax.all_gather(value_rows, "seq", axis=1, tiled=True)
    piece_rows = key_piece.shape[1]
    key_heads = key_piece.reshape(prompts, piece_rows, head_count, HD)
    value_heads = value_piece.reshape(prompts, piece_rows, head_count, HD)
    scores = (
        jnp.einsum("pqhd,pkhd->phqk", query_heads, key_heads, preferred_element_type=jnp.float32)
        * 0.125
    )
    position = jnp.arange(piece_rows, dtype=jnp.int32)
    owner_dev = position // dev_rows
    offset = position % dev_rows
    text_pos = owner_dev * txt_rows + offset - img_rows
    allowed = (offset < img_rows)[None, :] | (text_pos[None, :] < lengths[:, None])
    scores = jnp.where(allowed[:, None, None, :], scores, -1e30)
    newest = jnp.maximum(running, jnp.max(scores, axis=-1))
    weights = jnp.exp(scores - newest[..., None])
    totals = jnp.sum(weights, axis=-1)
    accumulated = jnp.einsum(
        "phqk,pkhd->phqd",
        weights.astype(jnp.bfloat16),
        value_heads,
        preferred_element_type=jnp.float32,
    )
    running, totals, accumulated = (newest, totals, accumulated)
    mixture = accumulated / totals[..., None]
    attended = (
        jnp.transpose(mixture, (0, 2, 1, 3))
        .reshape(prompts, img_rows, attn_width)
        .astype(jnp.bfloat16)
    )
    flattened = attended.reshape(prompts * img_rows, attn_width)
    full_out = lax.all_gather(w_out, ("guid", "req", "seq"), axis=0, tiled=True)
    projected = jnp.dot(flattened, full_out, preferred_element_type=jnp.float32)
    residual = img_hidden[0].astype(jnp.float32) + img_mod[0, :, 2][:, None, :] * projected.reshape(
        prompts, img_rows, model_width
    )
    final_in = modulate(residual, img_mod[0, :, 3], img_mod[0, :, 4])
    guid_index = lax.axis_index("guid")
    half_width = latent.shape[2]
    own_start = guid_index * half_width
    other_start = (1 - guid_index) * half_width
    whole_velocity = jnp.einsum(
        "prd,dc->prc", final_in, full_head, preferred_element_type=jnp.float32
    )
    own_velocity = lax.dynamic_slice_in_dim(whole_velocity, own_start, half_width, 2)
    partner_part = lax.dynamic_slice_in_dim(whole_velocity, other_start, half_width, 2)
    other_velocity = partner(partner_part.astype(jnp.bfloat16), "guid", 0).astype(
        partner_part.dtype
    )
    cond_velocity = jnp.where(guid_index == 0, own_velocity, other_velocity)
    free_velocity = jnp.where(guid_index == 0, other_velocity, own_velocity)
    guided = free_velocity + guide_scale * (cond_velocity - free_velocity)
    step_value = step[0].astype(jnp.float32)
    advanced = latent + (sigma_level(step_value + 1.0) - sigma_level(step_value)) * guided
    return (advanced, guided)


def solution(mesh):
    placed = (
        P("guid", "req", "seq", None),
        P("guid", "req", "seq", None),
        P("guid", "req", None, None),
        P("guid", "req", None, None),
        P(("guid", "req", "seq"), None),
        P(("guid", "req", "seq"), None),
        P(("guid", "req", "seq"), None),
        P(("guid", "req", "seq"), None),
        P("guid", "req"),
        P("req", "seq", "guid"),
        P(),
    )
    return jax.shard_map(
        local,
        mesh=mesh,
        in_specs=placed,
        out_specs=(P("req", "seq", "guid"), P("req", "seq", "guid")),
        check_vma=False,
    )
```

profile of v0, /device:TPU:0, one launch (start us, length us, event | category | flops | bytes accessed | tf_op | source)
XLA Modules:
  0.0 542.6 jit_solution(7397176703256413804)
XLA Ops:
  8.7 1.1 convert_reduce_fusion.1
  9.8 1.2 fusion.38
  11.0 1.5 convert_reduce_fusion
  13.8 72.9 %all-gather.17.cloned.1.call-done = bf16[128,12,3072]{2,1,0:T(8,128)(2,1)} async-done(((bf16[1,12,3072]{2,1,0:T(8,128)(2,1)}), bf16[128,12,3072]{2,1,0:T(8,128)(2,1)}) %all-gather.17.cloned.1.call-update) | async-done | bytes 9437200 | tf_op jit(solution)/shard_map/all_gather | solution.py:56
  86.7 13.7 %reshape.191 = bf16[1536,3072,1]{1,0,2:T(8,128)(2,1)} reshape(bf16[128,12,3072]{2,1,0:T(8,128)(2,1)} %all-gather.17.cloned.1.call-done) | data formatting | bytes 18874368
  100.4 5.4 %convolution_convert_fusion.1 = bf16[6,12,3072]{2,1,0:T(8,128)(2,1)S(1)} fusion(bf16[1536,3072,1]{1,0,2:T(8,128)(2,1)} %reshape.191, bf16[1,6,12,1536]{3,2,1,0:T(8,128)(2,1)S(1)} %copy-done.1, f32[6,1536]{1,0:T(8,128)S(1)} %get-tuple-element.20, f32[6,1536]{1,0:T(8,128)S(1)} %get-tuple-element.21, f32[6,12]{1,0:T(8,128)S(1)} %add_rsqrt_fusion.1, ...), kind=kOutput, calls=%fused_computation.11 | convolution fusion | flops 680361984 | bytes 10175040 | tf_op jit(solution)/shard_map/prd,de->pre/dot_general | solution.py:64
  106.6 55.7 %all-gather.15.cloned.1.call-done = bf16[128,12,3072]{2,1,0:T(8,128)(2,1)} async-done(((bf16[1,12,3072]{2,1,0:T(8,128)(2,1)}), bf16[128,12,3072]{2,1,0:T(8,128)(2,1)}) %all-gather.15.cloned.1.call-update) | async-done | bytes 9437200 | tf_op jit(solution)/shard_map/all_gather | solution.py:55
  162.3 13.7 %reshape.190 = bf16[1536,3072,1]{1,0,2:T(8,128)(2,1)} reshape(bf16[128,12,3072]{2,1,0:T(8,128)(2,1)} %all-gather.15.cloned.1.call-done) | data formatting | bytes 18874368
  176.0 7.9 %convolution_convert_fusion = bf16[6,64,3072]{2,1,0:T(8,128)(2,1)S(1)} fusion(bf16[1536,3072,1]{1,0,2:T(8,128)(2,1)} %reshape.190, bf16[1,6,64,1536]{3,2,1,0:T(8,128)(2,1)S(1)} %copy-done, f32[6,1536]{1,0:T(8,128)S(1)} %get-tuple-element.25, f32[6,1536]{1,0:T(8,128)S(1)} %get-tuple-element.24, f32[6,64]{1,0:T(8,128)S(1)} %add_rsqrt_fusion.2, ...), kind=kOutput, calls=%fused_computation.10 | convolution fusion | flops 3628597248 | bytes 13052928 | tf_op jit(solution)/shard_map/prd,de->pre/dot_general | solution.py:61
  184.9 1.6 copy.34
  186.7 1.6 copy.31
  189.6 56.3 %all-gather.2 = bf16[128,12,64]{2,1,0:T(8,128)(2,1)S(1)} all-gather(bf16[1,12,64]{2,1,0:T(8,128)(2,1)S(1)} %bitcast.88), channel_id=1, replica_groups=mesh['guid'=2,'req'=4,'seq'=16] {'guid','req','seq'}, dimensions={0}, use_global_device_ids=true | all-gather | bytes 198144 | tf_op jit(solution)/shard_map/all_gather | solution.py:57
  248.6 68.5 %all-gather.11.cloned.1.call-done = bf16[6,1216,1024]{2,0,1:T(8,128)(2,1)} async-done(((bf16[6,76,1024]{2,0,1:T(8,128)(2,1)}), bf16[6,1216,1024]{2,0,1:T(8,128)(2,1)}) %all-gather.11.cloned.1.call-update) | async-done | bytes 14942224 | tf_op jit(solution)/shard_map/all_gather | solution.py:79
  317.1 27.3 %copy.35 = bf16[6,1216,1024]{1,2,0:T(8,128)(2,1)} copy(bf16[6,1216,1024]{2,0,1:T(8,128)(2,1)} %all-gather.11.cloned.1.call-done) | data formatting | bytes 29884416 | tf_op jit(solution)/shard_map/all_gather | solution.py:79
  344.4 100.9 %all-gather.9.cloned.1.call-done = bf16[6,1216,1024]{2,0,1:T(8,128)(2,1)} async-done(((bf16[6,76,1024]{2,0,1:T(8,128)(2,1)}), bf16[6,1216,1024]{2,0,1:T(8,128)(2,1)}) %all-gather.9.cloned.1.call-update) | async-done | bytes 14942224 | tf_op jit(solution)/shard_map/all_gather | solution.py:78
  445.3 26.9 %copy.32 = bf16[6,1216,1024]{1,2,0:T(8,128)(2,1)} copy(bf16[6,1216,1024]{2,0,1:T(8,128)(2,1)} %all-gather.9.cloned.1.call-done) | data formatting | bytes 29884416 | tf_op jit(solution)/shard_map/all_gather | solution.py:78
  472.2 15.9 %fusion = (f32[6,16,64]{2,1,0:T(8,128)S(1)}, f32[6,16,64,1216]{3,2,1,0:T(8,128)}) fusion(pred[6,1216]{1,0:T(8,128)(4,1)S(1)} %compare_or_fusion, bf16[6,1216,16,64]{1,3,2,0:T(8,128)(2,1)} %bitcast.82, bf16[6,64,16,64]{3,2,1,0:T(8,128)(2,1)S(1)} %reshape.170), kind=kOutput, calls=%fused_computation.2 | convolution fusion | flops 978708480 | bytes 45644928 | tf_op jit(solution)/shard_map/pqhd,pkhd->phqk/dot_general | solution.py:84
  488.0 14.0 %fusion.1 = f32[6,16,64]{2,1,0:T(8,128)S(1)} fusion(f32[6,16,64,1216]{3,2,1,0:T(8,128)} %get-tuple-element.17, f32[6,16,64]{2,1,0:T(8,128)S(1)} %broadcast_maximum_fusion, pred[6,1216]{1,0:T(8,128)(4,1)S(1)} %compare_or_fusion), kind=kLoop, calls=%fused_computation.3 | loop fusion | flops 29878272 | bytes 29940864 | tf_op jit(solution)/shard_map/reduce_sum | solution.py:95
  502.1 18.7 %fusion.11 = bf16[6,64,16,64]{3,1,2,0:T(8,128)(2,1)} fusion(bf16[6,1216,16,64]{1,3,2,0:T(8,128)(2,1)} %bitcast.83, f32[6,16,64,1216]{3,2,1,0:T(8,128)} %get-tuple-element.17, f32[6,16,64]{2,1,0:T(8,128)S(1)} %broadcast_maximum_fusion, pred[6,1216]{1,0:T(8,128)(4,1)S(1)} %compare_or_fusion, f32[6,64,16]{1,2,0:T(8,128)S(1)} %bitcast.87), kind=kOutput, calls=%fused_computation.15 | convolution fusion | flops 986972160 | bytes 45669504 | tf_op jit(solution)/shard_map/phqk,pkhd->phqd/dot_general | solution.py:96
  520.8 2.4 copy.36
  523.2 1.1 convert_element_type.60
  524.4 3.4 fusion.70
  529.6 3.0 collective-permute-start
  533.4 1.9 collective-permute-done
  (68 shorter events, 11.2 us)
Async XLA Ops:
  7.2 5.4 copy-start
  7.2 5.8 %copy-start.10 = (f32[1,6,2,1536]{3,2,1,0:T(2,128)S(1)}, f32[1,6,2,1536]{3,2,1,0:T(2,128)}, u32[]{:S(2)}) copy-start(f32[1,6,2,1536]{3,2,1,0:T(2,128)} %param.14) | copy-start | bytes 221188
  7.2 5.9 %copy-start.5 = (f32[1,6,5,1536]{3,0,2,1:T(1,128)S(1)}, f32[1,6,5,1536]{3,0,2,1:T(1,128)}, u32[]{:S(2)}) copy-start(f32[1,6,5,1536]{3,0,2,1:T(1,128)} %param.13) | copy-start | bytes 552964
  7.2 79.5 %all-gather.17.cloned.1.call-start = ((), (), s32[]{:S(2)}) async-start(), calls=%async_computation.4 | async-start | bytes 12681216 | tf_op jit(solution)/shard_map/all_gather | solution.py:56
  7.9 154.4 %all-gather.15.cloned.1.call-start = ((), (), s32[]{:S(2)}) async-start(), calls=%async_computation.3 | async-start | bytes 12681216 | tf_op jit(solution)/shard_map/all_gather | solution.py:55
  8.7 308.4 %all-gather.11.cloned.1.call-start = ((), (), s32[]{:S(2)}) async-start(), calls=%async_computation.1 | async-start | bytes 21168128 | tf_op jit(solution)/shard_map/all_gather | solution.py:79
  13.8 86.6 %copy-start.1 = (bf16[1,6,12,1536]{3,2,1,0:T(8,128)(2,1)S(1)}, bf16[1,6,12,1536]{3,2,1,0:T(8,128)(2,1)}, u32[]{:S(2)}) copy-start(bf16[1,6,12,1536]{3,2,1,0:T(8,128)(2,1)} %param.12) | copy-start | bytes 663556
  183.9 0.9 copy-start.3
  184.9 1.7 copy-start.2
  186.5 258.8 %all-gather.9.cloned.1.call-start = ((), (), s32[]{:S(2)}) async-start(), calls=%async_computation | async-start | bytes 21168128 | tf_op jit(solution)/shard_map/all_gather | solution.py:78
  186.6 2.4 copy-start.8
  186.6 3.0 copy-start.13
  186.7 60.1 %copy-start.6 = (f32[1,6,1,1536]{3,0,2,1:T(1,128)S(1)}, f32[1,6,1,1536]{3,0,2,1:T(1,128)}, u32[]{:S(2)}) copy-start(f32[1,6,1,1536]{3,0,2,1:T(1,128)} %get-tuple-element.9) | copy-start | bytes 110596
  186.7 60.1 %copy-start.7 = (f32[1,6,1,1536]{3,0,2,1:T(1,128)S(1)}, f32[1,6,1,1536]{3,0,2,1:T(1,128)}, u32[]{:S(2)}) copy-start(f32[1,6,1,1536]{3,0,2,1:T(1,128)} %get-tuple-element.12) | copy-start | bytes 110596
  186.7 60.8 %copy-start.14 = (s32[1,6]{1,0:T(1,128)S(1)}, s32[1,6]{1,0:T(1,128)}, u32[]{:S(2)}) copy-start(s32[1,6]{1,0:T(1,128)} %param.19) | copy-start | bytes 76
  188.3 336.0 %all-gather.13.cloned.1.call-start = ((), (), s32[]{:S(2)}) async-start(), calls=%async_computation.2 | async-start | bytes 3170304 | tf_op jit(solution)/shard_map/all_gather | solution.py:110
  527.7 1.0 copy-start.4
  527.7 1.0 copy-start.11
  527.8 1.0 copy-start.12
  527.8 7.5 %copy-start.9 = (f32[6,64,32]{1,2,0:T(8,128)S(1)}, f32[6,64,32]{1,2,0:T(8,128)}, u32[]{:S(2)}) copy-start(f32[6,64,32]{1,2,0:T(8,128)} %param.20) | copy-start | bytes 147460
  529.6 5.7 %collective-permute-start = (bf16[6,64,32]{1,2,0:T(8,128)(2,1)S(1)}, bf16[6,64,32]{1,2,0:T(8,128)(2,1)S(1)}, u32[]{:S(2)}, u32[]{:S(2)}) collective-permute-start(bf16[6,64,32]{1,2,0:T(8,128)(2,1)S(1)} %dynamic-slice_convert_fusion), channel_id=1, source_target_pairs={{0,64},{64,0},{1,65},{65,1},{2,66},{66,2},{3,67},{67,3},{4,68},{68... | collective-permute-start | bytes 73736 | tf_op jit(solution)/shard_map/ppermute | solution.py:18
Sparse Core Ops, SparseCore 0:
  11.1 75.5 all-gather.16
  89.7 72.5 all-gather.14
  186.6 130.4 all-gather.10
  319.1 126.1 all-gather.8
  448.2 65.3 all-gather.12
where the time goes:
time: 545 us; the launch traced here: 543 us
  waiting for transfers between devices  302 us (55%)
  local copies, waits for them, and re-layouts  93.9 us (17%)
  blocking collectives  56.3 us (10%)
  matrix products  52.2 us (10%)
  other arithmetic  20.3 us (4%)
  between operations  14.9 us (3%)
    all_gather x1, waiting for transfers between devices, local(): key_piece = lax.all_gather(key_rows, 'seq', axis=1, tiled=True)  101 us
    all_gather x1, waiting for transfers between devices, local(): lax.all_gather(w_txt_qkv, ('guid', 'req', 'seq'), axis=0, tiled=True)  72.9 us
    all_gather x1, waiting for transfers between devices, local(): value_piece = lax.all_gather(value_rows, 'seq', axis=1, tiled=True)  68.5 us
    all_gather x1, blocking collectives, local(): lax.all_gather(w_head, ('guid', 'req', 'seq'), axis=0, tiled=True)  56.3 us
    all_gather x1, waiting for transfers between devices, local(): lax.all_gather(w_img_qkv, ('guid', 'req', 'seq'), axis=0, tiled=True)  55.7 us
    unnamed x34, local copies, waits for them, and re-layouts  30.3 us
    all_gather x1, local copies, waits for them, and re-layouts, local(): value_piece = lax.all_gather(value_rows, 'seq', axis=1, tiled=True)  27.3 us
    all_gather x1, local copies, waits for them, and re-layouts, local(): key_piece = lax.all_gather(key_rows, 'seq', axis=1, tiled=True)  26.9 us
  transfers between devices with their start and end apart: 6, of which 5 were waited for; matrix products, arithmetic and copies ran while one was open for 25% of the time, Pallas kernels for 0%

commit v1 on v0

--- a/solution.py
+++ b/solution.py
@@ -44,71 +44,71 @@
     latent,
     step,
 ):
+    all_axes = ("guid", "req", "seq")
     prompts = img_hidden.shape[1]
     img_rows = img_hidden.shape[2]
     txt_rows = txt_hidden.shape[2]
-    dev_rows = img_rows + txt_rows
     model_width = img_hidden.shape[3]
+    nseq = lax.axis_size("seq")
+
+    full_img = lax.all_gather(w_img_qkv, all_axes, axis=0, tiled=True)
+    full_txt = lax.all_gather(w_txt_qkv, all_axes, axis=0, tiled=True)
+    head_rows, head_cols = w_head.shape
+    full_head = lax.all_gather(
+        w_head.reshape(1, head_rows * head_cols), all_axes, axis=0, tiled=True
+    ).reshape(-1, head_cols)
+    full_out = lax.all_gather(w_out, all_axes, axis=0, tiled=True)
+
     image_in = modulate(img_hidden[0], img_mod[0, :, 0], img_mod[0, :, 1])
     text_in = modulate(txt_hidden[0], txt_mod[0, :, 0], txt_mod[0, :, 1])
-    full_img, full_txt, full_head = (
-        lax.all_gather(w_img_qkv, ("guid", "req", "seq"), axis=0, tiled=True),
-        lax.all_gather(w_txt_qkv, ("guid", "req", "seq"), axis=0, tiled=True),
-        lax.all_gather(w_head, ("guid", "req", "seq"), axis=0, tiled=True),
-    )
     attn_width = full_img.shape[1] // 3
     head_count = attn_width // HD
+    per_dev = head_count // nseq
     qkv_image = jnp.einsum(
         "prd,de->pre", image_in, full_img, preferred_element_type=jnp.float32
     ).astype(jnp.bfloat16)
     qkv_text = jnp.einsum(
         "prd,de->pre", text_in, full_txt, preferred_element_type=jnp.float32
     ).astype(jnp.bfloat16)
-    query_rows = qkv_image[..., :attn_width]
-    key_rows = jnp.concatenate(
-        [qkv_image[..., attn_width : 2 * attn_width], qkv_text[..., attn_width : 2 * attn_width]],
-        axis=1,
-    )
-    value_rows = jnp.concatenate(
-        [qkv_image[..., 2 * attn_width :], qkv_text[..., 2 * attn_width :]], axis=1
-    )
+
+    img_split = qkv_image.reshape(prompts, img_rows, 3, nseq, per_dev * HD)
+    img_heads = lax.all_to_all(img_split, "seq", 3, 1, tiled=True)
+    txt_split = qkv_text[..., attn_width:].reshape(prompts, txt_rows, 2, nseq, per_dev * HD)
+    txt_heads = lax.all_to_all(txt_split, "seq", 3, 1, tiled=True)
+    all_img = img_heads.shape[1]
+    all_txt = txt_heads.shape[1]
+
+    query_heads = img_heads[:, :, 0, 0].reshape(prompts, all_img, per_dev, HD)
+    key_heads = jnp.concatenate(
+        [img_heads[:, :, 1, 0], txt_heads[:, :, 0, 0]], axis=1
+    ).reshape(prompts, all_img + all_txt, per_dev, HD)
+    value_heads = jnp.concatenate(
+        [img_heads[:, :, 2, 0], txt_heads[:, :, 1, 0]], axis=1
+    ).reshape(prompts, all_img + all_txt, per_dev, HD)
+
     lengths = text_lengths[0]
-    query_heads = query_rows.reshape(prompts, img_rows, head_count, HD)
-    running = jnp.full((prompts, head_count, img_rows), -1e30, jnp.float32)
-    key_piece = lax.all_gather(key_rows, "seq", axis=1, tiled=True)
-    value_piece = lax.all_gather(value_rows, "seq", axis=1, tiled=True)
-    piece_rows = key_piece.shape[1]
-    key_heads = key_piece.reshape(prompts, piece_rows, head_count, HD)
-    value_heads = value_piece.reshape(prompts, piece_rows, head_count, HD)
     scores = (
         jnp.einsum("pqhd,pkhd->phqk", query_heads, key_heads, preferred_element_type=jnp.float32)
         * 0.125
     )
-    position = jnp.arange(piece_rows, dtype=jnp.int32)
-    owner_dev = position // dev_rows
-    offset = position % dev_rows
-    text_pos = owner_dev * txt_rows + offset - img_rows
-    allowed = (offset < img_rows)[None, :] | (text_pos[None, :] < lengths[:, None])
+    position = jnp.arange(all_img + all_txt, dtype=jnp.int32)
+    allowed = (position < all_img)[None, :] | ((position - all_img)[None, :] < lengths[:, None])
     scores = jnp.where(allowed[:, None, None, :], scores, -1e30)
-    newest = jnp.maximum(running, jnp.max(scores, axis=-1))
-    weights = jnp.exp(scores - newest[..., None])
+    highest = jnp.max(scores, axis=-1)
+    weights = jnp.exp(scores - highest[..., None])
     totals = jnp.sum(weights, axis=-1)
     accumulated = jnp.einsum(
-        "phqk,pkhd->phqd",
+        "phqk,pkhd->pqhd",
         weights.astype(jnp.bfloat16),
         value_heads,
         preferred_element_type=jnp.float32,
     )
-    running, totals, accumulated = (newest, totals, accumulated)
-    mixture = accumulated / totals[..., None]
-    attended = (
-        jnp.transpose(mixture, (0, 2, 1, 3))
-        .reshape(prompts, img_rows, attn_width)
-        .astype(jnp.bfloat16)
-    )
-    flattened = attended.reshape(prompts * img_rows, attn_width)
-    full_out = lax.all_gather(w_out, ("guid", "req", "seq"), axis=0, tiled=True)
-    projected = jnp.dot(flattened, full_out, preferred_element_type=jnp.float32)
+    mixture = accumulated / jnp.transpose(totals, (0, 2, 1))[..., None]
+    head_out = mixture.astype(jnp.bfloat16).reshape(prompts, all_img, 1, per_dev * HD)
+    token_out = lax.all_to_all(head_out, "seq", 1, 2, tiled=True)
+    attended = token_out.reshape(prompts * img_rows, attn_width)
+
+    projected = jnp.dot(attended, full_out, preferred_element_type=jnp.float32)
     residual = img_hidden[0].astype(jnp.float32) + img_mod[0, :, 2][:, None, :] * projected.reshape(
         prompts, img_rows, model_width
     )

time: 545 us -> 417 us (0.77)
  waiting for transfers between devices: 302 us -> 150 us
  starting transfers between devices: 3.24 us -> 18.9 us
  blocking collectives: 56.3 us -> 68.7 us
  matrix products: 52.2 us -> 42.3 us
    all_gather x5 -> x3, waiting for transfers between devices: 298 us -> 120 us  [the longest x1 72.3 us: local(): full_txt = lax.all_gather(w_txt_qkv, all_axes, axis=0, tiled=True)]
    all_gather x2 -> x0, local copies, waits for them, and re-layouts: 54.2 us -> none  [the longest x1 27.3 us: local(): value_piece = lax.all_gather(value_rows, 'seq', axis=1, tiled=True)]
    unnamed x34 -> x38, local copies, waits for them, and re-layouts: 30.3 us -> 54.8 us
    all_to_all x0 -> x6, local copies, waits for them, and re-layouts: none -> 23.7 us  [the longest x3 19.7 us: local(): img_heads = lax.all_to_all(img_split, 'seq', 3, 1, tiled=True)]
    all_to_all x0 -> x3, waiting for transfers between devices: none -> 23.2 us  [the longest x1 23.2 us: local(): img_heads = lax.all_to_all(img_split, 'seq', 3, 1, tiled=True)]
    all_to_all x0 -> x3, starting transfers between devices: none -> 18.5 us  [the longest x1 6.67 us: local(): img_heads = lax.all_to_all(img_split, 'seq', 3, 1, tiled=True)]
    all_gather x1, blocking collectives: 56.3 us -> 68.7 us  [local(): lax.all_gather(w_head.reshape(1, head_rows * head_cols), all_axes, axis=0...]
    reshape x1 -> x5, local copies, waits for them, and re-layouts: 1.02 us -> 12.6 us  [the longest x2 10.5 us: local(): img_split = qkv_image.reshape(prompts, img_rows, 3, nseq, per_dev * HD)]
  transfers between devices with their start and end apart: 6 -> 7, of which waited for: 5 -> 4; matrix products, arithmetic and copies ran while one was open for 25% -> 36% of each run, Pallas kernels for 0% -> 0%
where the time goes in v1:
time: 417 us; the launch traced here: 415 us
  waiting for transfers between devices  150 us (36%)
  local copies, waits for them, and re-layouts  99.3 us (24%)
  blocking collectives  68.7 us (16%)
  matrix products  42.3 us (10%)
  other arithmetic  21.2 us (5%)
  starting transfers between devices  18.9 us (5%)
  between operations  14.9 us (4%)
    all_gather x1, waiting for transfers between devices, local(): full_txt = lax.all_gather(w_txt_qkv, all_axes, axis=0, tiled=True)  72.3 us
    all_gather x1, blocking collectives, local(): lax.all_gather(w_head.reshape(1, head_rows * head_cols), all_axes, axis=0...  68.7 us
    unnamed x38, local copies, waits for them, and re-layouts  54.8 us
    all_gather x1, waiting for transfers between devices, local(): full_img = lax.all_gather(w_img_qkv, all_axes, axis=0, tiled=True)  47.7 us
    all_to_all x1, waiting for transfers between devices, local(): img_heads = lax.all_to_all(img_split, 'seq', 3, 1, tiled=True)  23.2 us
    all_to_all x3, local copies, waits for them, and re-layouts, local(): img_heads = lax.all_to_all(img_split, 'seq', 3, 1, tiled=True)  19.7 us
    reduce_sum x1, other arithmetic, local(): totals = jnp.sum(weights, axis=-1)  13.9 us
    dot_general x1, matrix products, local(): jnp.einsum('phqk,pkhd->pqhd', weights.astype(jnp.bfloat16), value_heads,...  13.4 us
  transfers between devices with their start and end apart: 7, of which 4 were waited for; matrix products, arithmetic and copies ran while one was open for 36% of the time, Pallas kernels for 0%

profile of v1, /device:TPU:0, one launch (start us, length us, event | category | flops | bytes accessed | tf_op | source)
XLA Modules:
  0.0 415.2 jit_solution(12379703206547483496)
XLA Ops:
  14.4 72.3 %all-gather.11.cloned.1.call-done = bf16[128,12,3072]{2,1,0:T(8,128)(2,1)} async-done(((bf16[1,12,3072]{2,1,0:T(8,128)(2,1)}), bf16[128,12,3072]{2,1,0:T(8,128)(2,1)}) %all-gather.11.cloned.1.call-update) | async-done | bytes 9437200 | tf_op jit(solution)/shard_map/all_gather | solution.py:55
  86.7 13.7 %reshape.207 = bf16[1536,3072,1]{1,0,2:T(8,128)(2,1)} reshape(bf16[128,12,3072]{2,1,0:T(8,128)(2,1)} %all-gather.11.cloned.1.call-done) | data formatting | bytes 18874368
  100.4 5.4 %fusion.48 = bf16[6,12,3072]{2,1,0:T(8,128)(2,1)S(1)} fusion(bf16[1536,3072,1]{1,0,2:T(8,128)(2,1)} %reshape.207, bf16[1,6,12,1536]{3,2,1,0:T(8,128)(2,1)S(1)} %copy-done.1, f32[6,1536]{1,0:T(8,128)S(1)} %get-tuple-element.19, f32[6,1536]{1,0:T(8,128)S(1)} %get-tuple-element.20, f32[6,12]{1,0:T(8,128)S(1)} %add_rsqrt_fusion.1, ...), kind=kOutput, calls=%fused_computation.53 | convolution fusion | flops 680140800 | bytes 10175040 | tf_op jit(solution)/shard_map/prd,de->pre/dot_general | solution.py:70
  108.0 6.6 %all-to-all-start.1 = ((bf16[16,2,4608]{2,1,0:T(2,128)(2,1)}), bf16[16,2,4608]{2,1,0:T(2,128)(2,1)}, u32[]{:S(2)}, u32[]{:S(2)}) async-start(bf16[16,2,4608]{2,1,0:T(2,128)(2,1)} %reshape.213), calls=%async_computation.1 | async-start | bytes 589824 | tf_op jit(solution)/shard_map/all_to_all | solution.py:77
  114.6 47.7 %all-gather.9.cloned.1.call-done = bf16[128,12,3072]{2,1,0:T(8,128)(2,1)} async-done(((bf16[1,12,3072]{2,1,0:T(8,128)(2,1)}), bf16[128,12,3072]{2,1,0:T(8,128)(2,1)}) %all-gather.9.cloned.1.call-update) | async-done | bytes 9437200 | tf_op jit(solution)/shard_map/all_gather | solution.py:54
  162.3 13.7 %reshape.206 = bf16[1536,3072,1]{1,0,2:T(8,128)(2,1)} reshape(bf16[128,12,3072]{2,1,0:T(8,128)(2,1)} %all-gather.9.cloned.1.call-done) | data formatting | bytes 18874368
  176.0 8.2 %convolution_convert_fusion = bf16[6,64,3072]{2,1,0:T(8,128)(2,1)S(1)} fusion(bf16[1536,3072,1]{1,0,2:T(8,128)(2,1)} %reshape.206, bf16[1,6,64,1536]{3,2,1,0:T(8,128)(2,1)S(1)} %copy-done, f32[6,1536]{1,0:T(8,128)} %get-tuple-element.24, f32[6,1536]{1,0:T(8,128)} %get-tuple-element.23, f32[6,64]{1,0:T(8,128)S(1)} %add_rsqrt_fusion.2, ...), kind=kOutput, calls=%fused_computation.7 | convolution fusion | flops 3628597248 | bytes 13052928 | tf_op jit(solution)/shard_map/prd,de->pre/dot_general | solution.py:67
  184.2 4.8 %reshape.182 = bf16[6,64,3,16,64]{4,3,2,1,0:T(8,128)(2,1)} reshape(bf16[6,64,3072]{2,1,0:T(8,128)(2,1)S(1)} %convolution_convert_fusion) | data formatting | bytes 4718592 | tf_op jit(solution)/shard_map/reshape | solution.py:74
  189.0 5.7 %copy.84 = bf16[6,64,3,16,64]{4,1,2,0,3:T(8,128)(2,1)} copy(bf16[6,64,3,16,64]{4,3,2,1,0:T(8,128)(2,1)} %reshape.182) | data formatting | bytes 4718592 | tf_op jit(solution)/shard_map/reshape | solution.py:74
  194.7 7.8 %reshape.215 = bf16[16,2,36864]{2,1,0:T(2,128)(2,1)} reshape(bf16[16,6,3,64,64]{4,3,2,1,0:T(8,128)(2,1)} %bitcast.122) | data formatting | bytes 4718592
  202.6 6.7 %all-to-all-start = ((bf16[16,2,36864]{2,1,0:T(2,128)(2,1)}), bf16[16,2,36864]{2,1,0:T(2,128)(2,1)S(1)}, u32[]{:S(2)}, u32[]{:S(2)}) async-start(bf16[16,2,36864]{2,1,0:T(2,128)(2,1)} %reshape.215), calls=%async_computation | async-start | bytes 4718592 | tf_op jit(solution)/shard_map/all_to_all | solution.py:75
  220.0 23.2 %all-to-all-done = bf16[16,2,36864]{2,1,0:T(2,128)(2,1)S(1)} async-done(((bf16[16,2,36864]{2,1,0:T(2,128)(2,1)}), bf16[16,2,36864]{2,1,0:T(2,128)(2,1)S(1)}, u32[]{:S(2)}, u32[]{:S(2)}) %all-to-all-start) | async-done | bytes 2359328 | tf_op jit(solution)/shard_map/all_to_all | solution.py:75
  243.1 5.4 %reshape.216 = bf16[16,6,3,64,64]{4,3,2,1,0:T(8,128)(2,1)} reshape(bf16[16,2,36864]{2,1,0:T(2,128)(2,1)S(1)} %all-to-all-done) | data formatting | bytes 4718592
  248.5 6.1 %bitcast_bitcast_fusion = bf16[6,16,64,3,1,64]{5,2,3,0,1,4:T(8,128)(2,1)} fusion(bf16[16,6,3,64,64]{4,3,2,1,0:T(8,128)(2,1)} %reshape.216), kind=kLoop, calls=%fused_computation.92 | loop fusion | bytes 4718592 | tf_op jit(solution)/shard_map/all_to_all | solution.py:75
  254.6 7.3 %copy.44 = bf16[6,16,64,3,1,64]{2,1,5,0,3,4:T(8,128)(2,1)} copy(bf16[6,16,64,3,1,64]{5,2,3,0,1,4:T(8,128)(2,1)} %bitcast_bitcast_fusion) | data formatting | bytes 4718592 | tf_op jit(solution)/shard_map/all_to_all | solution.py:75
  261.9 6.3 %all_to_all.40 = bf16[6,1024,3,1,64]{1,4,0,3,2:T(8,128)(2,1)S(1)} reshape(bf16[6,16,64,3,1,64]{2,1,5,0,3,4:T(8,128)(2,1)} %copy.44) | data formatting | bytes 4718592 | tf_op jit(solution)/shard_map/all_to_all | solution.py:75
  269.1 11.0 %fusion = (f32[6,1024]{1,0:T(8,128)S(1)}, f32[6,1024,1216]{1,2,0:T(8,128)}) fusion(pred[6,1216]{1,0:T(8,128)(4,1)S(1)} %compare_or_fusion, bf16[6,192,64]{1,2,0:T(8,128)(2,1)S(1)} %bitcast.128, bf16[6,1024,64]{1,2,0:T(8,128)(2,1)S(1)} %get-tuple-element.5, bf16[6,1024,3,1,64]{1,4,0,3,2:T(8,128)(2,1)S(1)} %all_to_all.40), kind=kOutput, calls=%fused_computation.2 | convolution fusion | flops 980576256 | bytes 31688704 | tf_op jit(solution)/shard_map/pqhd,pkhd->phqk/dot_general | solution.py:91
  280.1 13.9 %fusion.1 = f32[6,1024]{1,0:T(8,128)S(1)} fusion(f32[6,1024,1216]{1,2,0:T(8,128)} %get-tuple-element.16, f32[6,1024]{1,0:T(8,128)S(1)} %get-tuple-element.15, pred[6,1216]{1,0:T(8,128)(4,1)S(1)} %compare_or_fusion), kind=kLoop, calls=%fused_computation.3 | loop fusion | flops 29878272 | bytes 29940864 | tf_op jit(solution)/shard_map/reduce_sum | solution.py:99
  294.1 13.4 %fusion.24 = bf16[6,1024,1,64]{1,3,0,2:T(8,128)(2,1)} fusion(f32[6,1024,1216]{1,2,0:T(8,128)} %get-tuple-element.16, f32[6,1024]{1,0:T(8,128)S(1)} %get-tuple-element.15, pred[6,1216]{1,0:T(8,128)(4,1)S(1)} %compare_or_fusion, bf16[6,192,64]{1,2,0:T(8,128)(2,1)S(1)} %bitcast.129, bf16[6,1024,64]{1,2,0:T(8,128)(2,1)S(1)} %get-tuple-element.4, ...), kind=kOutput, calls=%fused_computation.26 | convolution fusion | flops 988839936 | bytes 31661184 | tf_op jit(solution)/shard_map/phqk,pkhd->pqhd/dot_general | solution.py:100
  312.3 5.2 %all-to-all-start.2 = ((bf16[16,2,12288]{2,1,0:T(2,128)(2,1)}), bf16[16,2,12288]{2,1,0:T(2,128)(2,1)}, u32[]{:S(2)}, u32[]{:S(2)}) async-start(bf16[16,2,12288]{2,1,0:T(2,128)(2,1)} %reshape.217), calls=%async_computation.2 | async-start | bytes 1572864 | tf_op jit(solution)/shard_map/all_to_all | solution.py:108
  317.7 68.7 %all-gather.2 = bf16[128,1,768]{2,1,0:T(2,128)(2,1)S(1)} all-gather(bf16[1,1,768]{2,1,0:T(2,128)(2,1)S(1)} %reshape.202), channel_id=1, replica_groups=mesh['guid'=2,'req'=4,'seq'=16] {'guid','req','seq'}, dimensions={0}, use_global_device_ids=true | all-gather | bytes 198144 | tf_op jit(solution)/shard_map/all_gather | solution.py:57
  388.6 3.5 reshape.218
  397.0 3.4 fusion.68
  403.1 4.8 %collective-permute-done = bf16[6,64,32]{1,2,0:T(8,128)(2,1)S(1)} collective-permute-done((bf16[6,64,32]{1,2,0:T(8,128)(2,1)S(1)}, bf16[6,64,32]{1,2,0:T(8,128)(2,1)S(1)}, u32[]{:S(2)}, u32[]{:S(2)}) %collective-permute-start) | collective-permute-done | bytes 24608 | tf_op jit(solution)/shard_map/ppermute | solution.py:18
  (77 shorter events, 35.4 us)
Async XLA Ops:
  7.2 5.3 %copy-start = (bf16[1,6,64,1536]{3,2,1,0:T(8,128)(2,1)S(1)}, bf16[1,6,64,1536]{3,2,1,0:T(8,128)(2,1)}, u32[]{:S(2)}) copy-start(bf16[1,6,64,1536]{3,2,1,0:T(8,128)(2,1)} %param.11) | copy-start | bytes 3538948
  7.2 5.8 %copy-start.10 = (f32[1,6,2,1536]{3,2,1,0:T(2,128)S(1)}, f32[1,6,2,1536]{3,2,1,0:T(2,128)}, u32[]{:S(2)}) copy-start(f32[1,6,2,1536]{3,2,1,0:T(2,128)} %param.14) | copy-start | bytes 221188
  7.2 5.8 %copy-start.5 = (f32[1,6,5,1536]{3,0,2,1:T(1,128)S(1)}, f32[1,6,5,1536]{3,0,2,1:T(1,128)}, u32[]{:S(2)}) copy-start(f32[1,6,5,1536]{3,0,2,1:T(1,128)} %param.13) | copy-start | bytes 552964
  7.2 79.5 %all-gather.11.cloned.1.call-start = ((), (), s32[]{:S(2)}) async-start(), calls=%async_computation.5 | async-start | bytes 12681216 | tf_op jit(solution)/shard_map/all_gather | solution.py:55
  7.9 154.4 %all-gather.9.cloned.1.call-start = ((), (), s32[]{:S(2)}) async-start(), calls=%async_computation.4 | async-start | bytes 12681216 | tf_op jit(solution)/shard_map/all_gather | solution.py:54
  14.4 86.0 %copy-start.1 = (bf16[1,6,12,1536]{3,2,1,0:T(8,128)(2,1)S(1)}, bf16[1,6,12,1536]{3,2,1,0:T(8,128)(2,1)}, u32[]{:S(2)}) copy-start(bf16[1,6,12,1536]{3,2,1,0:T(8,128)(2,1)} %param.12) | copy-start | bytes 663556
  108.0 94.6 %all-to-all-start.1 = ((bf16[16,2,4608]{2,1,0:T(2,128)(2,1)}), bf16[16,2,4608]{2,1,0:T(2,128)(2,1)}, u32[]{:S(2)}, u32[]{:S(2)}) async-start(bf16[16,2,4608]{2,1,0:T(2,128)(2,1)} %reshape.213), calls=%async_computation.1 | async-start | bytes 589824 | tf_op jit(solution)/shard_map/all_to_all | solution.py:77
  202.6 7.4 %copy-start.12 = (s32[1,6]{1,0:T(1,128)S(1)}, s32[1,6]{1,0:T(1,128)}, u32[]{:S(2)}) copy-start(s32[1,6]{1,0:T(1,128)} %param.19) | copy-start | bytes 76
  202.6 40.5 %all-to-all-start = ((bf16[16,2,36864]{2,1,0:T(2,128)(2,1)}), bf16[16,2,36864]{2,1,0:T(2,128)(2,1)S(1)}, u32[]{:S(2)}, u32[]{:S(2)}) async-start(bf16[16,2,36864]{2,1,0:T(2,128)(2,1)} %reshape.215), calls=%async_computation | async-start | bytes 4718592 | tf_op jit(solution)/shard_map/all_to_all | solution.py:75
  209.3 187.7 %all-gather.7.cloned.1.call-start = ((), (), s32[]{:S(2)}) async-start(), calls=%async_computation.3 | async-start | bytes 3170304 | tf_op jit(solution)/shard_map/all_gather | solution.py:60
  268.2 0.9 copy-start.2
  280.1 14.0 %copy-start.4 = (bf16[6,192,1,1,64]{1,4,0,3,2:T(8,128)(2,1)S(1)}, bf16[6,192,1,1,64]{1,4,0,3,2:T(8,128)(2,1)}, u32[]{:S(2)}) copy-start(bf16[6,192,1,1,64]{1,4,0,3,2:T(8,128)(2,1)} %copy.63) | copy-start | bytes 442372
  310.1 7.5 %copy-start.8 = (f32[1,6,1,1536]{3,0,2,1:T(1,128)S(1)}, f32[1,6,1,1536]{3,0,2,1:T(1,128)}, u32[]{:S(2)}) copy-start(f32[1,6,1,1536]{3,0,2,1:T(1,128)} %get-tuple-element.10) | copy-start | bytes 110596
  310.1 7.5 %copy-start.11 = (bf16[12,64]{1,0:T(8,128)(2,1)S(1)}, bf16[12,64]{1,0:T(8,128)(2,1)}, u32[]{:S(2)}) copy-start(bf16[12,64]{1,0:T(8,128)(2,1)} %param.18) | copy-start | bytes 4612
  310.1 78.5 %copy-start.6 = (f32[1,6,1,1536]{3,0,2,1:T(1,128)S(1)}, f32[1,6,1,1536]{3,0,2,1:T(1,128)}, u32[]{:S(2)}) copy-start(f32[1,6,1,1536]{3,0,2,1:T(1,128)} %get-tuple-element.8) | copy-start | bytes 110596
  310.1 78.5 %copy-start.7 = (f32[1,6,1,1536]{3,0,2,1:T(1,128)S(1)}, f32[1,6,1,1536]{3,0,2,1:T(1,128)}, u32[]{:S(2)}) copy-start(f32[1,6,1,1536]{3,0,2,1:T(1,128)} %get-tuple-element.11) | copy-start | bytes 110596
  312.3 76.3 %all-to-all-start.2 = ((bf16[16,2,12288]{2,1,0:T(2,128)(2,1)}), bf16[16,2,12288]{2,1,0:T(2,128)(2,1)}, u32[]{:S(2)}, u32[]{:S(2)}) async-start(bf16[16,2,12288]{2,1,0:T(2,128)(2,1)} %reshape.217), calls=%async_computation.2 | async-start | bytes 1572864 | tf_op jit(solution)/shard_map/all_to_all | solution.py:108
  400.4 1.0 copy-start.3
  400.4 7.6 %copy-start.9 = (f32[6,64,32]{1,2,0:T(8,128)S(1)}, f32[6,64,32]{1,2,0:T(8,128)}, u32[]{:S(2)}) copy-start(f32[6,64,32]{1,2,0:T(8,128)} %param.20) | copy-start | bytes 147460
  402.3 5.7 %collective-permute-start = (bf16[6,64,32]{1,2,0:T(8,128)(2,1)S(1)}, bf16[6,64,32]{1,2,0:T(8,128)(2,1)S(1)}, u32[]{:S(2)}, u32[]{:S(2)}) collective-permute-start(bf16[6,64,32]{1,2,0:T(8,128)(2,1)S(1)} %dynamic-slice_convert_fusion), channel_id=1, source_target_pairs={{0,64},{64,0},{1,65},{65,1},{2,66},{66,2},{3,67},{67,3},{4,68},{68... | collective-permute-start | bytes 73736 | tf_op jit(solution)/shard_map/ppermute | solution.py:18
Sparse Core Ops, SparseCore 0:
  11.1 75.5 all-gather.10
  89.7 72.5 all-gather.8
  213.2 73.6 all-gather.6

commit v2 on v1

--- a/solution.py
+++ b/solution.py
@@ -31,6 +31,16 @@
     return flow_shift * remaining / (1.0 + (flow_shift - 1.0) * remaining)
 
 
+def permute_columns(values):
+    lead = values.shape[:-1]
+    cores = lax.axis_size("core")
+    outer = lax.axis_size("guid") * lax.axis_size("xlo")
+    split = values.reshape(lead + (outer, cores, values.shape[-1] // (outer * cores)))
+    n = len(lead)
+    order = tuple(range(n)) + (n + 1, n, n + 2)
+    return jnp.transpose(split, order).reshape(values.shape)
+
+
 def local(
     img_hidden,
     txt_hidden,
@@ -44,23 +54,32 @@
     latent,
     step,
 ):
-    all_axes = ("guid", "req", "seq")
+    all_axes = ("guid", "xlo", "core", "seq")
     prompts = img_hidden.shape[1]
     img_rows = img_hidden.shape[2]
     txt_rows = txt_hidden.shape[2]
     model_width = img_hidden.shape[3]
     nseq = lax.axis_size("seq")
 
-    full_img = lax.all_gather(w_img_qkv, all_axes, axis=0, tiled=True)
-    full_txt = lax.all_gather(w_txt_qkv, all_axes, axis=0, tiled=True)
+    outer = ("guid", "xlo", "seq")
+    full_img = lax.all_gather(
+        lax.all_gather(w_img_qkv, outer, axis=0, tiled=True), "core", axis=0, tiled=True
+    )
+    full_txt = lax.all_gather(
+        lax.all_gather(w_txt_qkv, outer, axis=0, tiled=True), "core", axis=0, tiled=True
+    )
+    out_rows, out_cols = w_out.shape
     head_rows, head_cols = w_head.shape
-    full_head = lax.all_gather(
-        w_head.reshape(1, head_rows * head_cols), all_axes, axis=0, tiled=True
-    ).reshape(-1, head_cols)
-    full_out = lax.all_gather(w_out, all_axes, axis=0, tiled=True)
+    head_flat = w_head.reshape(1, head_rows * head_cols)
+    head_flat = jnp.pad(head_flat, ((0, 0), (0, out_cols - head_rows * head_cols)))
+    packed = lax.all_gather(
+        jnp.concatenate([w_out, head_flat], axis=0), all_axes, axis=0, tiled=False
+    )
+    full_out = packed[:, :out_rows].reshape(-1, out_cols)
+    full_head = packed[:, out_rows, : head_rows * head_cols].reshape(-1, head_cols)
 
-    image_in = modulate(img_hidden[0], img_mod[0, :, 0], img_mod[0, :, 1])
-    text_in = modulate(txt_hidden[0], txt_mod[0, :, 0], txt_mod[0, :, 1])
+    image_in = permute_columns(modulate(img_hidden[0], img_mod[0, :, 0], img_mod[0, :, 1]))
+    text_in = permute_columns(modulate(txt_hidden[0], txt_mod[0, :, 0], txt_mod[0, :, 1]))
     attn_width = full_img.shape[1] // 3
     head_count = attn_width // HD
     per_dev = head_count // nseq
@@ -134,23 +153,31 @@
 
 
 def solution(mesh):
+    shape = mesh.devices.shape
+    cores = 2
+    fine = jax.sharding.Mesh(
+        mesh.devices.reshape(shape[0], shape[1] // cores, cores, shape[2]),
+        ("guid", "xlo", "core", "seq"),
+    )
+    req = ("xlo", "core")
+    every = ("guid", "xlo", "core", "seq")
     placed = (
-        P("guid", "req", "seq", None),
-        P("guid", "req", "seq", None),
-        P("guid", "req", None, None),
-        P("guid", "req", None, None),
-        P(("guid", "req", "seq"), None),
-        P(("guid", "req", "seq"), None),
-        P(("guid", "req", "seq"), None),
-        P(("guid", "req", "seq"), None),
-        P("guid", "req"),
-        P("req", "seq", "guid"),
+        P("guid", req, "seq", None),
+        P("guid", req, "seq", None),
+        P("guid", req, None, None),
+        P("guid", req, None, None),
+        P(every, None),
+        P(every, None),
+        P(every, None),
+        P(every, None),
+        P("guid", req),
+        P(req, "seq", "guid"),
         P(),
     )
     return jax.shard_map(
         local,
-        mesh=mesh,
+        mesh=fine,
         in_specs=placed,
-        out_specs=(P("req", "seq", "guid"), P("req", "seq", "guid")),
+        out_specs=(P(req, "seq", "guid"), P(req, "seq", "guid")),
         check_vma=False,
     )

time: 417 us -> 393 us (0.942)
  blocking collectives: 68.7 us -> 0 us
  waiting for transfers between devices: 150 us -> 198 us
  local copies, waits for them, and re-layouts: 99.3 us -> 89.7 us
    all_gather x1 -> x0, blocking collectives: 68.7 us -> none  [local(): lax.all_gather(w_head.reshape(1, head_rows * head_cols), all_axes, axis=0...]
    all_gather x3 -> x5, waiting for transfers between devices: 120 us -> 155 us  [the longest x1 76.5 us: local(): lax.all_gather(w_txt_qkv, outer, axis=0, tiled=True)]
    unnamed x38 -> x37, local copies, waits for them, and re-layouts: 54.8 us -> 36.2 us
    all_to_all x1, waiting for transfers between devices: 0.01 us -> 10.1 us  [local(): token_out = lax.all_to_all(head_out, 'seq', 1, 2, tiled=True)]
    all_to_all x1, waiting for transfers between devices: 23.2 us -> 29.5 us  [local(): img_heads = lax.all_to_all(img_split, 'seq', 3, 1, tiled=True)]
    convert_element_type x0 -> x2, local copies, waits for them, and re-layouts: none -> 5.27 us  [the longest x1 4.7 us: local(): img_hidden[0].astype(jnp.float32)]
  transfers between devices with their start and end apart: 7 -> 9, of which waited for: 4 -> 6; matrix products, arithmetic and copies ran while one was open for 36% -> 34% of each run, Pallas kernels for 0% -> 0%
where the time goes in v2:
time: 393 us; the launch traced here: 391 us
  waiting for transfers between devices  198 us (50%)
  local copies, waits for them, and re-layouts  89.7 us (23%)
  matrix products  41.1 us (10%)
  other arithmetic  23.1 us (6%)
  starting transfers between devices  22.3 us (6%)
  between operations  16.5 us (4%)
    all_gather x1, waiting for transfers between devices, local(): lax.all_gather(w_txt_qkv, outer, axis=0, tiled=True)  76.5 us
    all_gather x1, waiting for transfers between devices, local(): lax.all_gather(w_img_qkv, outer, axis=0, tiled=True)  66.4 us
    unnamed x37, local copies, waits for them, and re-layouts  36.2 us
    all_to_all x1, waiting for transfers between devices, local(): img_heads = lax.all_to_all(img_split, 'seq', 3, 1, tiled=True)  29.5 us
    all_to_all x3, local copies, waits for them, and re-layouts, local(): img_heads = lax.all_to_all(img_split, 'seq', 3, 1, tiled=True)  19.7 us
    reduce_sum x1, other arithmetic, local(): totals = jnp.sum(weights, axis=-1)  14 us
    dot_general x1, matrix products, local(): jnp.einsum('phqk,pkhd->pqhd', weights.astype(jnp.bfloat16), value_heads,...  12.5 us
    all_gather x1, waiting for transfers between devices, local(): lax.all_gather(lax.all_gather(w_img_qkv, outer, axis=0, tiled=True), 'cor...  12.4 us
  transfers between devices with their start and end apart: 9, of which 6 were waited for; matrix products, arithmetic and copies ran while one was open for 34% of the time, Pallas kernels for 0%

profile of v2, /device:TPU:0, one launch (start us, length us, event | category | flops | bytes accessed | tf_op | source)
XLA Modules:
  0.0 391.1 jit_solution(1354282489148605827)
XLA Ops:
  9.5 76.5 %all-gather.16.cloned.1.call-done = bf16[64,12,3072]{2,1,0:T(8,128)(2,1)} async-done(((bf16[1,12,3072]{2,1,0:T(8,128)(2,1)}), bf16[64,12,3072]{2,1,0:T(8,128)(2,1)}) %all-gather.16.cloned.1.call-update) | async-done | bytes 4718608 | tf_op jit(solution)/shard_map/all_gather | solution.py:69
  86.0 7.6 %reshape.228 = bf16[768,3072]{1,0:T(8,128)(2,1)} reshape(bf16[64,12,3072]{2,1,0:T(8,128)(2,1)} %all-gather.16.cloned.1.call-done) | data formatting | bytes 9437184
  93.7 66.4 %all-gather.14.cloned.1.call-done = bf16[64,12,3072]{2,1,0:T(8,128)(2,1)} async-done(((bf16[1,12,3072]{2,1,0:T(8,128)(2,1)}), bf16[64,12,3072]{2,1,0:T(8,128)(2,1)}) %all-gather.14.cloned.1.call-update) | async-done | bytes 4718608 | tf_op jit(solution)/shard_map/all_gather | solution.py:66
  160.1 7.5 %reshape.226 = bf16[768,3072]{1,0:T(8,128)(2,1)} reshape(bf16[64,12,3072]{2,1,0:T(8,128)(2,1)} %all-gather.14.cloned.1.call-done) | data formatting | bytes 9437184
  169.4 4.7 %reshape.217 = f32[6,64,4,2,192]{4,3,2,1,0:T(2,128)S(1)} reshape(bf16[1,6,64,1536]{3,2,1,0:T(8,128)(2,1)} %param.11) | data formatting | bytes 3538944 | tf_op jit(solution)/shard_map/convert_element_type | solution.py:131
  186.3 5.3 %fusion.6 = bf16[6,12,3072]{2,1,0:T(8,128)(2,1)S(1)} fusion(bf16[6,12,1536]{2,1,0:T(8,128)(2,1)S(1)} %reshape.206, bf16[1536,3072]{1,0:T(8,128)(2,1)} %all-gather.12.cloned.1.call-done), kind=kOutput, calls=%fused_computation.7 | convolution fusion | flops 679477248 | bytes 10100736 | tf_op jit(solution)/shard_map/prd,de->pre/dot_general | solution.py:89
  193.7 6.4 %all-to-all-start.1 = ((bf16[16,2,4608]{2,1,0:T(2,128)(2,1)}), bf16[16,2,4608]{2,1,0:T(2,128)(2,1)S(1)}, u32[]{:S(2)}, u32[]{:S(2)}) async-start(bf16[16,2,4608]{2,1,0:T(2,128)(2,1)} %reshape.239), calls=%async_computation.1 | async-start | bytes 589824 | tf_op jit(solution)/shard_map/all_to_all | solution.py:96
  200.2 12.4 %all-gather.10.cloned.1.call-done = bf16[1536,3072]{1,0:T(8,128)(2,1)} async-done(((bf16[768,3072]{1,0:T(8,128)(2,1)}), bf16[1536,3072]{1,0:T(8,128)(2,1)}) %all-gather.10.cloned.1.call-update) | async-done | bytes 9437200 | tf_op jit(solution)/shard_map/all_gather | solution.py:65
  212.6 7.9 %fusion.10 = bf16[6,64,3072]{2,1,0:T(8,128)(2,1)S(1)} fusion(bf16[6,64,1536]{2,1,0:T(8,128)(2,1)} %reshape.204, bf16[1536,3072]{1,0:T(8,128)(2,1)} %all-gather.10.cloned.1.call-done), kind=kOutput, calls=%fused_computation.11 | convolution fusion | flops 3625058304 | bytes 12976128 | tf_op jit(solution)/shard_map/prd,de->pre/dot_general | solution.py:86
  220.5 4.8 %reshape.205 = bf16[6,64,3,16,64]{4,3,2,1,0:T(8,128)(2,1)} reshape(bf16[6,64,3072]{2,1,0:T(8,128)(2,1)S(1)} %fusion.10) | data formatting | bytes 4718592 | tf_op jit(solution)/shard_map/reshape | solution.py:93
  225.3 5.7 %copy.80 = bf16[6,64,3,16,64]{4,1,2,0,3:T(8,128)(2,1)} copy(bf16[6,64,3,16,64]{4,3,2,1,0:T(8,128)(2,1)} %reshape.205) | data formatting | bytes 4718592 | tf_op jit(solution)/shard_map/reshape | solution.py:93
  231.0 7.8 %reshape.241 = bf16[16,2,36864]{2,1,0:T(2,128)(2,1)} reshape(bf16[16,6,3,64,64]{4,3,2,1,0:T(8,128)(2,1)} %bitcast.113) | data formatting | bytes 4718592
  238.9 7.2 %all-to-all-start = ((bf16[16,2,36864]{2,1,0:T(2,128)(2,1)}), bf16[16,2,36864]{2,1,0:T(2,128)(2,1)S(1)}, u32[]{:S(2)}, u32[]{:S(2)}) async-start(bf16[16,2,36864]{2,1,0:T(2,128)(2,1)} %reshape.241), calls=%async_computation | async-start | bytes 4718592 | tf_op jit(solution)/shard_map/all_to_all | solution.py:94
  250.6 29.5 %all-to-all-done = bf16[16,2,36864]{2,1,0:T(2,128)(2,1)S(1)} async-done(((bf16[16,2,36864]{2,1,0:T(2,128)(2,1)}), bf16[16,2,36864]{2,1,0:T(2,128)(2,1)S(1)}, u32[]{:S(2)}, u32[]{:S(2)}) %all-to-all-start) | async-done | bytes 2359328 | tf_op jit(solution)/shard_map/all_to_all | solution.py:94
  280.1 5.3 %reshape.242 = bf16[16,6,3,64,64]{4,3,2,1,0:T(8,128)(2,1)} reshape(bf16[16,2,36864]{2,1,0:T(2,128)(2,1)S(1)} %all-to-all-done) | data formatting | bytes 4718592
  285.4 6.1 %bitcast_bitcast_fusion = bf16[6,16,64,3,1,64]{5,2,3,0,1,4:T(8,128)(2,1)} fusion(bf16[16,6,3,64,64]{4,3,2,1,0:T(8,128)(2,1)} %reshape.242), kind=kLoop, calls=%fused_computation.84 | loop fusion | bytes 4718592 | tf_op jit(solution)/shard_map/all_to_all | solution.py:94
  291.5 7.3 %copy.48 = bf16[6,16,64,3,1,64]{2,1,5,0,3,4:T(8,128)(2,1)} copy(bf16[6,16,64,3,1,64]{5,2,3,0,1,4:T(8,128)(2,1)} %bitcast_bitcast_fusion) | data formatting | bytes 4718592 | tf_op jit(solution)/shard_map/all_to_all | solution.py:94
  298.8 6.3 %all_to_all.40 = bf16[6,1024,3,1,64]{1,4,0,3,2:T(8,128)(2,1)S(1)} reshape(bf16[6,16,64,3,1,64]{2,1,5,0,3,4:T(8,128)(2,1)} %copy.48) | data formatting | bytes 4718592 | tf_op jit(solution)/shard_map/all_to_all | solution.py:94
  306.1 11.1 %fusion = (f32[6,1024]{1,0:T(8,128)S(1)}, f32[6,1024,1216]{1,2,0:T(8,128)}) fusion(pred[6,1216]{1,0:T(8,128)(4,1)S(1)} %compare_or_fusion, bf16[6,192,64]{1,2,0:T(8,128)(2,1)S(1)} %bitcast.119, bf16[6,1024,64]{1,2,0:T(8,128)(2,1)S(1)} %get-tuple-element.5, bf16[6,1024,3,1,64]{1,4,0,3,2:T(8,128)(2,1)S(1)} %all_to_all.40), kind=kOutput, calls=%fused_computation.2 | convolution fusion | flops 980576256 | bytes 31688704 | tf_op jit(solution)/shard_map/pqhd,pkhd->phqk/dot_general | solution.py:110
  317.2 14.0 %fusion.1 = f32[6,1024]{1,0:T(8,128)S(1)} fusion(f32[6,1024,1216]{1,2,0:T(8,128)} %get-tuple-element.16, f32[6,1024]{1,0:T(8,128)S(1)} %get-tuple-element.15, pred[6,1216]{1,0:T(8,128)(4,1)S(1)} %compare_or_fusion), kind=kLoop, calls=%fused_computation.3 | loop fusion | flops 29878272 | bytes 29940864 | tf_op jit(solution)/shard_map/reduce_sum | solution.py:118
  331.2 12.5 %fusion.22 = bf16[6,1024,1,64]{1,3,0,2:T(8,128)(2,1)S(1)} fusion(f32[6,1024,1216]{1,2,0:T(8,128)} %get-tuple-element.16, f32[6,1024]{1,0:T(8,128)S(1)} %get-tuple-element.15, pred[6,1216]{1,0:T(8,128)(4,1)S(1)} %compare_or_fusion, bf16[6,192,64]{1,2,0:T(8,128)(2,1)S(1)} %bitcast.120, bf16[6,1024,64]{1,2,0:T(8,128)(2,1)S(1)} %get-tuple-element.4, ...), kind=kOutput, calls=%fused_computation.27 | convolution fusion | flops 988839936 | bytes 31661184 | tf_op jit(solution)/shard_map/phqk,pkhd->pqhd/dot_general | solution.py:119
  347.6 5.5 %all-to-all-start.2 = ((bf16[16,2,12288]{2,1,0:T(2,128)(2,1)}), bf16[16,2,12288]{2,1,0:T(2,128)(2,1)S(1)}, u32[]{:S(2)}, u32[]{:S(2)}) async-start(bf16[16,2,12288]{2,1,0:T(2,128)(2,1)} %reshape.243), calls=%async_computation.2 | async-start | bytes 1572864 | tf_op jit(solution)/shard_map/all_to_all | solution.py:127
  356.6 10.1 %all-to-all-done.2 = bf16[16,2,12288]{2,1,0:T(2,128)(2,1)S(1)} async-done(((bf16[16,2,12288]{2,1,0:T(2,128)(2,1)}), bf16[16,2,12288]{2,1,0:T(2,128)(2,1)S(1)}, u32[]{:S(2)}, u32[]{:S(2)}) %all-to-all-start.2) | async-done | bytes 786464 | tf_op jit(solution)/shard_map/all_to_all | solution.py:127
  372.8 3.4 fusion.52
  (95 shorter events, 43.1 us)
Async XLA Ops:
  8.0 78.0 %all-gather.16.cloned.1.call-start = ((), (), s32[]{:S(2)}) async-start(), calls=%async_computation.6 | async-start | bytes 6389760 | tf_op jit(solution)/shard_map/all_gather | solution.py:69
  8.7 151.3 %all-gather.14.cloned.1.call-start = ((), (), s32[]{:S(2)}) async-start(), calls=%async_computation.5 | async-start | bytes 6389760 | tf_op jit(solution)/shard_map/all_gather | solution.py:66
  9.5 176.8 %all-gather.12.cloned.1.call-start = ((), (), s32[]{:S(2)}) async-start(), calls=%async_computation.4 | async-start | bytes 14155776 | tf_op jit(solution)/shard_map/all_gather | solution.py:68
  93.6 119.0 %all-gather.10.cloned.1.call-start = ((), (), s32[]{:S(2)}) async-start(), calls=%async_computation.3 | async-start | bytes 14155776 | tf_op jit(solution)/shard_map/all_gather | solution.py:65
  167.6 0.9 copy-start.4
  180.4 3.4 copy-start.9
  180.4 3.8 copy-start.1
  193.7 45.1 %all-to-all-start.1 = ((bf16[16,2,4608]{2,1,0:T(2,128)(2,1)}), bf16[16,2,4608]{2,1,0:T(2,128)(2,1)S(1)}, u32[]{:S(2)}, u32[]{:S(2)}) async-start(bf16[16,2,4608]{2,1,0:T(2,128)(2,1)} %reshape.239), calls=%async_computation.1 | async-start | bytes 589824 | tf_op jit(solution)/shard_map/all_to_all | solution.py:96
  238.9 7.3 %copy-start.11 = (bf16[12,64]{1,0:T(8,128)(2,1)S(1)}, bf16[12,64]{1,0:T(8,128)(2,1)}, u32[]{:S(2)}) copy-start(bf16[12,64]{1,0:T(8,128)(2,1)} %param.18) | copy-start | bytes 4612
  238.9 7.4 %copy-start.10 = (bf16[8,1536]{1,0:T(8,128)(2,1)S(1)}, bf16[8,1536]{1,0:T(8,128)(2,1)}, u32[]{:S(2)}) copy-start(bf16[8,1536]{1,0:T(8,128)(2,1)} %param.17) | copy-start | bytes 73732
  238.9 8.1 %copy-start.12 = (s32[1,6]{1,0:T(1,128)S(1)}, s32[1,6]{1,0:T(1,128)}, u32[]{:S(2)}) copy-start(s32[1,6]{1,0:T(1,128)} %param.19) | copy-start | bytes 76
  238.9 41.2 %all-to-all-start = ((bf16[16,2,36864]{2,1,0:T(2,128)(2,1)}), bf16[16,2,36864]{2,1,0:T(2,128)(2,1)S(1)}, u32[]{:S(2)}, u32[]{:S(2)}) async-start(bf16[16,2,36864]{2,1,0:T(2,128)(2,1)} %reshape.241), calls=%async_computation | async-start | bytes 4718592 | tf_op jit(solution)/shard_map/all_to_all | solution.py:94
  246.1 107.1 %all-gather.18.cloned.1.call-start = ((), (), s32[]{:S(2)}) async-start(), calls=%async_computation.7 | async-start | bytes 6340608 | tf_op jit(solution)/shard_map/all_gather | solution.py:75
  305.1 0.9 copy-start.2
  343.7 9.4 %copy-start.7 = (f32[1,6,1,1536]{3,0,2,1:T(1,128)S(1)}, f32[1,6,1,1536]{3,0,2,1:T(1,128)}, u32[]{:S(2)}) copy-start(f32[1,6,1,1536]{3,0,2,1:T(1,128)} %get-tuple-element.10) | copy-start | bytes 110596
  343.7 9.4 %copy-start.5 = (f32[1,6,1,1536]{3,0,2,1:T(1,128)S(1)}, f32[1,6,1,1536]{3,0,2,1:T(1,128)}, u32[]{:S(2)}) copy-start(f32[1,6,1,1536]{3,0,2,1:T(1,128)} %get-tuple-element.8) | copy-start | bytes 110596
  343.7 9.4 %copy-start.6 = (f32[1,6,1,1536]{3,0,2,1:T(1,128)S(1)}, f32[1,6,1,1536]{3,0,2,1:T(1,128)}, u32[]{:S(2)}) copy-start(f32[1,6,1,1536]{3,0,2,1:T(1,128)} %get-tuple-element.11) | copy-start | bytes 110596
  347.6 19.1 %all-to-all-start.2 = ((bf16[16,2,12288]{2,1,0:T(2,128)(2,1)}), bf16[16,2,12288]{2,1,0:T(2,128)(2,1)S(1)}, u32[]{:S(2)}, u32[]{:S(2)}) async-start(bf16[16,2,12288]{2,1,0:T(2,128)(2,1)} %reshape.243), calls=%async_computation.2 | async-start | bytes 1572864 | tf_op jit(solution)/shard_map/all_to_all | solution.py:127
  367.9 4.9 %copy-start = (bf16[1,6,64,1536]{3,2,1,0:T(8,128)(2,1)S(1)}, bf16[1,6,64,1536]{3,2,1,0:T(8,128)(2,1)}, u32[]{:S(2)}) copy-start(bf16[1,6,64,1536]{3,2,1,0:T(8,128)(2,1)} %param.11) | copy-start | bytes 3538948
  372.8 3.8 copy-start.3
  376.3 7.0 %copy-start.8 = (f32[6,64,32]{1,2,0:T(8,128)S(1)}, f32[6,64,32]{1,2,0:T(8,128)}, u32[]{:S(2)}) copy-start(f32[6,64,32]{1,2,0:T(8,128)} %param.20) | copy-start | bytes 147460
  377.6 5.7 %collective-permute-start = (bf16[6,64,32]{1,2,0:T(8,128)(2,1)S(1)}, bf16[6,64,32]{1,2,0:T(8,128)(2,1)S(1)}, u32[]{:S(2)}, u32[]{:S(2)}) collective-permute-start(bf16[6,64,32]{1,2,0:T(8,128)(2,1)S(1)} %dynamic-slice_convert_fusion), channel_id=1, source_target_pairs={{0,64},{64,0},{1,65},{65,1},{2,66},{66,2},{3,67},{67,3},{4,68},{68... | collective-permute-start | bytes 73736 | tf_op jit(solution)/shard_map/ppermute | solution.py:18
Sparse Core Ops, SparseCore 0:
  11.6 74.3 all-gather.15
  88.9 71.1 all-gather.13
  161.7 23.5 all-gather.11
  186.9 25.6 all-gather.9
Sparse Core Ops, SparseCore 1:
  250.3 77.6 all-gather.17

commit v3 on v2

--- a/solution.py
+++ b/solution.py
@@ -31,16 +31,6 @@
     return flow_shift * remaining / (1.0 + (flow_shift - 1.0) * remaining)
 
 
-def permute_columns(values):
-    lead = values.shape[:-1]
-    cores = lax.axis_size("core")
-    outer = lax.axis_size("guid") * lax.axis_size("xlo")
-    split = values.reshape(lead + (outer, cores, values.shape[-1] // (outer * cores)))
-    n = len(lead)
-    order = tuple(range(n)) + (n + 1, n, n + 2)
-    return jnp.transpose(split, order).reshape(values.shape)
-
-
 def local(
     img_hidden,
     txt_hidden,
@@ -61,13 +51,9 @@
     model_width = img_hidden.shape[3]
     nseq = lax.axis_size("seq")
 
-    outer = ("guid", "xlo", "seq")
-    full_img = lax.all_gather(
-        lax.all_gather(w_img_qkv, outer, axis=0, tiled=True), "core", axis=0, tiled=True
-    )
-    full_txt = lax.all_gather(
-        lax.all_gather(w_txt_qkv, outer, axis=0, tiled=True), "core", axis=0, tiled=True
-    )
+    attn_width = w_img_qkv.shape[1] // 3
+    full_txt = lax.all_gather(w_txt_qkv[:, attn_width:], all_axes, axis=0, tiled=True)
+    full_img = lax.all_gather(w_img_qkv, all_axes, axis=0, tiled=True)
     out_rows, out_cols = w_out.shape
     head_rows, head_cols = w_head.shape
     head_flat = w_head.reshape(1, head_rows * head_cols)
@@ -78,9 +64,8 @@
     full_out = packed[:, :out_rows].reshape(-1, out_cols)
     full_head = packed[:, out_rows, : head_rows * head_cols].reshape(-1, head_cols)
 
-    image_in = permute_columns(modulate(img_hidden[0], img_mod[0, :, 0], img_mod[0, :, 1]))
-    text_in = permute_columns(modulate(txt_hidden[0], txt_mod[0, :, 0], txt_mod[0, :, 1]))
-    attn_width = full_img.shape[1] // 3
+    image_in = modulate(img_hidden[0], img_mod[0, :, 0], img_mod[0, :, 1])
+    text_in = modulate(txt_hidden[0], txt_mod[0, :, 0], txt_mod[0, :, 1])
     head_count = attn_width // HD
     per_dev = head_count // nseq
     qkv_image = jnp.einsum(
@@ -92,7 +77,7 @@
 
     img_split = qkv_image.reshape(prompts, img_rows, 3, nseq, per_dev * HD)
     img_heads = lax.all_to_all(img_split, "seq", 3, 1, tiled=True)
-    txt_split = qkv_text[..., attn_width:].reshape(prompts, txt_rows, 2, nseq, per_dev * HD)
+    txt_split = qkv_text.reshape(prompts, txt_rows, 2, nseq, per_dev * HD)
     txt_heads = lax.all_to_all(txt_split, "seq", 3, 1, tiled=True)
     all_img = img_heads.shape[1]
     all_txt = txt_heads.shape[1]

time: 393 us -> 356 us (0.906)
  waiting for transfers between devices: 198 us -> 157 us
  local copies, waits for them, and re-layouts: 89.7 us -> 100 us
  starting transfers between devices: 22.3 us -> 18.3 us
    all_gather x4 -> x2, waiting for transfers between devices: 155 us -> 121 us  [the longest x1 68.7 us: local(): lax.all_gather(w_txt_qkv[:, attn_width:], all_axes, axis=0, tiled=True)]
    unnamed x37 -> x38, local copies, waits for them, and re-layouts: 36.2 us -> 53.3 us
    all_to_all x1, waiting for transfers between devices: 29.5 us -> 22.4 us  [local(): img_heads = lax.all_to_all(img_split, 'seq', 3, 1, tiled=True)]
    convert_element_type x2 -> x0, local copies, waits for them, and re-layouts: 5.27 us -> none  [the longest x1 4.7 us: local(): img_hidden[0].astype(jnp.float32)]
  transfers between devices with their start and end apart: 9 -> 7, of which waited for: 6 -> 5; matrix products, arithmetic and copies ran while one was open for 34% -> 40% of each run, Pallas kernels for 0% -> 0%
where the time goes in v3:
time: 356 us; the launch traced here: 353 us
  waiting for transfers between devices  157 us (44%)
  local copies, waits for them, and re-layouts  100 us (28%)
  matrix products  41.1 us (12%)
  other arithmetic  21.5 us (6%)
  starting transfers between devices  18.3 us (5%)
  between operations  14.9 us (4%)
    all_gather x1, waiting for transfers between devices, local(): lax.all_gather(w_txt_qkv[:, attn_width:], all_axes, axis=0, tiled=True)  68.7 us
    unnamed x38, local copies, waits for them, and re-layouts  53.3 us
    all_gather x1, waiting for transfers between devices, local(): full_img = lax.all_gather(w_img_qkv, all_axes, axis=0, tiled=True)  52.3 us
    all_to_all x1, waiting for transfers between devices, local(): img_heads = lax.all_to_all(img_split, 'seq', 3, 1, tiled=True)  22.4 us
    all_to_all x3, local copies, waits for them, and re-layouts, local(): img_heads = lax.all_to_all(img_split, 'seq', 3, 1, tiled=True)  19.7 us
    reduce_sum x1, other arithmetic, local(): totals = jnp.sum(weights, axis=-1)  14.1 us
    dot_general x1, matrix products, local(): jnp.einsum('phqk,pkhd->pqhd', weights.astype(jnp.bfloat16), value_heads,...  13.4 us
    dot_general x1, matrix products, local(): jnp.einsum('pqhd,pkhd->phqk', query_heads, key_heads, preferred_element_t...  11.2 us
  transfers between devices with their start and end apart: 7, of which 5 were waited for; matrix products, arithmetic and copies ran while one was open for 40% of the time, Pallas kernels for 0%

profile of v3, /device:TPU:0, one launch (start us, length us, event | category | flops | bytes accessed | tf_op | source)
XLA Modules:
  0.0 353.4 jit_solution(14496524449746834699)
XLA Ops:
  15.3 68.7 %all-gather.10.cloned.1.call-done = bf16[128,12,2048]{2,1,0:T(8,128)(2,1)} async-done(((bf16[1,12,2048]{2,1,0:T(8,128)(2,1)}), bf16[128,12,2048]{2,1,0:T(8,128)(2,1)}) %all-gather.10.cloned.1.call-update) | async-done | bytes 6291472 | tf_op jit(solution)/shard_map/all_gather | solution.py:55
  83.9 10.7 %reshape.207 = bf16[1536,2048,1]{1,0,2:T(8,128)(2,1)} reshape(bf16[128,12,2048]{2,1,0:T(8,128)(2,1)} %all-gather.10.cloned.1.call-done) | data formatting | bytes 12582912
  94.6 4.0 %convolution_convert_fusion.1 = bf16[6,12,2048]{2,1,0:T(8,128)(2,1)S(1)} fusion(bf16[1536,2048,1]{1,0,2:T(8,128)(2,1)} %reshape.207, bf16[1,6,12,1536]{3,2,1,0:T(8,128)(2,1)S(1)} %copy-done.1, f32[6,1536]{1,0:T(8,128)S(1)} %get-tuple-element.19, f32[6,1536]{1,0:T(8,128)S(1)} %get-tuple-element.20, f32[6,12]{1,0:T(8,128)S(1)} %add_rsqrt_fusion.1, ...), kind=kOutput, calls=%fused_computation.23 | convolution fusion | flops 453795840 | bytes 6881856 | tf_op jit(solution)/shard_map/prd,de->pre/dot_general | solution.py:74
  100.8 4.4 %all-to-all-start.1 = ((bf16[16,2,4608]{2,1,0:T(2,128)(2,1)}), bf16[16,2,4608]{2,1,0:T(2,128)(2,1)}, u32[]{:S(2)}, u32[]{:S(2)}) async-start(bf16[16,2,4608]{2,1,0:T(2,128)(2,1)} %reshape.213), calls=%async_computation.1 | async-start | bytes 589824 | tf_op jit(solution)/shard_map/all_to_all | solution.py:81
  105.2 52.3 %all-gather.8.cloned.1.call-done = bf16[128,12,3072]{2,1,0:T(8,128)(2,1)} async-done(((bf16[1,12,3072]{2,1,0:T(8,128)(2,1)}), bf16[128,12,3072]{2,1,0:T(8,128)(2,1)}) %all-gather.8.cloned.1.call-update) | async-done | bytes 9437200 | tf_op jit(solution)/shard_map/all_gather | solution.py:56
  157.6 13.7 %reshape.206 = bf16[1536,3072,1]{1,0,2:T(8,128)(2,1)} reshape(bf16[128,12,3072]{2,1,0:T(8,128)(2,1)} %all-gather.8.cloned.1.call-done) | data formatting | bytes 18874368
  171.2 8.2 %convolution_convert_fusion = bf16[6,64,3072]{2,1,0:T(8,128)(2,1)S(1)} fusion(bf16[1536,3072,1]{1,0,2:T(8,128)(2,1)} %reshape.206, bf16[1,6,64,1536]{3,2,1,0:T(8,128)(2,1)S(1)} %copy-done, f32[6,1536]{1,0:T(8,128)} %get-tuple-element.24, f32[6,1536]{1,0:T(8,128)} %get-tuple-element.23, f32[6,64]{1,0:T(8,128)S(1)} %add_rsqrt_fusion.2, ...), kind=kOutput, calls=%fused_computation.7 | convolution fusion | flops 3628597248 | bytes 13052928 | tf_op jit(solution)/shard_map/prd,de->pre/dot_general | solution.py:71
  179.5 4.8 %reshape.182 = bf16[6,64,3,16,64]{4,3,2,1,0:T(8,128)(2,1)} reshape(bf16[6,64,3072]{2,1,0:T(8,128)(2,1)S(1)} %convolution_convert_fusion) | data formatting | bytes 4718592 | tf_op jit(solution)/shard_map/reshape | solution.py:78
  184.3 5.7 %copy.83 = bf16[6,64,3,16,64]{4,1,2,0,3:T(8,128)(2,1)} copy(bf16[6,64,3,16,64]{4,3,2,1,0:T(8,128)(2,1)} %reshape.182) | data formatting | bytes 4718592 | tf_op jit(solution)/shard_map/reshape | solution.py:78
  190.0 7.8 %reshape.215 = bf16[16,2,36864]{2,1,0:T(2,128)(2,1)} reshape(bf16[16,6,3,64,64]{4,3,2,1,0:T(8,128)(2,1)} %bitcast.127) | data formatting | bytes 4718592
  197.9 6.7 %all-to-all-start = ((bf16[16,2,36864]{2,1,0:T(2,128)(2,1)}), bf16[16,2,36864]{2,1,0:T(2,128)(2,1)S(1)}, u32[]{:S(2)}, u32[]{:S(2)}) async-start(bf16[16,2,36864]{2,1,0:T(2,128)(2,1)} %reshape.215), calls=%async_computation | async-start | bytes 4718592 | tf_op jit(solution)/shard_map/all_to_all | solution.py:79
  216.2 22.4 %all-to-all-done = bf16[16,2,36864]{2,1,0:T(2,128)(2,1)S(1)} async-done(((bf16[16,2,36864]{2,1,0:T(2,128)(2,1)}), bf16[16,2,36864]{2,1,0:T(2,128)(2,1)S(1)}, u32[]{:S(2)}, u32[]{:S(2)}) %all-to-all-start) | async-done | bytes 2359328 | tf_op jit(solution)/shard_map/all_to_all | solution.py:79
  238.7 5.4 %reshape.216 = bf16[16,6,3,64,64]{4,3,2,1,0:T(8,128)(2,1)} reshape(bf16[16,2,36864]{2,1,0:T(2,128)(2,1)S(1)} %all-to-all-done) | data formatting | bytes 4718592
  244.0 6.1 %bitcast_bitcast_fusion = bf16[6,16,64,3,1,64]{5,2,3,0,1,4:T(8,128)(2,1)} fusion(bf16[16,6,3,64,64]{4,3,2,1,0:T(8,128)(2,1)} %reshape.216), kind=kLoop, calls=%fused_computation.97 | loop fusion | bytes 4718592 | tf_op jit(solution)/shard_map/all_to_all | solution.py:79
  250.1 7.3 %copy.43 = bf16[6,16,64,3,1,64]{2,1,5,0,3,4:T(8,128)(2,1)} copy(bf16[6,16,64,3,1,64]{5,2,3,0,1,4:T(8,128)(2,1)} %bitcast_bitcast_fusion) | data formatting | bytes 4718592 | tf_op jit(solution)/shard_map/all_to_all | solution.py:79
  257.4 6.3 %all_to_all.40 = bf16[6,1024,3,1,64]{1,4,0,3,2:T(8,128)(2,1)S(1)} reshape(bf16[6,16,64,3,1,64]{2,1,5,0,3,4:T(8,128)(2,1)} %copy.43) | data formatting | bytes 4718592 | tf_op jit(solution)/shard_map/all_to_all | solution.py:79
  264.7 11.2 %fusion = (f32[6,1024]{1,0:T(8,128)S(1)}, f32[6,1024,1216]{1,2,0:T(8,128)}) fusion(pred[6,1216]{1,0:T(8,128)(4,1)S(1)} %compare_or_fusion, bf16[6,192,64]{1,2,0:T(8,128)(2,1)S(1)} %bitcast.133, bf16[6,1024,64]{1,2,0:T(8,128)(2,1)S(1)} %get-tuple-element.5, bf16[6,1024,3,1,64]{1,4,0,3,2:T(8,128)(2,1)S(1)} %all_to_all.40), kind=kOutput, calls=%fused_computation.2 | convolution fusion | flops 980576256 | bytes 31688704 | tf_op jit(solution)/shard_map/pqhd,pkhd->phqk/dot_general | solution.py:95
  275.8 14.1 %fusion.1 = f32[6,1024]{1,0:T(8,128)S(1)} fusion(f32[6,1024,1216]{1,2,0:T(8,128)} %get-tuple-element.16, f32[6,1024]{1,0:T(8,128)S(1)} %get-tuple-element.15, pred[6,1216]{1,0:T(8,128)(4,1)S(1)} %compare_or_fusion), kind=kLoop, calls=%fused_computation.3 | loop fusion | flops 29878272 | bytes 29940864 | tf_op jit(solution)/shard_map/reduce_sum | solution.py:103
  289.9 13.4 %fusion.19 = bf16[6,1024,1,64]{1,3,0,2:T(8,128)(2,1)} fusion(f32[6,1024,1216]{1,2,0:T(8,128)} %get-tuple-element.16, f32[6,1024]{1,0:T(8,128)S(1)} %get-tuple-element.15, pred[6,1216]{1,0:T(8,128)(4,1)S(1)} %compare_or_fusion, bf16[6,192,64]{1,2,0:T(8,128)(2,1)S(1)} %bitcast.134, bf16[6,1024,64]{1,2,0:T(8,128)(2,1)S(1)} %get-tuple-element.4, ...), kind=kOutput, calls=%fused_computation.27 | convolution fusion | flops 988839936 | bytes 31661184 | tf_op jit(solution)/shard_map/phqk,pkhd->pqhd/dot_general | solution.py:104
  308.1 5.1 %all-to-all-start.2 = ((bf16[16,2,12288]{2,1,0:T(2,128)(2,1)}), bf16[16,2,12288]{2,1,0:T(2,128)(2,1)}, u32[]{:S(2)}, u32[]{:S(2)}) async-start(bf16[16,2,12288]{2,1,0:T(2,128)(2,1)} %reshape.217), calls=%async_computation.2 | async-start | bytes 1572864 | tf_op jit(solution)/shard_map/all_to_all | solution.py:112
  316.7 10.1 %all-to-all-done.2 = bf16[16,2,12288]{2,1,0:T(2,128)(2,1)} async-done(((bf16[16,2,12288]{2,1,0:T(2,128)(2,1)}), bf16[16,2,12288]{2,1,0:T(2,128)(2,1)}, u32[]{:S(2)}, u32[]{:S(2)}) %all-to-all-start.2) | async-done | bytes 786464 | tf_op jit(solution)/shard_map/all_to_all | solution.py:112
  326.8 3.5 reshape.218
  335.2 3.4 fusion.65
  343.0 3.1 collective-permute-done
  (77 shorter events, 40.1 us)
Async XLA Ops:
  7.2 6.2 %copy-start = (bf16[1,6,64,1536]{3,2,1,0:T(8,128)(2,1)S(1)}, bf16[1,6,64,1536]{3,2,1,0:T(8,128)(2,1)}, u32[]{:S(2)}) copy-start(bf16[1,6,64,1536]{3,2,1,0:T(8,128)(2,1)} %param.11) | copy-start | bytes 3538948
  7.2 6.7 %copy-start.10 = (f32[1,6,2,1536]{3,2,1,0:T(2,128)S(1)}, f32[1,6,2,1536]{3,2,1,0:T(2,128)}, u32[]{:S(2)}) copy-start(f32[1,6,2,1536]{3,2,1,0:T(2,128)} %param.14) | copy-start | bytes 221188
  7.2 6.8 %copy-start.5 = (f32[1,6,5,1536]{3,0,2,1:T(1,128)S(1)}, f32[1,6,5,1536]{3,0,2,1:T(1,128)}, u32[]{:S(2)}) copy-start(f32[1,6,5,1536]{3,0,2,1:T(1,128)} %param.13) | copy-start | bytes 552964
  7.2 76.7 %all-gather.10.cloned.1.call-start = ((), (), s32[]{:S(2)}) async-start(), calls=%async_computation.4 | async-start | bytes 8454144 | tf_op jit(solution)/shard_map/all_gather | solution.py:55
  8.8 148.7 %all-gather.8.cloned.1.call-start = ((), (), s32[]{:S(2)}) async-start(), calls=%async_computation.3 | async-start | bytes 12681216 | tf_op jit(solution)/shard_map/all_gather | solution.py:56
  15.3 79.4 %copy-start.1 = (bf16[1,6,12,1536]{3,2,1,0:T(8,128)(2,1)S(1)}, bf16[1,6,12,1536]{3,2,1,0:T(8,128)(2,1)}, u32[]{:S(2)}) copy-start(bf16[1,6,12,1536]{3,2,1,0:T(8,128)(2,1)} %param.12) | copy-start | bytes 663556
  100.8 97.1 %all-to-all-start.1 = ((bf16[16,2,4608]{2,1,0:T(2,128)(2,1)}), bf16[16,2,4608]{2,1,0:T(2,128)(2,1)}, u32[]{:S(2)}, u32[]{:S(2)}) async-start(bf16[16,2,4608]{2,1,0:T(2,128)(2,1)} %reshape.213), calls=%async_computation.1 | async-start | bytes 589824 | tf_op jit(solution)/shard_map/all_to_all | solution.py:81
  197.9 6.9 %copy-start.11 = (bf16[12,64]{1,0:T(8,128)(2,1)S(1)}, bf16[12,64]{1,0:T(8,128)(2,1)}, u32[]{:S(2)}) copy-start(bf16[12,64]{1,0:T(8,128)(2,1)} %param.18) | copy-start | bytes 4612
  197.9 8.4 %copy-start.12 = (s32[1,6]{1,0:T(1,128)S(1)}, s32[1,6]{1,0:T(1,128)}, u32[]{:S(2)}) copy-start(s32[1,6]{1,0:T(1,128)} %param.19) | copy-start | bytes 76
  197.9 40.8 %all-to-all-start = ((bf16[16,2,36864]{2,1,0:T(2,128)(2,1)}), bf16[16,2,36864]{2,1,0:T(2,128)(2,1)S(1)}, u32[]{:S(2)}, u32[]{:S(2)}) async-start(bf16[16,2,36864]{2,1,0:T(2,128)(2,1)} %reshape.215), calls=%async_computation | async-start | bytes 4718592 | tf_op jit(solution)/shard_map/all_to_all | solution.py:79
  204.6 108.8 %all-gather.12.cloned.1.call-start = ((), (), s32[]{:S(2)}) async-start(), calls=%async_computation.5 | async-start | bytes 6340608 | tf_op jit(solution)/shard_map/all_gather | solution.py:61
  263.7 0.9 copy-start.2
  275.8 14.1 %copy-start.4 = (bf16[6,192,1,1,64]{1,4,0,3,2:T(8,128)(2,1)S(1)}, bf16[6,192,1,1,64]{1,4,0,3,2:T(8,128)(2,1)}, u32[]{:S(2)}) copy-start(bf16[6,192,1,1,64]{1,4,0,3,2:T(8,128)(2,1)} %copy.62) | copy-start | bytes 442372
  305.9 7.3 %copy-start.8 = (f32[1,6,1,1536]{3,0,2,1:T(1,128)S(1)}, f32[1,6,1,1536]{3,0,2,1:T(1,128)}, u32[]{:S(2)}) copy-start(f32[1,6,1,1536]{3,0,2,1:T(1,128)} %get-tuple-element.10) | copy-start | bytes 110596
  305.9 7.3 %copy-start.6 = (f32[1,6,1,1536]{3,0,2,1:T(1,128)S(1)}, f32[1,6,1,1536]{3,0,2,1:T(1,128)}, u32[]{:S(2)}) copy-start(f32[1,6,1,1536]{3,0,2,1:T(1,128)} %get-tuple-element.8) | copy-start | bytes 110596
  305.9 7.3 %copy-start.7 = (f32[1,6,1,1536]{3,0,2,1:T(1,128)S(1)}, f32[1,6,1,1536]{3,0,2,1:T(1,128)}, u32[]{:S(2)}) copy-start(f32[1,6,1,1536]{3,0,2,1:T(1,128)} %get-tuple-element.11) | copy-start | bytes 110596
  308.1 18.7 %all-to-all-start.2 = ((bf16[16,2,12288]{2,1,0:T(2,128)(2,1)}), bf16[16,2,12288]{2,1,0:T(2,128)(2,1)}, u32[]{:S(2)}, u32[]{:S(2)}) async-start(bf16[16,2,12288]{2,1,0:T(2,128)(2,1)} %reshape.217), calls=%async_computation.2 | async-start | bytes 1572864 | tf_op jit(solution)/shard_map/all_to_all | solution.py:112
  338.5 1.0 copy-start.3
  338.6 7.6 %copy-start.9 = (f32[6,64,32]{1,2,0:T(8,128)S(1)}, f32[6,64,32]{1,2,0:T(8,128)}, u32[]{:S(2)}) copy-start(f32[6,64,32]{1,2,0:T(8,128)} %param.20) | copy-start | bytes 147460
  340.5 5.7 %collective-permute-start = (bf16[6,64,32]{1,2,0:T(8,128)(2,1)S(1)}, bf16[6,64,32]{1,2,0:T(8,128)(2,1)S(1)}, u32[]{:S(2)}, u32[]{:S(2)}) collective-permute-start(bf16[6,64,32]{1,2,0:T(8,128)(2,1)S(1)} %dynamic-slice_convert_fusion), channel_id=1, source_target_pairs={{0,64},{64,0},{1,65},{65,1},{2,66},{66,2},{3,67},{67,3},{4,68},{68... | collective-permute-start | bytes 73736 | tf_op jit(solution)/shard_map/ppermute | solution.py:18
Sparse Core Ops, SparseCore 0:
  11.7 72.1 all-gather.9
  87.0 70.5 all-gather.7
  209.0 75.6 all-gather.11

commit v4 on v3

--- a/solution.py
+++ b/solution.py
@@ -2,6 +2,8 @@
 import jax.numpy as jnp
 from jax import lax
 from jax.sharding import PartitionSpec as P
+from jax.experimental import pallas as pl
+from jax.experimental.pallas import tpu as pltpu
 
 HD = 64
 STEPS = 28
@@ -29,6 +31,51 @@
 def sigma_level(step_value):
     remaining = 1.0 - step_value / STEPS
     return flow_shift * remaining / (1.0 + (flow_shift - 1.0) * remaining)
+
+
+def attend_kernel(len_ref, q_ref, ki_ref, vi_ref, kt_ref, vt_ref, o_ref):
+    length = len_ref[pl.program_id(0)]
+    q = q_ref[0]
+    dims = (((1,), (1,)), ((), ()))
+    s_img = lax.dot_general(q, ki_ref[0], dims, preferred_element_type=jnp.float32) * 0.125
+    s_txt = lax.dot_general(q, kt_ref[0], dims, preferred_element_type=jnp.float32) * 0.125
+    col = lax.broadcasted_iota(jnp.int32, s_txt.shape, 1)
+    s_txt = jnp.where(col < length, s_txt, -1e30)
+    highest = jnp.maximum(
+        jnp.max(s_img, axis=1, keepdims=True), jnp.max(s_txt, axis=1, keepdims=True)
+    )
+    e_img = jnp.exp(s_img - highest)
+    e_txt = jnp.exp(s_txt - highest)
+    totals = jnp.sum(e_img, axis=1, keepdims=True) + jnp.sum(e_txt, axis=1, keepdims=True)
+    acc = jnp.dot(
+        e_img.astype(jnp.bfloat16), vi_ref[0], preferred_element_type=jnp.float32
+    ) + jnp.dot(e_txt.astype(jnp.bfloat16), vt_ref[0], preferred_element_type=jnp.float32)
+    o_ref[0] = (acc / totals).astype(o_ref.dtype)
+
+
+def attend(lengths, q, k_img, v_img, k_txt, v_txt, block=256):
+    batch, rows, width = q.shape
+    n_img = k_img.shape[1]
+    n_txt = k_txt.shape[1]
+    flops = 4 * batch * rows * (n_img + n_txt) * width
+    moved = 2 * (q.size * 2 + k_img.size * 2 + k_txt.size * 2)
+    return pl.pallas_call(
+        attend_kernel,
+        grid=(batch, rows // block),
+        in_specs=[
+            pl.BlockSpec(memory_space=pltpu.SMEM),
+            pl.BlockSpec((1, block, width), lambda b, i: (b, i, 0)),
+            pl.BlockSpec((1, n_img, width), lambda b, i: (b, 0, 0)),
+            pl.BlockSpec((1, n_img, width), lambda b, i: (b, 0, 0)),
+            pl.BlockSpec((1, n_txt, width), lambda b, i: (b, 0, 0)),
+            pl.BlockSpec((1, n_txt, width), lambda b, i: (b, 0, 0)),
+        ],
+        out_specs=pl.BlockSpec((1, block, width), lambda b, i: (b, i, 0)),
+        out_shape=jax.ShapeDtypeStruct(q.shape, jnp.bfloat16),
+        cost_estimate=pl.CostEstimate(
+            flops=flops, transcendentals=batch * rows * (n_img + n_txt), bytes_accessed=moved
+        ),
+    )(lengths, q, k_img, v_img, k_txt, v_txt)
 
 
 def local(
@@ -82,33 +129,17 @@
     all_img = img_heads.shape[1]
     all_txt = txt_heads.shape[1]
 
-    query_heads = img_heads[:, :, 0, 0].reshape(prompts, all_img, per_dev, HD)
-    key_heads = jnp.concatenate(
-        [img_heads[:, :, 1, 0], txt_heads[:, :, 0, 0]], axis=1
-    ).reshape(prompts, all_img + all_txt, per_dev, HD)
-    value_heads = jnp.concatenate(
-        [img_heads[:, :, 2, 0], txt_heads[:, :, 1, 0]], axis=1
-    ).reshape(prompts, all_img + all_txt, per_dev, HD)
-
+    assert per_dev == 1
     lengths = text_lengths[0]
-    scores = (
-        jnp.einsum("pqhd,pkhd->phqk", query_heads, key_heads, preferred_element_type=jnp.float32)
-        * 0.125
+    mixture = attend(
+        lengths,
+        img_heads[:, :, 0, 0],
+        img_heads[:, :, 1, 0],
+        img_heads[:, :, 2, 0],
+        txt_heads[:, :, 0, 0],
+        txt_heads[:, :, 1, 0],
     )
-    position = jnp.arange(all_img + all_txt, dtype=jnp.int32)
-    allowed = (position < all_img)[None, :] | ((position - all_img)[None, :] < lengths[:, None])
-    scores = jnp.where(allowed[:, None, None, :], scores, -1e30)
-    highest = jnp.max(scores, axis=-1)
-    weights = jnp.exp(scores - highest[..., None])
-    totals = jnp.sum(weights, axis=-1)
-    accumulated = jnp.einsum(
-        "phqk,pkhd->pqhd",
-        weights.astype(jnp.bfloat16),
-        value_heads,
-        preferred_element_type=jnp.float32,
-    )
-    mixture = accumulated / jnp.transpose(totals, (0, 2, 1))[..., None]
-    head_out = mixture.astype(jnp.bfloat16).reshape(prompts, all_img, 1, per_dev * HD)
+    head_out = mixture.reshape(prompts, all_img, 1, per_dev * HD)
     token_out = lax.all_to_all(head_out, "seq", 1, 2, tiled=True)
     attended = token_out.reshape(prompts * img_rows, attn_width)
 

time: 356 us -> 333 us (0.935)
  matrix products: 41.1 us -> 16.5 us
  Pallas kernels: 0 us -> 24.3 us
  other arithmetic: 21.5 us -> 5.4 us
  local copies, waits for them, and re-layouts: 100 us -> 84.2 us
  waiting for transfers between devices: 157 us -> 168 us
    dot_general x2 -> x0, matrix products: 24.5 us -> none  [the longest x1 13.4 us: local(): jnp.einsum('phqk,pkhd->pqhd', weights.astype(jnp.bfloat16), value_heads,...]
    pallas_call x0 -> x1, Pallas kernels: none -> 24.3 us  [attend(): pl.pallas_call(attend_kernel, grid=(batch, rows // block), in_specs=[pl.B...]
    all_to_all x3 -> x2, local copies, waits for them, and re-layouts: 19.7 us -> 5.02 us  [local(): img_heads = lax.all_to_all(img_split, 'seq', 3, 1, tiled=True)]
    reduce_sum x1 -> x0, other arithmetic: 14.1 us -> none  [local(): totals = jnp.sum(weights, axis=-1)]
    all_to_all x1, waiting for transfers between devices: 22.4 us -> 34 us  [local(): img_heads = lax.all_to_all(img_split, 'seq', 3, 1, tiled=True)]
    unnamed x38 -> x30, local copies, waits for them, and re-layouts: 53.3 us -> 50.2 us
  transfers between devices with their start and end apart: 7 -> 7, of which waited for: 5 -> 5; matrix products, arithmetic and copies ran while one was open for 40% -> 27% of each run, Pallas kernels for 0% -> 7%
where the time goes in v4:
time: 333 us; the launch traced here: 331 us
  waiting for transfers between devices  168 us (50%)
  local copies, waits for them, and re-layouts  84.2 us (25%)
  Pallas kernels  24.3 us (7%)
  starting transfers between devices  17.5 us (5%)
  matrix products  16.5 us (5%)
  between operations  14.8 us (4%)
  other arithmetic  5.4 us (2%)
    all_gather x1, waiting for transfers between devices, local(): lax.all_gather(w_txt_qkv[:, attn_width:], all_axes, axis=0, tiled=True)  68.3 us
    all_gather x1, waiting for transfers between devices, local(): full_img = lax.all_gather(w_img_qkv, all_axes, axis=0, tiled=True)  52.3 us
    unnamed x30, local copies, waits for them, and re-layouts  50.2 us
    all_to_all x1, waiting for transfers between devices, local(): img_heads = lax.all_to_all(img_split, 'seq', 3, 1, tiled=True)  34 us
    pallas_call x1, Pallas kernels, attend(): pl.pallas_call(attend_kernel, grid=(batch, rows // block), in_specs=[pl.B...  24.3 us
    reshape x2, local copies, waits for them, and re-layouts, local(): img_split = qkv_image.reshape(prompts, img_rows, 3, nseq, per_dev * HD)  10.5 us
    all_to_all x1, waiting for transfers between devices, local(): token_out = lax.all_to_all(head_out, 'seq', 1, 2, tiled=True)  9.26 us
    dot_general x1, matrix products, local(): jnp.einsum('prd,de->pre', image_in, full_img, preferred_element_type=jnp....  8.24 us
  transfers between devices with their start and end apart: 7, of which 5 were waited for; matrix products, arithmetic and copies ran while one was open for 27% of the time, Pallas kernels for 7%

profile of v4, /device:TPU:0, one launch (start us, length us, event | category | flops | bytes accessed | tf_op | source)
XLA Modules:
  0.0 330.6 jit_solution(6600201178561152915)
XLA Ops:
  15.6 68.3 %all-gather.10.cloned.1.call-done = bf16[128,12,2048]{2,1,0:T(8,128)(2,1)} async-done(((bf16[1,12,2048]{2,1,0:T(8,128)(2,1)}), bf16[128,12,2048]{2,1,0:T(8,128)(2,1)}) %all-gather.10.cloned.1.call-update) | async-done | bytes 6291472 | tf_op jit(solution)/shard_map/all_gather | solution.py:102
  83.9 10.7 %reshape.133 = bf16[1536,2048,1]{1,0,2:T(8,128)(2,1)} reshape(bf16[128,12,2048]{2,1,0:T(8,128)(2,1)} %all-gather.10.cloned.1.call-done) | data formatting | bytes 12582912
  94.7 4.0 %convolution_convert_fusion.1 = bf16[6,12,2048]{2,1,0:T(8,128)(2,1)S(1)} fusion(bf16[1536,2048,1]{1,0,2:T(8,128)(2,1)} %reshape.133, bf16[1,6,12,1536]{3,2,1,0:T(8,128)(2,1)S(1)} %copy-done.1, f32[6,1536]{1,0:T(8,128)S(1)} %get-tuple-element.22, f32[6,1536]{1,0:T(8,128)S(1)} %get-tuple-element.23, f32[6,12]{1,0:T(8,128)S(1)} %add_rsqrt_fusion.1, ...), kind=kOutput, calls=%fused_computation.16 | convolution fusion | flops 453795840 | bytes 6881856 | tf_op jit(solution)/shard_map/prd,de->pre/dot_general | solution.py:121
  100.8 4.4 %all-to-all-start.1 = ((bf16[16,2,4608]{2,1,0:T(2,128)(2,1)}), bf16[16,2,4608]{2,1,0:T(2,128)(2,1)}, u32[]{:S(2)}, u32[]{:S(2)}) async-start(bf16[16,2,4608]{2,1,0:T(2,128)(2,1)} %reshape.141), calls=%async_computation.1 | async-start | bytes 589824 | tf_op jit(solution)/shard_map/all_to_all | solution.py:128
  105.2 52.3 %all-gather.8.cloned.1.call-done = bf16[128,12,3072]{2,1,0:T(8,128)(2,1)} async-done(((bf16[1,12,3072]{2,1,0:T(8,128)(2,1)}), bf16[128,12,3072]{2,1,0:T(8,128)(2,1)}) %all-gather.8.cloned.1.call-update) | async-done | bytes 9437200 | tf_op jit(solution)/shard_map/all_gather | solution.py:103
  157.6 13.7 %reshape.132 = bf16[1536,3072,1]{1,0,2:T(8,128)(2,1)} reshape(bf16[128,12,3072]{2,1,0:T(8,128)(2,1)} %all-gather.8.cloned.1.call-done) | data formatting | bytes 18874368
  171.3 8.2 %convolution_convert_fusion = bf16[6,64,3072]{2,1,0:T(8,128)(2,1)S(1)} fusion(bf16[1536,3072,1]{1,0,2:T(8,128)(2,1)} %reshape.132, bf16[1,6,64,1536]{3,2,1,0:T(8,128)(2,1)S(1)} %copy-done, f32[6,1536]{1,0:T(8,128)} %get-tuple-element.21, f32[6,1536]{1,0:T(8,128)} %get-tuple-element.20, f32[6,64]{1,0:T(8,128)S(1)} %add_rsqrt_fusion.2, ...), kind=kOutput, calls=%fused_computation | convolution fusion | flops 3628597248 | bytes 13052928 | tf_op jit(solution)/shard_map/prd,de->pre/dot_general | solution.py:118
  179.5 4.8 %reshape.108 = bf16[6,64,3,16,64]{4,3,2,1,0:T(8,128)(2,1)} reshape(bf16[6,64,3072]{2,1,0:T(8,128)(2,1)S(1)} %convolution_convert_fusion) | data formatting | bytes 4718592 | tf_op jit(solution)/shard_map/reshape | solution.py:125
  184.3 5.7 %copy.75 = bf16[6,64,3,16,64]{4,1,0,2,3:T(8,128)(2,1)} copy(bf16[6,64,3,16,64]{4,3,2,1,0:T(8,128)(2,1)} %reshape.108) | data formatting | bytes 4718592 | tf_op jit(solution)/shard_map/reshape | solution.py:125
  190.1 7.9 %reshape.139 = bf16[16,2,36864]{2,1,0:T(2,128)(2,1)} reshape(bf16[16,3,6,64,64]{4,3,2,1,0:T(8,128)(2,1)} %bitcast.121) | data formatting | bytes 4718592
  198.0 6.5 %all-to-all-start = ((bf16[16,2,36864]{2,1,0:T(2,128)(2,1)}), bf16[16,2,36864]{2,1,0:T(2,128)(2,1)S(1)}, u32[]{:S(2)}, u32[]{:S(2)}) async-start(bf16[16,2,36864]{2,1,0:T(2,128)(2,1)} %reshape.139), calls=%async_computation | async-start | bytes 4718592 | tf_op jit(solution)/shard_map/all_to_all | solution.py:126
  211.0 34.0 %all-to-all-done = bf16[16,2,36864]{2,1,0:T(2,128)(2,1)S(1)} async-done(((bf16[16,2,36864]{2,1,0:T(2,128)(2,1)}), bf16[16,2,36864]{2,1,0:T(2,128)(2,1)S(1)}, u32[]{:S(2)}, u32[]{:S(2)}) %all-to-all-start) | async-done | bytes 2359328 | tf_op jit(solution)/shard_map/all_to_all | solution.py:126
  245.0 5.2 %reshape.140 = bf16[16,3,6,64,64]{4,3,2,1,0:T(8,128)(2,1)} reshape(bf16[16,2,36864]{2,1,0:T(2,128)(2,1)S(1)} %all-to-all-done) | data formatting | bytes 4718592
  250.3 3.4 %bitcast_bitcast_fusion = bf16[6,16,64,3,1,64]{5,2,0,3,1,4:T(8,128)(2,1)S(1)} fusion(bf16[16,3,6,64,64]{4,3,2,1,0:T(8,128)(2,1)} %reshape.140), kind=kLoop, calls=%fused_computation.75 | loop fusion | bytes 4718592 | tf_op jit(solution)/shard_map/all_to_all | solution.py:126
  255.3 2.2 slice_bitcast_fusion.6
  257.5 24.3 %shard_map.122 = bf16[6,1024,64]{2,1,0:T(8,128)(2,1)} custom-call(s32[6]{0:T(128)} %bitcast.132, bf16[6,1024,64]{2,1,0:T(8,128)(2,1)} %get-tuple-element.6.q_ref, bf16[6,1024,64]{2,1,0:T(8,128)(2,1)} %get-tuple-element.5.ki_ref, bf16[6,1024,64]{2,1,0:T(8,128)(2,1)} %get-tuple-element.4.vi_ref, bf16[6,192,64]{2,1,0:T(8,128)(2,1)} %bitcast.128, ...), custom_call_target="tpu_custom_call" | custom-call | flops 1912602624 | bytes 3440640 | tf_op jit(solution)/shard_map/pallas_call | solution.py:62
  281.8 2.5 copy.76
  286.5 4.8 %all-to-all-start.2 = ((bf16[16,2,12288]{2,1,0:T(2,128)(2,1)}), bf16[16,2,12288]{2,1,0:T(2,128)(2,1)}, u32[]{:S(2)}, u32[]{:S(2)}) async-start(bf16[16,2,12288]{2,1,0:T(2,128)(2,1)} %reshape.143), calls=%async_computation.2 | async-start | bytes 1572864 | tf_op jit(solution)/shard_map/all_to_all | solution.py:143
  291.4 2.4 slice_reduce_fusion
  294.8 9.3 %all-to-all-done.2 = bf16[16,2,12288]{2,1,0:T(2,128)(2,1)} async-done(((bf16[16,2,12288]{2,1,0:T(2,128)(2,1)}), bf16[16,2,12288]{2,1,0:T(2,128)(2,1)}, u32[]{:S(2)}, u32[]{:S(2)}) %all-to-all-start.2) | async-done | bytes 786464 | tf_op jit(solution)/shard_map/all_to_all | solution.py:143
  304.1 3.5 %reshape.144 = bf16[1024,1,6,64]{3,2,1,0:T(8,128)(2,1)S(1)} reshape(bf16[16,2,12288]{2,1,0:T(2,128)(2,1)} %all-to-all-done.2) | data formatting | bytes 1572864
  309.7 2.7 dot_general.16
  312.4 3.4 %fusion.42 = (f32[6,64]{1,0:T(8,128)S(1)}, f32[6,64,1536]{2,1,0:T(8,128)S(1)}) fusion(bf16[6,64,1024]{2,1,0:T(8,128)(2,1)S(1)} %dot_general.16, bf16[128,9,1536]{2,1,0:T(8,128)(2,1)} %all-gather.12.cloned.1.call-done, f32[6,1536]{1,0:T(8,128)S(1)} %bitcast.131, bf16[1,6,64,1536]{3,2,1,0:T(8,128)(2,1)S(1)} %copy-done), kind=kOutput, calls=%fused_computation.74 | convolution fusion | flops 1210318464 | bytes 7509504 | tf_op jit(solution)/shard_map/dot_general | solution.py:146
  320.1 3.2 collective-permute-done
  (63 shorter events, 28.2 us)
Async XLA Ops:
  7.2 6.2 %copy-start = (bf16[1,6,64,1536]{3,2,1,0:T(8,128)(2,1)S(1)}, bf16[1,6,64,1536]{3,2,1,0:T(8,128)(2,1)}, u32[]{:S(2)}) copy-start(bf16[1,6,64,1536]{3,2,1,0:T(8,128)(2,1)} %param.11) | copy-start | bytes 3538948
  7.2 6.6 %copy-start.1 = (bf16[1,6,12,1536]{3,2,1,0:T(8,128)(2,1)S(1)}, bf16[1,6,12,1536]{3,2,1,0:T(8,128)(2,1)}, u32[]{:S(2)}) copy-start(bf16[1,6,12,1536]{3,2,1,0:T(8,128)(2,1)} %param.12) | copy-start | bytes 663556
  7.2 7.0 %copy-start.8 = (f32[1,6,2,1536]{3,2,1,0:T(2,128)S(1)}, f32[1,6,2,1536]{3,2,1,0:T(2,128)}, u32[]{:S(2)}) copy-start(f32[1,6,2,1536]{3,2,1,0:T(2,128)} %param.14) | copy-start | bytes 221188
  7.2 7.1 %copy-start.3 = (f32[1,6,5,1536]{3,0,2,1:T(1,128)S(1)}, f32[1,6,5,1536]{3,0,2,1:T(1,128)}, u32[]{:S(2)}) copy-start(f32[1,6,5,1536]{3,0,2,1:T(1,128)} %param.13) | copy-start | bytes 552964
  7.2 76.7 %all-gather.10.cloned.1.call-start = ((), (), s32[]{:S(2)}) async-start(), calls=%async_computation.4 | async-start | bytes 8454144 | tf_op jit(solution)/shard_map/all_gather | solution.py:102
  8.9 148.7 %all-gather.8.cloned.1.call-start = ((), (), s32[]{:S(2)}) async-start(), calls=%async_computation.3 | async-start | bytes 12681216 | tf_op jit(solution)/shard_map/all_gather | solution.py:103
  9.6 281.8 %all-gather.12.cloned.1.call-start = ((), (), s32[]{:S(2)}) async-start(), calls=%async_computation.5 | async-start | bytes 6340608 | tf_op jit(solution)/shard_map/all_gather | solution.py:108
  100.8 97.2 %all-to-all-start.1 = ((bf16[16,2,4608]{2,1,0:T(2,128)(2,1)}), bf16[16,2,4608]{2,1,0:T(2,128)(2,1)}, u32[]{:S(2)}, u32[]{:S(2)}) async-start(bf16[16,2,4608]{2,1,0:T(2,128)(2,1)} %reshape.141), calls=%async_computation.1 | async-start | bytes 589824 | tf_op jit(solution)/shard_map/all_to_all | solution.py:128
  198.0 47.0 %all-to-all-start = ((bf16[16,2,36864]{2,1,0:T(2,128)(2,1)}), bf16[16,2,36864]{2,1,0:T(2,128)(2,1)S(1)}, u32[]{:S(2)}, u32[]{:S(2)}) async-start(bf16[16,2,36864]{2,1,0:T(2,128)(2,1)} %reshape.139), calls=%async_computation | async-start | bytes 4718592 | tf_op jit(solution)/shard_map/all_to_all | solution.py:126
  284.3 7.0 %copy-start.6 = (f32[1,6,1,1536]{3,0,2,1:T(1,128)S(1)}, f32[1,6,1,1536]{3,0,2,1:T(1,128)}, u32[]{:S(2)}) copy-start(f32[1,6,1,1536]{3,0,2,1:T(1,128)} %get-tuple-element.11) | copy-start | bytes 110596
  284.3 7.0 %copy-start.4 = (f32[1,6,1,1536]{3,0,2,1:T(1,128)S(1)}, f32[1,6,1,1536]{3,0,2,1:T(1,128)}, u32[]{:S(2)}) copy-start(f32[1,6,1,1536]{3,0,2,1:T(1,128)} %get-tuple-element.9) | copy-start | bytes 110596
  284.3 7.0 %copy-start.5 = (f32[1,6,1,1536]{3,0,2,1:T(1,128)S(1)}, f32[1,6,1,1536]{3,0,2,1:T(1,128)}, u32[]{:S(2)}) copy-start(f32[1,6,1,1536]{3,0,2,1:T(1,128)} %get-tuple-element.12) | copy-start | bytes 110596
  286.5 17.5 %all-to-all-start.2 = ((bf16[16,2,12288]{2,1,0:T(2,128)(2,1)}), bf16[16,2,12288]{2,1,0:T(2,128)(2,1)}, u32[]{:S(2)}, u32[]{:S(2)}) async-start(bf16[16,2,12288]{2,1,0:T(2,128)(2,1)} %reshape.143), calls=%async_computation.2 | async-start | bytes 1572864 | tf_op jit(solution)/shard_map/all_to_all | solution.py:143
  315.8 1.0 copy-start.2
  315.8 7.6 %copy-start.7 = (f32[6,64,32]{1,2,0:T(8,128)S(1)}, f32[6,64,32]{1,2,0:T(8,128)}, u32[]{:S(2)}) copy-start(f32[6,64,32]{1,2,0:T(8,128)} %param.20) | copy-start | bytes 147460
  317.7 5.7 %collective-permute-start = (bf16[6,64,32]{1,2,0:T(8,128)(2,1)S(1)}, bf16[6,64,32]{1,2,0:T(8,128)(2,1)S(1)}, u32[]{:S(2)}, u32[]{:S(2)}) collective-permute-start(bf16[6,64,32]{1,2,0:T(8,128)(2,1)S(1)} %dynamic-slice_convert_fusion), channel_id=1, source_target_pairs={{0,64},{64,0},{1,65},{65,1},{2,66},{66,2},{3,67},{67,3},{4,68},{68... | collective-permute-start | bytes 73736 | tf_op jit(solution)/shard_map/ppermute | solution.py:20
Sparse Core Ops, SparseCore 0:
  11.7 72.1 all-gather.9
  87.0 70.5 all-gather.7
  160.7 87.0 all-gather.11

commit v5 on v4

--- a/solution.py
+++ b/solution.py
@@ -78,7 +78,7 @@
     )(lengths, q, k_img, v_img, k_txt, v_txt)
 
 
-def local(
+def block(
     img_hidden,
     txt_hidden,
     img_mod,
@@ -99,15 +99,18 @@
     nseq = lax.axis_size("seq")
 
     attn_width = w_img_qkv.shape[1] // 3
-    full_txt = lax.all_gather(w_txt_qkv[:, attn_width:], all_axes, axis=0, tiled=True)
-    full_img = lax.all_gather(w_img_qkv, all_axes, axis=0, tiled=True)
+    img_kv_rows = w_img_qkv[:, attn_width:]
+    img_q_rows = w_img_qkv[:, :attn_width]
+    txt_kv_rows = w_txt_qkv[:, attn_width:]
+    full_img_kv = lax.all_gather(img_kv_rows, all_axes, axis=0, tiled=True)
+    full_img_q = lax.all_gather(img_q_rows, all_axes, axis=0, tiled=True)
+    full_txt = lax.all_gather(txt_kv_rows, all_axes, axis=0, tiled=True)
     out_rows, out_cols = w_out.shape
     head_rows, head_cols = w_head.shape
     head_flat = w_head.reshape(1, head_rows * head_cols)
     head_flat = jnp.pad(head_flat, ((0, 0), (0, out_cols - head_rows * head_cols)))
-    packed = lax.all_gather(
-        jnp.concatenate([w_out, head_flat], axis=0), all_axes, axis=0, tiled=False
-    )
+    out_rows_local = jnp.concatenate([w_out, head_flat], axis=0)
+    packed = lax.all_gather(out_rows_local, all_axes, axis=0, tiled=False)
     full_out = packed[:, :out_rows].reshape(-1, out_cols)
     full_head = packed[:, out_rows, : head_rows * head_cols].reshape(-1, head_cols)
 
@@ -115,27 +118,34 @@
     text_in = modulate(txt_hidden[0], txt_mod[0, :, 0], txt_mod[0, :, 1])
     head_count = attn_width // HD
     per_dev = head_count // nseq
-    qkv_image = jnp.einsum(
-        "prd,de->pre", image_in, full_img, preferred_element_type=jnp.float32
+    kv_image = jnp.einsum(
+        "prd,de->pre", image_in, full_img_kv, preferred_element_type=jnp.float32
+    ).astype(jnp.bfloat16)
+    q_image = jnp.einsum(
+        "prd,de->pre", image_in, full_img_q, preferred_element_type=jnp.float32
     ).astype(jnp.bfloat16)
     qkv_text = jnp.einsum(
         "prd,de->pre", text_in, full_txt, preferred_element_type=jnp.float32
     ).astype(jnp.bfloat16)
 
-    img_split = qkv_image.reshape(prompts, img_rows, 3, nseq, per_dev * HD)
-    img_heads = lax.all_to_all(img_split, "seq", 3, 1, tiled=True)
-    txt_split = qkv_text.reshape(prompts, txt_rows, 2, nseq, per_dev * HD)
-    txt_heads = lax.all_to_all(txt_split, "seq", 3, 1, tiled=True)
-    all_img = img_heads.shape[1]
-    all_txt = txt_heads.shape[1]
+    kv_heads = lax.all_to_all(
+        kv_image.reshape(prompts, img_rows, 2, nseq, per_dev * HD), "seq", 3, 1, tiled=True
+    )
+    q_heads = lax.all_to_all(
+        q_image.reshape(prompts, img_rows, nseq, per_dev * HD), "seq", 2, 1, tiled=True
+    )
+    txt_heads = lax.all_to_all(
+        qkv_text.reshape(prompts, txt_rows, 2, nseq, per_dev * HD), "seq", 3, 1, tiled=True
+    )
+    all_img = q_heads.shape[1]
 
     assert per_dev == 1
     lengths = text_lengths[0]
     mixture = attend(
         lengths,
-        img_heads[:, :, 0, 0],
-        img_heads[:, :, 1, 0],
-        img_heads[:, :, 2, 0],
+        q_heads[:, :, 0],
+        kv_heads[:, :, 0, 0],
+        kv_heads[:, :, 1, 0],
         txt_heads[:, :, 0, 0],
         txt_heads[:, :, 1, 0],
     )
@@ -191,7 +201,7 @@
         P(),
     )
     return jax.shard_map(
-        local,
+        block,
         mesh=fine,
         in_specs=placed,
         out_specs=(P(req, "seq", "guid"), P(req, "seq", "guid")),

time: 333 us -> 375 us (1.13)
  waiting for transfers between devices: 168 us -> 208 us
  starting transfers between devices: 17.5 us -> 22.4 us
  local copies, waits for them, and re-layouts: 84.2 us -> 79.9 us
    all_gather x3 -> x4, waiting for transfers between devices: 121 us -> 176 us  [the longest x1 63.2 us: block(): full_img_q = lax.all_gather(img_q_rows, all_axes, axis=0, tiled=True)]
    all_to_all x3 -> x4, waiting for transfers between devices: 43.2 us -> 27.9 us  [the longest x1 20 us: block(): lax.all_to_all(kv_image.reshape(prompts, img_rows, 2, nseq, per_dev * HD)...]
    all_to_all x3 -> x4, starting transfers between devices: 15.7 us -> 21.2 us  [the longest x1 7.39 us: block(): lax.all_to_all(kv_image.reshape(prompts, img_rows, 2, nseq, per_dev * HD)...]
    all_to_all x5 -> x7, local copies, waits for them, and re-layouts: 9.08 us -> 6.34 us  [the longest x1 2.19 us: block(): token_out = lax.all_to_all(head_out, 'seq', 1, 2, tiled=True)]
    dot_general x4 -> x5, matrix products: 16.5 us -> 18.2 us  [the longest x1 6.64 us: block(): jnp.einsum('prd,de->pre', image_in, full_img_kv, preferred_element_type=j...]
    reshape x6 -> x8, local copies, waits for them, and re-layouts: 14.8 us -> 13.2 us  [the longest x2 7.42 us: block(): kv_image.reshape(prompts, img_rows, 2, nseq, per_dev * HD)]
    unnamed x30 -> x51, local copies, waits for them, and re-layouts: 50.2 us -> 50.7 us
  transfers between devices with their start and end apart: 7 -> 9, of which waited for: 5 -> 6; matrix products, arithmetic and copies ran while one was open for 27% -> 24% of each run, Pallas kernels for 7% -> 7%
where the time goes in v5:
time: 375 us; the launch traced here: 373 us
  waiting for transfers between devices  208 us (55%)
  local copies, waits for them, and re-layouts  79.9 us (21%)
  Pallas kernels  24.3 us (6%)
  starting transfers between devices  22.4 us (6%)
  matrix products  18.2 us (5%)
  between operations  15 us (4%)
  other arithmetic  4.77 us (1%)
    all_gather x1, waiting for transfers between devices, block(): full_img_q = lax.all_gather(img_q_rows, all_axes, axis=0, tiled=True)  63.2 us
    all_gather x1, waiting for transfers between devices, block(): full_txt = lax.all_gather(txt_kv_rows, all_axes, axis=0, tiled=True)  59 us
    all_gather x1, waiting for transfers between devices, block(): full_img_kv = lax.all_gather(img_kv_rows, all_axes, axis=0, tiled=True)  54 us
    unnamed x51, local copies, waits for them, and re-layouts  50.7 us
    pallas_call x1, Pallas kernels, attend(): pl.pallas_call(attend_kernel, grid=(batch, rows // block), in_specs=[pl.B...  24.3 us
    all_to_all x1, waiting for transfers between devices, block(): lax.all_to_all(kv_image.reshape(prompts, img_rows, 2, nseq, per_dev * HD)...  20 us
    all_to_all x1, waiting for transfers between devices, block(): token_out = lax.all_to_all(head_out, 'seq', 1, 2, tiled=True)  7.96 us
  transfers between devices with their start and end apart: 9, of which 6 were waited for; matrix products, arithmetic and copies ran while one was open for 24% of the time, Pallas kernels for 7%

profile of v5, /device:TPU:0, one launch (start us, length us, event | category | flops | bytes accessed | tf_op | source)
XLA Modules:
  0.0 372.8 jit_solution(16008621661020290904)
XLA Ops:
  17.0 63.2 %all-gather.10.cloned.1.call-done = bf16[128,12,1024]{2,1,0:T(8,128)(2,1)} async-done(((bf16[1,12,1024]{2,1,0:T(8,128)(2,1)}), bf16[128,12,1024]{2,1,0:T(8,128)(2,1)}) %all-gather.10.cloned.1.call-update) | async-done | bytes 3145744 | tf_op jit(solution)/shard_map/all_gather | solution.py:106
  80.2 6.1 %reshape.139 = bf16[1536,1024,1]{1,0,2:T(8,128)(2,1)} reshape(bf16[128,12,1024]{2,1,0:T(8,128)(2,1)} %all-gather.10.cloned.1.call-done) | data formatting | bytes 6291456
  86.3 3.3 convolution_convert_fusion.2
  93.0 4.5 %all-to-all-start = ((bf16[16,2,12288]{2,1,0:T(2,128)(2,1)}), bf16[16,2,12288]{2,1,0:T(2,128)(2,1)S(1)}, u32[]{:S(2)}, u32[]{:S(2)}) async-start(bf16[16,2,12288]{2,1,0:T(2,128)(2,1)} %reshape.148), calls=%async_computation | async-start | bytes 1572864 | tf_op jit(solution)/shard_map/all_to_all | solution.py:134
  97.8 59.0 %all-gather.14.cloned.1.call-done = bf16[128,12,2048]{2,1,0:T(8,128)(2,1)} async-done(((bf16[1,12,2048]{2,1,0:T(8,128)(2,1)}), bf16[128,12,2048]{2,1,0:T(8,128)(2,1)}) %all-gather.14.cloned.1.call-update) | async-done | bytes 6291472 | tf_op jit(solution)/shard_map/all_gather | solution.py:107
  156.8 10.7 %reshape.141 = bf16[1536,2048,1]{1,0,2:T(8,128)(2,1)} reshape(bf16[128,12,2048]{2,1,0:T(8,128)(2,1)} %all-gather.14.cloned.1.call-done) | data formatting | bytes 12582912
  167.5 4.0 %convolution_convert_fusion.1 = bf16[6,12,2048]{2,1,0:T(8,128)(2,1)S(1)} fusion(bf16[1536,2048,1]{1,0,2:T(8,128)(2,1)} %reshape.141, bf16[1,6,12,1536]{3,2,1,0:T(8,128)(2,1)S(1)} %copy-done.5, f32[6,1536]{1,0:T(8,128)S(1)} %get-tuple-element.21, f32[6,1536]{1,0:T(8,128)S(1)} %get-tuple-element.22, f32[6,12]{1,0:T(8,128)S(1)} %add_rsqrt_fusion.1, ...), kind=kOutput, calls=%fused_computation.16 | convolution fusion | flops 453795840 | bytes 6881856 | tf_op jit(solution)/shard_map/prd,de->pre/dot_general | solution.py:127
  173.7 54.0 %all-gather.12.cloned.1.call-done = bf16[128,12,2048]{2,1,0:T(8,128)(2,1)} async-done(((bf16[1,12,2048]{2,1,0:T(8,128)(2,1)}), bf16[128,12,2048]{2,1,0:T(8,128)(2,1)}) %all-gather.12.cloned.1.call-update) | async-done | bytes 6291472 | tf_op jit(solution)/shard_map/all_gather | solution.py:105
  227.7 10.7 %reshape.140 = bf16[1536,2048,1]{1,0,2:T(8,128)(2,1)} reshape(bf16[128,12,2048]{2,1,0:T(8,128)(2,1)} %all-gather.12.cloned.1.call-done) | data formatting | bytes 12582912
  238.4 4.4 %all-to-all-start.2 = ((bf16[16,2,4608]{2,1,0:T(2,128)(2,1)}), bf16[16,2,4608]{2,1,0:T(2,128)(2,1)S(1)}, u32[]{:S(2)}, u32[]{:S(2)}) async-start(bf16[16,2,4608]{2,1,0:T(2,128)(2,1)} %reshape.152), calls=%async_computation.2 | async-start | bytes 589824 | tf_op jit(solution)/shard_map/all_to_all | solution.py:137
  242.9 6.6 %convolution_convert_fusion = bf16[6,64,2048]{2,1,0:T(8,128)(2,1)} fusion(bf16[1536,2048,1]{1,0,2:T(8,128)(2,1)} %reshape.140, bf16[1,6,64,1536]{3,2,1,0:T(8,128)(2,1)S(1)} %copy-done.1, f32[6,1536]{1,0:T(8,128)S(1)} %copy-done.16, f32[6,1536]{1,0:T(8,128)S(1)} %copy-done.14, f32[6,64]{1,0:T(8,128)S(1)} %add_rsqrt_fusion.2, ...), kind=kOutput, calls=%fused_computation.9 | convolution fusion | flops 2420244480 | bytes 9120768 | tf_op jit(solution)/shard_map/prd,de->pre/dot_general | solution.py:121
  249.5 4.6 %reshape.113 = bf16[6,64,2,16,64]{4,3,2,1,0:T(8,128)(2,1)S(1)} reshape(bf16[6,64,2048]{2,1,0:T(8,128)(2,1)} %convolution_convert_fusion) | data formatting | bytes 3145728 | tf_op jit(solution)/shard_map/reshape | solution.py:132
  254.1 2.8 copy.80
  256.9 5.0 %reshape.150 = bf16[16,2,24576]{2,1,0:T(2,128)(2,1)} reshape(bf16[16,2,6,64,64]{4,3,2,1,0:T(8,128)(2,1)} %bitcast.134) | data formatting | bytes 3145728
  261.9 7.4 %all-to-all-start.1 = ((bf16[16,2,24576]{2,1,0:T(2,128)(2,1)}), bf16[16,2,24576]{2,1,0:T(2,128)(2,1)}, u32[]{:S(2)}, u32[]{:S(2)}) async-start(bf16[16,2,24576]{2,1,0:T(2,128)(2,1)} %reshape.150), calls=%async_computation.1 | async-start | bytes 3145728 | tf_op jit(solution)/shard_map/all_to_all | solution.py:131
  275.5 20.0 %all-to-all-done.1 = bf16[16,2,24576]{2,1,0:T(2,128)(2,1)} async-done(((bf16[16,2,24576]{2,1,0:T(2,128)(2,1)}), bf16[16,2,24576]{2,1,0:T(2,128)(2,1)}, u32[]{:S(2)}, u32[]{:S(2)}) %all-to-all-start.1) | async-done | bytes 1572896 | tf_op jit(solution)/shard_map/all_to_all | solution.py:131
  295.5 3.8 %reshape.151 = bf16[16,2,6,64,64]{4,3,2,1,0:T(8,128)(2,1)S(1)} reshape(bf16[16,2,24576]{2,1,0:T(2,128)(2,1)} %all-to-all-done.1) | data formatting | bytes 3145728
  303.1 24.3 %shard_map.122 = bf16[6,1024,64]{2,1,0:T(8,128)(2,1)} custom-call(s32[6]{0:T(128)} %bitcast.146, bf16[6,1024,64]{2,1,0:T(8,128)(2,1)} %bitcast.142, bf16[6,1024,64]{2,1,0:T(8,128)(2,1)} %get-tuple-element.5.ki_ref, bf16[6,1024,64]{2,1,0:T(8,128)(2,1)} %get-tuple-element.4.vi_ref, bf16[6,192,64]{2,1,0:T(8,128)(2,1)} %bitcast.143, bf16[6,192,64]{2,1,0:T(8,128)(2,1)} %bitcast.144), custom_call_target="tpu_custom_call" | custom-call | flops 1912602624 | bytes 3440640 | tf_op jit(solution)/shard_map/pallas_call | solution.py:62
  327.4 2.5 copy.81
  332.1 4.9 %all-to-all-start.3 = ((bf16[16,2,12288]{2,1,0:T(2,128)(2,1)}), bf16[16,2,12288]{2,1,0:T(2,128)(2,1)S(1)}, u32[]{:S(2)}, u32[]{:S(2)}) async-start(bf16[16,2,12288]{2,1,0:T(2,128)(2,1)} %reshape.154), calls=%async_computation.3 | async-start | bytes 1572864 | tf_op jit(solution)/shard_map/all_to_all | solution.py:153
  340.5 8.0 %all-to-all-done.3 = bf16[16,2,12288]{2,1,0:T(2,128)(2,1)S(1)} async-done(((bf16[16,2,12288]{2,1,0:T(2,128)(2,1)}), bf16[16,2,12288]{2,1,0:T(2,128)(2,1)S(1)}, u32[]{:S(2)}, u32[]{:S(2)}) %all-to-all-start.3) | async-done | bytes 786464 | tf_op jit(solution)/shard_map/all_to_all | solution.py:153
  351.9 2.7 dot_general.20
  354.6 3.4 fusion.39
  361.6 3.9 %collective-permute-done = bf16[6,64,32]{1,2,0:T(8,128)(2,1)S(1)} collective-permute-done((bf16[6,64,32]{1,2,0:T(8,128)(2,1)S(1)}, bf16[6,64,32]{1,2,0:T(8,128)(2,1)S(1)}, u32[]{:S(2)}, u32[]{:S(2)}) %collective-permute-start) | collective-permute-done | bytes 24608 | tf_op jit(solution)/shard_map/ppermute | solution.py:20
  (94 shorter events, 37.9 us)
Async XLA Ops:
  7.2 8.4 %copy-start = (bf16[1,6,64,1536]{3,2,1,0:T(8,128)(2,1)S(1)}, bf16[1,6,64,1536]{3,2,1,0:T(8,128)(2,1)}, u32[]{:S(2)}) copy-start(bf16[1,6,64,1536]{3,2,1,0:T(8,128)(2,1)} %param.11) | copy-start | bytes 3538948
  7.2 8.9 %copy-start.5 = (bf16[1,6,12,1536]{3,2,1,0:T(8,128)(2,1)S(1)}, bf16[1,6,12,1536]{3,2,1,0:T(8,128)(2,1)}, u32[]{:S(2)}) copy-start(bf16[1,6,12,1536]{3,2,1,0:T(8,128)(2,1)} %param.12) | copy-start | bytes 663556
  7.2 9.0 %copy-start.12 = (f32[1,6,2,1536]{3,2,1,0:T(2,128)S(1)}, f32[1,6,2,1536]{3,2,1,0:T(2,128)}, u32[]{:S(2)}) copy-start(f32[1,6,2,1536]{3,2,1,0:T(2,128)} %param.14) | copy-start | bytes 221188
  7.2 9.1 %copy-start.7 = (f32[1,6,5,1536]{3,0,2,1:T(1,128)S(1)}, f32[1,6,5,1536]{3,0,2,1:T(1,128)}, u32[]{:S(2)}) copy-start(f32[1,6,5,1536]{3,0,2,1:T(1,128)} %param.13) | copy-start | bytes 552964
  7.2 73.0 %all-gather.10.cloned.1.call-start = ((), (), s32[]{:S(2)}) async-start(), calls=%async_computation.4 | async-start | bytes 4227072 | tf_op jit(solution)/shard_map/all_gather | solution.py:106
  8.8 148.0 %all-gather.14.cloned.1.call-start = ((), (), s32[]{:S(2)}) async-start(), calls=%async_computation.6 | async-start | bytes 8454144 | tf_op jit(solution)/shard_map/all_gather | solution.py:107
  10.3 217.4 %all-gather.12.cloned.1.call-start = ((), (), s32[]{:S(2)}) async-start(), calls=%async_computation.5 | async-start | bytes 8454144 | tf_op jit(solution)/shard_map/all_gather | solution.py:105
  11.9 325.2 %all-gather.16.cloned.1.call-start = ((), (), s32[]{:S(2)}) async-start(), calls=%async_computation.7 | async-start | bytes 6340608 | tf_op jit(solution)/shard_map/all_gather | solution.py:113
  16.9 69.4 %copy-start.13 = (f32[6,1536]{1,0:T(8,128)}, f32[6,1536]{1,0:T(8,128)S(1)}, u32[]{:S(2)}) copy-start(f32[6,1536]{1,0:T(8,128)S(1)} %get-tuple-element.19) | copy-start | bytes 110596
  16.9 69.4 %copy-start.15 = (f32[6,1536]{1,0:T(8,128)}, f32[6,1536]{1,0:T(8,128)S(1)}, u32[]{:S(2)}) copy-start(f32[6,1536]{1,0:T(8,128)S(1)} %get-tuple-element.20) | copy-start | bytes 110596
  93.0 145.4 %all-to-all-start = ((bf16[16,2,12288]{2,1,0:T(2,128)(2,1)}), bf16[16,2,12288]{2,1,0:T(2,128)(2,1)S(1)}, u32[]{:S(2)}, u32[]{:S(2)}) async-start(bf16[16,2,12288]{2,1,0:T(2,128)(2,1)} %reshape.148), calls=%async_computation | async-start | bytes 1572864 | tf_op jit(solution)/shard_map/all_to_all | solution.py:134
  173.7 69.2 %copy-start.1 = (bf16[1,6,64,1536]{3,2,1,0:T(8,128)(2,1)S(1)}, bf16[1,6,64,1536]{3,2,1,0:T(8,128)(2,1)}, u32[]{:S(2)}) copy-start(bf16[1,6,64,1536]{3,2,1,0:T(8,128)(2,1)} %param.11) | copy-start | bytes 3538948
  173.7 69.2 %copy-start.14 = (f32[6,1536]{1,0:T(8,128)S(1)}, f32[6,1536]{1,0:T(8,128)}, u32[]{:S(2)}) copy-start(f32[6,1536]{1,0:T(8,128)} %copy-done.13) | copy-start | bytes 110596
  173.7 69.2 %copy-start.16 = (f32[6,1536]{1,0:T(8,128)S(1)}, f32[6,1536]{1,0:T(8,128)}, u32[]{:S(2)}) copy-start(f32[6,1536]{1,0:T(8,128)} %copy-done.15) | copy-start | bytes 110596
  238.4 23.5 %all-to-all-start.2 = ((bf16[16,2,4608]{2,1,0:T(2,128)(2,1)}), bf16[16,2,4608]{2,1,0:T(2,128)(2,1)S(1)}, u32[]{:S(2)}, u32[]{:S(2)}) async-start(bf16[16,2,4608]{2,1,0:T(2,128)(2,1)} %reshape.152), calls=%async_computation.2 | async-start | bytes 589824 | tf_op jit(solution)/shard_map/all_to_all | solution.py:137
  261.9 7.4 %copy-start.4 = (bf16[16,2,12288]{2,1,0:T(2,128)(2,1)S(1)}, bf16[16,2,12288]{2,1,0:T(2,128)(2,1)}, u32[]{:S(2)}) copy-start(bf16[16,2,12288]{2,1,0:T(2,128)(2,1)} %copy-done.3) | copy-start | bytes 2359300
  261.9 33.6 %all-to-all-start.1 = ((bf16[16,2,24576]{2,1,0:T(2,128)(2,1)}), bf16[16,2,24576]{2,1,0:T(2,128)(2,1)}, u32[]{:S(2)}, u32[]{:S(2)}) async-start(bf16[16,2,24576]{2,1,0:T(2,128)(2,1)} %reshape.150), calls=%async_computation.1 | async-start | bytes 3145728 | tf_op jit(solution)/shard_map/all_to_all | solution.py:131
  329.9 7.1 %copy-start.10 = (f32[1,6,1,1536]{3,0,2,1:T(1,128)S(1)}, f32[1,6,1,1536]{3,0,2,1:T(1,128)}, u32[]{:S(2)}) copy-start(f32[1,6,1,1536]{3,0,2,1:T(1,128)} %get-tuple-element.10) | copy-start | bytes 110596
  329.9 7.1 %copy-start.8 = (f32[1,6,1,1536]{3,0,2,1:T(1,128)S(1)}, f32[1,6,1,1536]{3,0,2,1:T(1,128)}, u32[]{:S(2)}) copy-start(f32[1,6,1,1536]{3,0,2,1:T(1,128)} %get-tuple-element.8) | copy-start | bytes 110596
  329.9 7.1 %copy-start.9 = (f32[1,6,1,1536]{3,0,2,1:T(1,128)S(1)}, f32[1,6,1,1536]{3,0,2,1:T(1,128)}, u32[]{:S(2)}) copy-start(f32[1,6,1,1536]{3,0,2,1:T(1,128)} %get-tuple-element.11) | copy-start | bytes 110596
  332.1 16.4 %all-to-all-start.3 = ((bf16[16,2,12288]{2,1,0:T(2,128)(2,1)}), bf16[16,2,12288]{2,1,0:T(2,128)(2,1)S(1)}, u32[]{:S(2)}, u32[]{:S(2)}) async-start(bf16[16,2,12288]{2,1,0:T(2,128)(2,1)} %reshape.154), calls=%async_computation.3 | async-start | bytes 1572864 | tf_op jit(solution)/shard_map/all_to_all | solution.py:153
  349.7 4.9 %copy-start.2 = (bf16[1,6,64,1536]{3,2,1,0:T(8,128)(2,1)S(1)}, bf16[1,6,64,1536]{3,2,1,0:T(8,128)(2,1)}, u32[]{:S(2)}) copy-start(bf16[1,6,64,1536]{3,2,1,0:T(8,128)(2,1)} %param.11) | copy-start | bytes 3538948
  358.0 7.6 %copy-start.11 = (f32[6,64,32]{1,2,0:T(8,128)S(1)}, f32[6,64,32]{1,2,0:T(8,128)}, u32[]{:S(2)}) copy-start(f32[6,64,32]{1,2,0:T(8,128)} %param.20) | copy-start | bytes 147460
  359.8 5.7 %collective-permute-start = (bf16[6,64,32]{1,2,0:T(8,128)(2,1)S(1)}, bf16[6,64,32]{1,2,0:T(8,128)(2,1)S(1)}, u32[]{:S(2)}, u32[]{:S(2)}) collective-permute-start(bf16[6,64,32]{1,2,0:T(8,128)(2,1)S(1)} %dynamic-slice_convert_fusion), channel_id=1, source_target_pairs={{0,64},{64,0},{1,65},{65,1},{2,66},{66,2},{3,67},{67,3},{4,68},{68... | collective-permute-start | bytes 73736 | tf_op jit(solution)/shard_map/ppermute | solution.py:20
  (2 other events, 5.4 us)
Sparse Core Ops, SparseCore 0:
  11.2 68.9 all-gather.9
  83.9 72.8 all-gather.13
  160.5 67.1 all-gather.11
  230.7 73.4 all-gather.15

commit v6 on v4

--- a/solution.py
+++ b/solution.py
@@ -99,15 +99,22 @@
     nseq = lax.axis_size("seq")
 
     attn_width = w_img_qkv.shape[1] // 3
-    full_txt = lax.all_gather(w_txt_qkv[:, attn_width:], all_axes, axis=0, tiled=True)
-    full_img = lax.all_gather(w_img_qkv, all_axes, axis=0, tiled=True)
     out_rows, out_cols = w_out.shape
     head_rows, head_cols = w_head.shape
+    local_rows = w_img_qkv.shape[0]
     head_flat = w_head.reshape(1, head_rows * head_cols)
     head_flat = jnp.pad(head_flat, ((0, 0), (0, out_cols - head_rows * head_cols)))
-    packed = lax.all_gather(
-        jnp.concatenate([w_out, head_flat], axis=0), all_axes, axis=0, tiled=False
-    )
+    tail = jnp.concatenate([w_out, head_flat], axis=0)
+    tail_width = tail.size // local_rows
+    img_width = w_img_qkv.shape[1]
+    txt_width = w_txt_qkv.shape[1] - attn_width
+    local_all = jnp.concatenate(
+        [w_img_qkv, w_txt_qkv[:, attn_width:], tail.reshape(local_rows, tail_width)], axis=1
+    )
+    gathered = lax.all_gather(local_all, all_axes, axis=0, tiled=False)
+    full_img = gathered[:, :, :img_width].reshape(-1, img_width)
+    full_txt = gathered[:, :, img_width : img_width + txt_width].reshape(-1, txt_width)
+    packed = gathered[:, :, img_width + txt_width :].reshape(-1, out_rows + 1, out_cols)
     full_out = packed[:, :out_rows].reshape(-1, out_cols)
     full_head = packed[:, out_rows, : head_rows * head_cols].reshape(-1, head_cols)
 

time: 333 us -> 327 us (0.982)
  waiting for transfers between devices: 168 us -> 122 us
  local copies, waits for them, and re-layouts: 84.2 us -> 118 us
  other arithmetic: 5.4 us -> 8.97 us
    slice x0 -> x6, local copies, waits for them, and re-layouts: none -> 32 us  [the longest x1 10.9 us: local(): full_img = gathered[:, :, :img_width].reshape(-1, img_width)]
    all_gather x3 -> x1, waiting for transfers between devices: 121 us -> 91 us  [local(): gathered = lax.all_gather(local_all, all_axes, axis=0, tiled=False)]
    reshape x0 -> x3, local copies, waits for them, and re-layouts: none -> 24.5 us  [the longest x1 13.7 us: local(): full_img = gathered[:, :, :img_width].reshape(-1, img_width)]
    unnamed x30 -> x38, local copies, waits for them, and re-layouts: 50.2 us -> 29.6 us
    all_to_all x1, waiting for transfers between devices: 9.26 us -> 0.01 us  [local(): token_out = lax.all_to_all(head_out, 'seq', 1, 2, tiled=True)]
    all_to_all x1, waiting for transfers between devices: 34 us -> 28.7 us  [local(): img_heads = lax.all_to_all(img_split, 'seq', 3, 1, tiled=True)]
  transfers between devices with their start and end apart: 7 -> 5, of which waited for: 5 -> 3; matrix products, arithmetic and copies ran while one was open for 27% -> 18% of each run, Pallas kernels for 7% -> 0%
where the time goes in v6:
time: 327 us; the launch traced here: 325 us
  waiting for transfers between devices  122 us (37%)
  local copies, waits for them, and re-layouts  118 us (36%)
  Pallas kernels  24.3 us (7%)
  starting transfers between devices  19.9 us (6%)
  matrix products  16.5 us (5%)
  between operations  15.1 us (5%)
  other arithmetic  8.97 us (3%)
    all_gather x1, waiting for transfers between devices, local(): gathered = lax.all_gather(local_all, all_axes, axis=0, tiled=False)  91 us
    unnamed x38, local copies, waits for them, and re-layouts  29.6 us
    all_to_all x1, waiting for transfers between devices, local(): img_heads = lax.all_to_all(img_split, 'seq', 3, 1, tiled=True)  28.7 us
    pallas_call x1, Pallas kernels, attend(): pl.pallas_call(attend_kernel, grid=(batch, rows // block), in_specs=[pl.B...  24.3 us
    reshape x1, local copies, waits for them, and re-layouts, local(): full_img = gathered[:, :, :img_width].reshape(-1, img_width)  13.7 us
    slice x1, local copies, waits for them, and re-layouts, local(): full_img = gathered[:, :, :img_width].reshape(-1, img_width)  10.9 us
    reshape x1, local copies, waits for them, and re-layouts, local(): gathered[:, :, img_width:img_width + txt_width].reshape(-1, txt_width)  10.8 us
    reshape x2, local copies, waits for them, and re-layouts, local(): img_split = qkv_image.reshape(prompts, img_rows, 3, nseq, per_dev * HD)  10.5 us
  transfers between devices with their start and end apart: 5, of which 3 were waited for; matrix products, arithmetic and copies ran while one was open for 18% of the time, Pallas kernels for 0%

profile of v6, /device:TPU:0, one launch (start us, length us, event | category | flops | bytes accessed | tf_op | source)
XLA Modules:
  0.0 324.7 jit_solution(8345588816842294810)
XLA Ops:
  17.1 91.0 %all-gather.4.cloned.1.call-done = bf16[128,12,6272]{2,1,0:T(8,128)(2,1)} async-done(((bf16[1,12,6272]{2,1,0:T(8,128)(2,1)}), bf16[128,12,6272]{2,1,0:T(8,128)(2,1)}) %all-gather.4.cloned.1.call-update) | async-done | bytes 19267600 | tf_op jit(solution)/shard_map/all_gather | solution.py:114
  108.1 10.9 %slice.72 = bf16[128,12,3072]{2,1,0:T(8,128)(2,1)} slice(bf16[128,12,6272]{2,1,0:T(8,128)(2,1)} %all-gather.4.cloned.1.call-done), slice={[0:128], [0:12], [0:3072]} | slice | bytes 18874368 | tf_op jit(solution)/shard_map/slice | solution.py:115
  119.0 13.7 %reshape.146 = bf16[1536,3072,1]{1,0,2:T(8,128)(2,1)} reshape(bf16[128,12,3072]{2,1,0:T(8,128)(2,1)} %slice.72) | data formatting | bytes 18874368 | tf_op jit(solution)/shard_map/reshape | solution.py:115
  132.7 8.4 %slice.76 = bf16[128,12,2048]{2,1,0:T(8,128)(2,1)} slice(bf16[128,12,6272]{2,1,0:T(8,128)(2,1)} %all-gather.4.cloned.1.call-done), slice={[0:128], [0:12], [3072:5120]} | slice | bytes 12582912 | tf_op jit(solution)/shard_map/slice | solution.py:116
  141.1 10.8 %reshape.147 = bf16[1536,2048,1]{1,0,2:T(8,128)(2,1)} reshape(bf16[128,12,2048]{2,1,0:T(8,128)(2,1)} %slice.76) | data formatting | bytes 12582912 | tf_op jit(solution)/shard_map/reshape | solution.py:116
  151.8 4.0 %convolution_convert_fusion.1 = bf16[6,12,2048]{2,1,0:T(8,128)(2,1)S(1)} fusion(bf16[1536,2048,1]{1,0,2:T(8,128)(2,1)} %reshape.147, bf16[1,6,12,1536]{3,2,1,0:T(8,128)(2,1)S(1)} %copy-done.2, f32[6,1536]{1,0:T(8,128)S(1)} %get-tuple-element.22, f32[6,1536]{1,0:T(8,128)S(1)} %get-tuple-element.23, f32[6,12]{1,0:T(8,128)S(1)} %add_rsqrt_fusion.1, ...), kind=kOutput, calls=%fused_computation.17 | convolution fusion | flops 453795840 | bytes 6881856 | tf_op jit(solution)/shard_map/prd,de->pre/dot_general | solution.py:128
  157.9 5.9 %all-to-all-start.1 = ((bf16[16,2,4608]{2,1,0:T(2,128)(2,1)}), bf16[16,2,4608]{2,1,0:T(2,128)(2,1)}, u32[]{:S(2)}, u32[]{:S(2)}) async-start(bf16[16,2,4608]{2,1,0:T(2,128)(2,1)} %reshape.154), calls=%async_computation.1 | async-start | bytes 589824 | tf_op jit(solution)/shard_map/all_to_all | solution.py:135
  163.8 8.3 %convolution_convert_fusion = bf16[6,64,3072]{2,1,0:T(8,128)(2,1)S(1)} fusion(bf16[1536,3072,1]{1,0,2:T(8,128)(2,1)} %reshape.146, bf16[1,6,64,1536]{3,2,1,0:T(8,128)(2,1)S(1)} %copy-done, f32[6,1536]{1,0:T(8,128)} %get-tuple-element.21, f32[6,1536]{1,0:T(8,128)} %get-tuple-element.20, f32[6,64]{1,0:T(8,128)S(1)} %add_rsqrt_fusion.2, ...), kind=kOutput, calls=%fused_computation | convolution fusion | flops 3628597248 | bytes 13052928 | tf_op jit(solution)/shard_map/prd,de->pre/dot_general | solution.py:125
  172.1 4.8 %reshape.125 = bf16[6,64,3,16,64]{4,3,2,1,0:T(8,128)(2,1)} reshape(bf16[6,64,3072]{2,1,0:T(8,128)(2,1)S(1)} %convolution_convert_fusion) | data formatting | bytes 4718592 | tf_op jit(solution)/shard_map/reshape | solution.py:132
  176.9 5.7 %copy.96 = bf16[6,64,3,16,64]{4,1,0,2,3:T(8,128)(2,1)} copy(bf16[6,64,3,16,64]{4,3,2,1,0:T(8,128)(2,1)} %reshape.125) | data formatting | bytes 4718592 | tf_op jit(solution)/shard_map/reshape | solution.py:132
  182.6 7.8 %reshape.152 = bf16[16,2,36864]{2,1,0:T(2,128)(2,1)} reshape(bf16[16,3,6,64,64]{4,3,2,1,0:T(8,128)(2,1)} %bitcast.109) | data formatting | bytes 4718592
  190.4 7.2 %all-to-all-start = ((bf16[16,2,36864]{2,1,0:T(2,128)(2,1)}), bf16[16,2,36864]{2,1,0:T(2,128)(2,1)S(1)}, u32[]{:S(2)}, u32[]{:S(2)}) async-start(bf16[16,2,36864]{2,1,0:T(2,128)(2,1)} %reshape.152), calls=%async_computation | async-start | bytes 4718592 | tf_op jit(solution)/shard_map/all_to_all | solution.py:133
  202.3 28.7 %all-to-all-done = bf16[16,2,36864]{2,1,0:T(2,128)(2,1)S(1)} async-done(((bf16[16,2,36864]{2,1,0:T(2,128)(2,1)}), bf16[16,2,36864]{2,1,0:T(2,128)(2,1)S(1)}, u32[]{:S(2)}, u32[]{:S(2)}) %all-to-all-start) | async-done | bytes 2359328 | tf_op jit(solution)/shard_map/all_to_all | solution.py:133
  231.0 5.3 %reshape.153 = bf16[16,3,6,64,64]{4,3,2,1,0:T(8,128)(2,1)} reshape(bf16[16,2,36864]{2,1,0:T(2,128)(2,1)S(1)} %all-to-all-done) | data formatting | bytes 4718592
  236.3 3.4 %bitcast_bitcast_fusion = bf16[6,16,64,3,1,64]{5,2,0,3,1,4:T(8,128)(2,1)S(1)} fusion(bf16[16,3,6,64,64]{4,3,2,1,0:T(8,128)(2,1)} %reshape.153), kind=kLoop, calls=%fused_computation.77 | loop fusion | bytes 4718592 | tf_op jit(solution)/shard_map/all_to_all | solution.py:133
  243.6 24.3 %shard_map.122 = bf16[6,1024,64]{2,1,0:T(8,128)(2,1)} custom-call(s32[6]{0:T(128)} %bitcast.121, bf16[6,1024,64]{2,1,0:T(8,128)(2,1)} %get-tuple-element.6.q_ref, bf16[6,1024,64]{2,1,0:T(8,128)(2,1)} %get-tuple-element.5.ki_ref, bf16[6,1024,64]{2,1,0:T(8,128)(2,1)} %get-tuple-element.4.vi_ref, bf16[6,192,64]{2,1,0:T(8,128)(2,1)} %bitcast.118, ...), custom_call_target="tpu_custom_call" | custom-call | flops 1912602624 | bytes 3440640 | tf_op jit(solution)/shard_map/pallas_call | solution.py:62
  272.7 4.5 %all-to-all-start.2 = ((bf16[16,2,12288]{2,1,0:T(2,128)(2,1)}), bf16[16,2,12288]{2,1,0:T(2,128)(2,1)}, u32[]{:S(2)}, u32[]{:S(2)}) async-start(bf16[16,2,12288]{2,1,0:T(2,128)(2,1)} %reshape.156), calls=%async_computation.2 | async-start | bytes 1572864 | tf_op jit(solution)/shard_map/all_to_all | solution.py:150
  278.5 4.9 %slice.79 = bf16[128,12,1152]{2,1,0:T(8,128)(2,1)} slice(bf16[128,12,6272]{2,1,0:T(8,128)(2,1)} %all-gather.4.cloned.1.call-done), slice={[0:128], [0:12], [5120:6272]} | slice | bytes 7077888 | tf_op jit(solution)/shard_map/slice | solution.py:117
  283.4 5.6 %copy.71 = bf16[128,12,1152]{0,2,1:T(8,128)(2,1)S(1)} copy(bf16[128,12,1152]{2,1,0:T(8,128)(2,1)} %slice.79) | data formatting | bytes 7077888
  291.6 5.1 %copy.57 = bf16[128,8,1536]{2,1,0:T(8,128)(2,1)} copy(bf16[128,8,1536]{0,2,1:T(8,128)(2,1)} %slice.80) | data formatting | bytes 6291456 | tf_op jit(solution)/shard_map/slice | solution.py:118
  297.8 3.5 %reshape.157 = bf16[1024,1,6,64]{3,2,1,0:T(8,128)(2,1)S(1)} reshape(bf16[16,2,12288]{2,1,0:T(2,128)(2,1)} %all-to-all-done.2) | data formatting | bytes 1572864
  303.5 2.7 dot_general.16
  306.2 3.4 %fusion.48 = (f32[6,64]{1,0:T(8,128)S(1)}, f32[6,64,1536]{2,1,0:T(8,128)S(1)}) fusion(bf16[6,64,1024]{2,1,0:T(8,128)(2,1)S(1)} %dot_general.16, bf16[128,8,1536]{2,1,0:T(8,128)(2,1)} %copy.57, f32[6,1536]{1,0:T(8,128)S(1)} %bitcast.120, bf16[1,6,64,1536]{3,2,1,0:T(8,128)(2,1)S(1)} %copy-done.1), kind=kOutput, calls=%fused_computation.76 | convolution fusion | flops 1210318464 | bytes 7509504 | tf_op jit(solution)/shard_map/dot_general | solution.py:153
  314.6 2.6 collective-permute-done
  (76 shorter events, 37.2 us)
Async XLA Ops:
  7.2 8.0 %copy-start = (bf16[1,6,64,1536]{3,2,1,0:T(8,128)(2,1)S(1)}, bf16[1,6,64,1536]{3,2,1,0:T(8,128)(2,1)}, u32[]{:S(2)}) copy-start(bf16[1,6,64,1536]{3,2,1,0:T(8,128)(2,1)} %param.11) | copy-start | bytes 3538948
  7.2 8.5 %copy-start.10 = (f32[1,6,2,1536]{3,2,1,0:T(2,128)S(1)}, f32[1,6,2,1536]{3,2,1,0:T(2,128)}, u32[]{:S(2)}) copy-start(f32[1,6,2,1536]{3,2,1,0:T(2,128)} %param.14) | copy-start | bytes 221188
  7.2 8.5 %copy-start.5 = (f32[1,6,5,1536]{3,0,2,1:T(1,128)S(1)}, f32[1,6,5,1536]{3,0,2,1:T(1,128)}, u32[]{:S(2)}) copy-start(f32[1,6,5,1536]{3,0,2,1:T(1,128)} %param.13) | copy-start | bytes 552964
  7.2 100.9 %all-gather.4.cloned.1.call-start = ((), (), s32[]{:S(2)}) async-start(), calls=%async_computation.3 | async-start | bytes 25890816 | tf_op jit(solution)/shard_map/all_gather | solution.py:114
  141.1 10.8 %copy-start.2 = (bf16[1,6,12,1536]{3,2,1,0:T(8,128)(2,1)S(1)}, bf16[1,6,12,1536]{3,2,1,0:T(8,128)(2,1)}, u32[]{:S(2)}) copy-start(bf16[1,6,12,1536]{3,2,1,0:T(8,128)(2,1)} %param.12) | copy-start | bytes 663556
  157.9 32.5 %all-to-all-start.1 = ((bf16[16,2,4608]{2,1,0:T(2,128)(2,1)}), bf16[16,2,4608]{2,1,0:T(2,128)(2,1)}, u32[]{:S(2)}, u32[]{:S(2)}) async-start(bf16[16,2,4608]{2,1,0:T(2,128)(2,1)} %reshape.154), calls=%async_computation.1 | async-start | bytes 589824 | tf_op jit(solution)/shard_map/all_to_all | solution.py:135
  190.4 40.6 %all-to-all-start = ((bf16[16,2,36864]{2,1,0:T(2,128)(2,1)}), bf16[16,2,36864]{2,1,0:T(2,128)(2,1)S(1)}, u32[]{:S(2)}, u32[]{:S(2)}) async-start(bf16[16,2,36864]{2,1,0:T(2,128)(2,1)} %reshape.152), calls=%async_computation | async-start | bytes 4718592 | tf_op jit(solution)/shard_map/all_to_all | solution.py:133
  270.4 6.8 %copy-start.8 = (f32[1,6,1,1536]{3,0,2,1:T(1,128)S(1)}, f32[1,6,1,1536]{3,0,2,1:T(1,128)}, u32[]{:S(2)}) copy-start(f32[1,6,1,1536]{3,0,2,1:T(1,128)} %get-tuple-element.11) | copy-start | bytes 110596
  270.4 7.4 %copy-start.6 = (f32[1,6,1,1536]{3,0,2,1:T(1,128)S(1)}, f32[1,6,1,1536]{3,0,2,1:T(1,128)}, u32[]{:S(2)}) copy-start(f32[1,6,1,1536]{3,0,2,1:T(1,128)} %get-tuple-element.9) | copy-start | bytes 110596
  270.4 7.4 %copy-start.7 = (f32[1,6,1,1536]{3,0,2,1:T(1,128)S(1)}, f32[1,6,1,1536]{3,0,2,1:T(1,128)}, u32[]{:S(2)}) copy-start(f32[1,6,1,1536]{3,0,2,1:T(1,128)} %get-tuple-element.12) | copy-start | bytes 110596
  272.7 25.2 %all-to-all-start.2 = ((bf16[16,2,12288]{2,1,0:T(2,128)(2,1)}), bf16[16,2,12288]{2,1,0:T(2,128)(2,1)}, u32[]{:S(2)}, u32[]{:S(2)}) async-start(bf16[16,2,12288]{2,1,0:T(2,128)(2,1)} %reshape.156), calls=%async_computation.2 | async-start | bytes 1572864 | tf_op jit(solution)/shard_map/all_to_all | solution.py:150
  291.6 5.1 %copy-start.3 = (bf16[128,1,768]{0,2,1:T(8,128)(2,1)S(1)}, bf16[128,1,768]{0,2,1:T(8,128)(2,1)}, u32[]{:S(2)}) copy-start(bf16[128,1,768]{0,2,1:T(8,128)(2,1)} %slice.81) | copy-start | bytes 589828
  301.3 4.9 %copy-start.1 = (bf16[1,6,64,1536]{3,2,1,0:T(8,128)(2,1)S(1)}, bf16[1,6,64,1536]{3,2,1,0:T(8,128)(2,1)}, u32[]{:S(2)}) copy-start(bf16[1,6,64,1536]{3,2,1,0:T(8,128)(2,1)} %param.11) | copy-start | bytes 3538948
  301.3 4.9 %copy-start.11 = (f32[1,6,1,1536]{3,1,2,0:T(8,128)S(1)}, f32[1,6,1,1536]{3,1,2,0:T(8,128)}, u32[]{:S(2)}) copy-start(f32[1,6,1,1536]{3,1,2,0:T(8,128)} %copy.95) | copy-start | bytes 110596
  309.6 1.0 copy-start.4
  309.6 1.0 copy-start.12
  309.6 1.0 copy-start.13
  309.6 7.5 %copy-start.9 = (f32[6,64,32]{1,2,0:T(8,128)S(1)}, f32[6,64,32]{1,2,0:T(8,128)}, u32[]{:S(2)}) copy-start(f32[6,64,32]{1,2,0:T(8,128)} %param.20) | copy-start | bytes 147460
  311.5 5.7 %collective-permute-start = (bf16[6,64,32]{1,2,0:T(8,128)(2,1)S(1)}, bf16[6,64,32]{1,2,0:T(8,128)(2,1)S(1)}, u32[]{:S(2)}, u32[]{:S(2)}) collective-permute-start(bf16[6,64,32]{1,2,0:T(8,128)(2,1)S(1)} %dynamic-slice_convert_fusion), channel_id=1, source_target_pairs={{0,64},{64,0},{1,65},{65,1},{2,66},{66,2},{3,67},{67,3},{4,68},{68... | collective-permute-start | bytes 73736 | tf_op jit(solution)/shard_map/ppermute | solution.py:20
Sparse Core Ops, SparseCore 0:
  11.5 96.5 all-gather.3

commit v7 on v6

--- a/solution.py
+++ b/solution.py
@@ -112,9 +112,10 @@
         [w_img_qkv, w_txt_qkv[:, attn_width:], tail.reshape(local_rows, tail_width)], axis=1
     )
     gathered = lax.all_gather(local_all, all_axes, axis=0, tiled=False)
-    full_img = gathered[:, :, :img_width].reshape(-1, img_width)
-    full_txt = gathered[:, :, img_width : img_width + txt_width].reshape(-1, txt_width)
-    packed = gathered[:, :, img_width + txt_width :].reshape(-1, out_rows + 1, out_cols)
+    full_all = gathered.reshape(-1, local_all.shape[1])
+    full_img = full_all[:, :img_width]
+    full_txt = full_all[:, img_width : img_width + txt_width]
+    packed = full_all[:, img_width + txt_width :].reshape(-1, out_rows + 1, out_cols)
     full_out = packed[:, :out_rows].reshape(-1, out_cols)
     full_head = packed[:, out_rows, : head_rows * head_cols].reshape(-1, head_cols)
 

time: 327 us -> 301 us (0.920)
  local copies, waits for them, and re-layouts: 118 us -> 91.7 us
    slice x5 -> x2, local copies, waits for them, and re-layouts: 31.1 us -> 2 us  [local(): full_all[:, img_width + txt_width:].reshape(-1, out_rows + 1, out_cols)]
    unnamed x38 -> x36, local copies, waits for them, and re-layouts: 29.6 us -> 50.4 us
    reshape x2 -> x1, local copies, waits for them, and re-layouts: 24.5 us -> 5.47 us  [local(): full_all[:, img_width + txt_width:].reshape(-1, out_rows + 1, out_cols)]
  transfers between devices with their start and end apart: 5 -> 5, of which waited for: 3 -> 3; matrix products, arithmetic and copies ran while one was open for 18% -> 16% of each run, Pallas kernels for 0% -> 0%
where the time goes in v7:
time: 301 us; the launch traced here: 298 us
  waiting for transfers between devices  122 us (41%)
  local copies, waits for them, and re-layouts  91.7 us (30%)
  Pallas kernels  24.3 us (8%)
  starting transfers between devices  20 us (7%)
  matrix products  15.9 us (5%)
  between operations  15.1 us (5%)
  other arithmetic  8.98 us (3%)
    all_gather x1, waiting for transfers between devices, local(): gathered = lax.all_gather(local_all, all_axes, axis=0, tiled=False)  91 us
    unnamed x36, local copies, waits for them, and re-layouts  50.4 us
    all_to_all x1, waiting for transfers between devices, local(): img_heads = lax.all_to_all(img_split, 'seq', 3, 1, tiled=True)  28.7 us
    pallas_call x1, Pallas kernels, attend(): pl.pallas_call(attend_kernel, grid=(batch, rows // block), in_specs=[pl.B...  24.3 us
    reshape x2, local copies, waits for them, and re-layouts, local(): img_split = qkv_image.reshape(prompts, img_rows, 3, nseq, per_dev * HD)  10.5 us
    dot_general x1, matrix products, local(): jnp.einsum('prd,de->pre', image_in, full_img, preferred_element_type=jnp....  7.7 us
    all_to_all x1, starting transfers between devices, local(): img_heads = lax.all_to_all(img_split, 'seq', 3, 1, tiled=True)  7.18 us
  transfers between devices with their start and end apart: 5, of which 3 were waited for; matrix products, arithmetic and copies ran while one was open for 16% of the time, Pallas kernels for 0%

profile of v7, /device:TPU:0, one launch (start us, length us, event | category | flops | bytes accessed | tf_op | source)
XLA Modules:
  0.0 298.4 jit_solution(14510468621192711525)
XLA Ops:
  17.0 91.0 %all-gather.4.cloned.1.call-done = bf16[128,12,6272]{2,1,0:T(8,128)(2,1)} async-done(((bf16[1,12,6272]{2,1,0:T(8,128)(2,1)}), bf16[128,12,6272]{2,1,0:T(8,128)(2,1)}) %all-gather.4.cloned.1.call-update) | async-done | bytes 19267600 | tf_op jit(solution)/shard_map/all_gather | solution.py:114
  108.1 26.5 %reshape.139 = bf16[1536,6272]{1,0:T(8,128)(2,1)} reshape(bf16[128,12,6272]{2,1,0:T(8,128)(2,1)} %all-gather.4.cloned.1.call-done) | data formatting | bytes 38535168
  134.5 4.0 %fusion.13 = bf16[6,12,2048]{2,1,0:T(8,128)(2,1)S(1)} fusion(bf16[1536,6272]{1,0:T(8,128)(2,1)} %reshape.139, bf16[1,6,12,1536]{3,2,1,0:T(8,128)(2,1)S(1)} %copy-done.2, f32[6,1536]{1,0:T(8,128)S(1)} %get-tuple-element.22, f32[6,1536]{1,0:T(8,128)S(1)} %get-tuple-element.23, f32[6,12]{1,0:T(8,128)S(1)} %add_rsqrt_fusion.1, ...), kind=kOutput, calls=%fused_computation.20 | convolution fusion | flops 453795840 | bytes 6881856 | tf_op jit(solution)/shard_map/prd,de->pre/dot_general | solution.py:129
  140.7 5.9 %all-to-all-start.1 = ((bf16[16,2,4608]{2,1,0:T(2,128)(2,1)}), bf16[16,2,4608]{2,1,0:T(2,128)(2,1)}, u32[]{:S(2)}, u32[]{:S(2)}) async-start(bf16[16,2,4608]{2,1,0:T(2,128)(2,1)} %reshape.147), calls=%async_computation.1 | async-start | bytes 589824 | tf_op jit(solution)/shard_map/all_to_all | solution.py:136
  146.6 7.7 %fusion.2 = bf16[6,64,3072]{2,1,0:T(8,128)(2,1)S(1)} fusion(bf16[1536,6272]{1,0:T(8,128)(2,1)} %reshape.139, bf16[1,6,64,1536]{3,2,1,0:T(8,128)(2,1)S(1)} %copy-done, f32[6,1536]{1,0:T(8,128)} %get-tuple-element.21, f32[6,1536]{1,0:T(8,128)} %get-tuple-element.20, f32[6,64]{1,0:T(8,128)S(1)} %add_rsqrt_fusion.2, f32[6,64]{1,0:T(8,128)S(1)} %broadcast_multiply_fusion.2), kind=kOutput, calls=%fused_computation.4 | convolution fusion | flops 3628597248 | bytes 13077504 | tf_op jit(solution)/shard_map/prd,de->pre/dot_general | solution.py:126
  154.3 4.8 %reshape.120 = bf16[6,64,3,16,64]{4,3,2,1,0:T(8,128)(2,1)} reshape(bf16[6,64,3072]{2,1,0:T(8,128)(2,1)S(1)} %fusion.2) | data formatting | bytes 4718592 | tf_op jit(solution)/shard_map/reshape | solution.py:133
  159.1 5.7 %copy.75 = bf16[6,64,3,16,64]{4,1,0,2,3:T(8,128)(2,1)} copy(bf16[6,64,3,16,64]{4,3,2,1,0:T(8,128)(2,1)} %reshape.120) | data formatting | bytes 4718592 | tf_op jit(solution)/shard_map/reshape | solution.py:133
  164.8 7.9 %reshape.145 = bf16[16,2,36864]{2,1,0:T(2,128)(2,1)} reshape(bf16[16,3,6,64,64]{4,3,2,1,0:T(8,128)(2,1)} %bitcast.126) | data formatting | bytes 4718592
  172.7 7.2 %all-to-all-start = ((bf16[16,2,36864]{2,1,0:T(2,128)(2,1)}), bf16[16,2,36864]{2,1,0:T(2,128)(2,1)S(1)}, u32[]{:S(2)}, u32[]{:S(2)}) async-start(bf16[16,2,36864]{2,1,0:T(2,128)(2,1)} %reshape.145), calls=%async_computation | async-start | bytes 4718592 | tf_op jit(solution)/shard_map/all_to_all | solution.py:134
  184.5 28.7 %all-to-all-done = bf16[16,2,36864]{2,1,0:T(2,128)(2,1)S(1)} async-done(((bf16[16,2,36864]{2,1,0:T(2,128)(2,1)}), bf16[16,2,36864]{2,1,0:T(2,128)(2,1)S(1)}, u32[]{:S(2)}, u32[]{:S(2)}) %all-to-all-start) | async-done | bytes 2359328 | tf_op jit(solution)/shard_map/all_to_all | solution.py:134
  213.3 5.2 %reshape.146 = bf16[16,3,6,64,64]{4,3,2,1,0:T(8,128)(2,1)} reshape(bf16[16,2,36864]{2,1,0:T(2,128)(2,1)S(1)} %all-to-all-done) | data formatting | bytes 4718592
  218.5 3.4 %bitcast_bitcast_fusion = bf16[6,16,64,3,1,64]{5,2,0,3,1,4:T(8,128)(2,1)S(1)} fusion(bf16[16,3,6,64,64]{4,3,2,1,0:T(8,128)(2,1)} %reshape.146), kind=kLoop, calls=%fused_computation.78 | loop fusion | bytes 4718592 | tf_op jit(solution)/shard_map/all_to_all | solution.py:134
  223.5 2.2 slice_bitcast_fusion.14
  225.8 24.3 %shard_map.122 = bf16[6,1024,64]{2,1,0:T(8,128)(2,1)} custom-call(s32[6]{0:T(128)} %bitcast.136, bf16[6,1024,64]{2,1,0:T(8,128)(2,1)} %get-tuple-element.6.q_ref, bf16[6,1024,64]{2,1,0:T(8,128)(2,1)} %get-tuple-element.5.ki_ref, bf16[6,1024,64]{2,1,0:T(8,128)(2,1)} %get-tuple-element.4.vi_ref, bf16[6,192,64]{2,1,0:T(8,128)(2,1)} %bitcast.133, ...), custom_call_target="tpu_custom_call" | custom-call | flops 1912602624 | bytes 3440640 | tf_op jit(solution)/shard_map/pallas_call | solution.py:62
  250.1 2.5 copy.76
  252.6 2.2 reshape.149
  254.8 4.5 %all-to-all-start.2 = ((bf16[16,2,12288]{2,1,0:T(2,128)(2,1)}), bf16[16,2,12288]{2,1,0:T(2,128)(2,1)}, u32[]{:S(2)}, u32[]{:S(2)}) async-start(bf16[16,2,12288]{2,1,0:T(2,128)(2,1)} %reshape.149), calls=%async_computation.2 | async-start | bytes 1572864 | tf_op jit(solution)/shard_map/all_to_all | solution.py:151
  262.6 5.5 %reshape.123 = bf16[128,9,1536]{2,1,0:T(8,128)(2,1)} reshape(bf16[1536,1152]{1,0:T(8,128)(2,1)S(1)} %slice-done) | data formatting | bytes 7077888 | tf_op jit(solution)/shard_map/reshape | solution.py:118
  268.0 2.4 slice_reduce_fusion
  271.5 3.5 %reshape.150 = bf16[1024,1,6,64]{3,2,1,0:T(8,128)(2,1)S(1)} reshape(bf16[16,2,12288]{2,1,0:T(2,128)(2,1)} %all-to-all-done.2) | data formatting | bytes 1572864
  277.1 2.7 dot_general.16
  279.9 3.4 %fusion.45 = (f32[6,64]{1,0:T(8,128)S(1)}, f32[6,64,1536]{2,1,0:T(8,128)S(1)}) fusion(bf16[6,64,1024]{2,1,0:T(8,128)(2,1)S(1)} %dot_general.16, bf16[128,9,1536]{2,1,0:T(8,128)(2,1)} %reshape.123, f32[6,1536]{1,0:T(8,128)S(1)} %bitcast.135, bf16[1,6,64,1536]{3,2,1,0:T(8,128)(2,1)S(1)} %copy-done.1), kind=kOutput, calls=%fused_computation.77 | convolution fusion | flops 1210318464 | bytes 7509504 | tf_op jit(solution)/shard_map/dot_general | solution.py:154
  285.1 2.3 collective-permute-start
  288.2 2.6 collective-permute-done
  (69 shorter events, 27.2 us)
Async XLA Ops:
  7.2 8.0 %copy-start = (bf16[1,6,64,1536]{3,2,1,0:T(8,128)(2,1)S(1)}, bf16[1,6,64,1536]{3,2,1,0:T(8,128)(2,1)}, u32[]{:S(2)}) copy-start(bf16[1,6,64,1536]{3,2,1,0:T(8,128)(2,1)} %param.11) | copy-start | bytes 3538948
  7.2 8.5 %copy-start.9 = (f32[1,6,2,1536]{3,2,1,0:T(2,128)S(1)}, f32[1,6,2,1536]{3,2,1,0:T(2,128)}, u32[]{:S(2)}) copy-start(f32[1,6,2,1536]{3,2,1,0:T(2,128)} %param.14) | copy-start | bytes 221188
  7.2 8.5 %copy-start.4 = (f32[1,6,5,1536]{3,0,2,1:T(1,128)S(1)}, f32[1,6,5,1536]{3,0,2,1:T(1,128)}, u32[]{:S(2)}) copy-start(f32[1,6,5,1536]{3,0,2,1:T(1,128)} %param.13) | copy-start | bytes 552964
  7.2 100.9 %all-gather.4.cloned.1.call-start = ((), (), s32[]{:S(2)}) async-start(), calls=%async_computation.3 | async-start | bytes 25890816 | tf_op jit(solution)/shard_map/all_gather | solution.py:114
  17.0 117.5 %copy-start.2 = (bf16[1,6,12,1536]{3,2,1,0:T(8,128)(2,1)S(1)}, bf16[1,6,12,1536]{3,2,1,0:T(8,128)(2,1)}, u32[]{:S(2)}) copy-start(bf16[1,6,12,1536]{3,2,1,0:T(8,128)(2,1)} %param.12) | copy-start | bytes 663556
  140.7 32.0 %all-to-all-start.1 = ((bf16[16,2,4608]{2,1,0:T(2,128)(2,1)}), bf16[16,2,4608]{2,1,0:T(2,128)(2,1)}, u32[]{:S(2)}, u32[]{:S(2)}) async-start(bf16[16,2,4608]{2,1,0:T(2,128)(2,1)} %reshape.147), calls=%async_computation.1 | async-start | bytes 589824 | tf_op jit(solution)/shard_map/all_to_all | solution.py:136
  172.7 40.6 %all-to-all-start = ((bf16[16,2,36864]{2,1,0:T(2,128)(2,1)}), bf16[16,2,36864]{2,1,0:T(2,128)(2,1)S(1)}, u32[]{:S(2)}, u32[]{:S(2)}) async-start(bf16[16,2,36864]{2,1,0:T(2,128)(2,1)} %reshape.145), calls=%async_computation | async-start | bytes 4718592 | tf_op jit(solution)/shard_map/all_to_all | solution.py:134
  252.6 6.7 %copy-start.7 = (f32[1,6,1,1536]{3,0,2,1:T(1,128)S(1)}, f32[1,6,1,1536]{3,0,2,1:T(1,128)}, u32[]{:S(2)}) copy-start(f32[1,6,1,1536]{3,0,2,1:T(1,128)} %get-tuple-element.11) | copy-start | bytes 110596
  252.6 7.4 %copy-start.5 = (f32[1,6,1,1536]{3,0,2,1:T(1,128)S(1)}, f32[1,6,1,1536]{3,0,2,1:T(1,128)}, u32[]{:S(2)}) copy-start(f32[1,6,1,1536]{3,0,2,1:T(1,128)} %get-tuple-element.9) | copy-start | bytes 110596
  252.6 7.3 %copy-start.6 = (f32[1,6,1,1536]{3,0,2,1:T(1,128)S(1)}, f32[1,6,1,1536]{3,0,2,1:T(1,128)}, u32[]{:S(2)}) copy-start(f32[1,6,1,1536]{3,0,2,1:T(1,128)} %get-tuple-element.12) | copy-start | bytes 110596
  254.8 16.7 %all-to-all-start.2 = ((bf16[16,2,12288]{2,1,0:T(2,128)(2,1)}), bf16[16,2,12288]{2,1,0:T(2,128)(2,1)}, u32[]{:S(2)}, u32[]{:S(2)}) async-start(bf16[16,2,12288]{2,1,0:T(2,128)(2,1)} %reshape.149), calls=%async_computation.2 | async-start | bytes 1572864 | tf_op jit(solution)/shard_map/all_to_all | solution.py:151
  260.6 2.0 slice-start
  274.9 4.9 %copy-start.1 = (bf16[1,6,64,1536]{3,2,1,0:T(8,128)(2,1)S(1)}, bf16[1,6,64,1536]{3,2,1,0:T(8,128)(2,1)}, u32[]{:S(2)}) copy-start(bf16[1,6,64,1536]{3,2,1,0:T(8,128)(2,1)} %param.11) | copy-start | bytes 3538948
  275.0 4.9 %copy-start.10 = (f32[1,6,1,1536]{3,1,2,0:T(8,128)S(1)}, f32[1,6,1,1536]{3,1,2,0:T(8,128)}, u32[]{:S(2)}) copy-start(f32[1,6,1,1536]{3,1,2,0:T(8,128)} %copy.74) | copy-start | bytes 110596
  283.2 1.0 copy-start.3
  283.2 1.0 copy-start.11
  283.2 1.0 copy-start.12
  283.3 7.6 %copy-start.8 = (f32[6,64,32]{1,2,0:T(8,128)S(1)}, f32[6,64,32]{1,2,0:T(8,128)}, u32[]{:S(2)}) copy-start(f32[6,64,32]{1,2,0:T(8,128)} %param.20) | copy-start | bytes 147460
  285.1 5.7 %collective-permute-start = (bf16[6,64,32]{1,2,0:T(8,128)(2,1)S(1)}, bf16[6,64,32]{1,2,0:T(8,128)(2,1)S(1)}, u32[]{:S(2)}, u32[]{:S(2)}) collective-permute-start(bf16[6,64,32]{1,2,0:T(8,128)(2,1)S(1)} %dynamic-slice_convert_fusion), channel_id=1, source_target_pairs={{0,64},{64,0},{1,65},{65,1},{2,66},{66,2},{3,67},{67,3},{4,68},{68... | collective-permute-start | bytes 73736 | tf_op jit(solution)/shard_map/ppermute | solution.py:20
Sparse Core Ops, SparseCore 0:
  11.5 96.5 all-gather.3

commit v8 on v7

--- a/solution.py
+++ b/solution.py
@@ -130,22 +130,34 @@
         "prd,de->pre", text_in, full_txt, preferred_element_type=jnp.float32
     ).astype(jnp.bfloat16)
 
-    img_split = qkv_image.reshape(prompts, img_rows, 3, nseq, per_dev * HD)
-    img_heads = lax.all_to_all(img_split, "seq", 3, 1, tiled=True)
-    txt_split = qkv_text.reshape(prompts, txt_rows, 2, nseq, per_dev * HD)
-    txt_heads = lax.all_to_all(txt_split, "seq", 3, 1, tiled=True)
-    all_img = img_heads.shape[1]
-    all_txt = txt_heads.shape[1]
-
+    width = per_dev * HD
+    img_send = jnp.transpose(
+        qkv_image.reshape(prompts, img_rows, 3, nseq, width), (3, 0, 1, 2, 4)
+    ).reshape(nseq, -1)
+    txt_send = jnp.transpose(
+        qkv_text.reshape(prompts, txt_rows, 2, nseq, width), (3, 0, 1, 2, 4)
+    ).reshape(nseq, -1)
+    n_img = img_send.shape[1]
+    received = lax.all_to_all(
+        jnp.concatenate([img_send, txt_send], axis=1), "seq", 0, 0, tiled=True
+    )
+    img_recv = received[:, :n_img].reshape(nseq, prompts, img_rows, 3, width)
+    txt_recv = received[:, n_img:].reshape(nseq, prompts, txt_rows, 2, width)
+
+    def rows_of(part, which):
+        picked = part[:, :, :, which]
+        return jnp.transpose(picked, (1, 0, 2, 3)).reshape(prompts, -1, width)
+
+    all_img = nseq * img_rows
     assert per_dev == 1
     lengths = text_lengths[0]
     mixture = attend(
         lengths,
-        img_heads[:, :, 0, 0],
-        img_heads[:, :, 1, 0],
-        img_heads[:, :, 2, 0],
-        txt_heads[:, :, 0, 0],
-        txt_heads[:, :, 1, 0],
+        rows_of(img_recv, 0),
+        rows_of(img_recv, 1),
+        rows_of(img_recv, 2),
+        rows_of(txt_recv, 0),
+        rows_of(txt_recv, 1),
     )
     head_out = mixture.reshape(prompts, all_img, 1, per_dev * HD)
     token_out = lax.all_to_all(head_out, "seq", 1, 2, tiled=True)

time: 301 us -> 339 us (1.13)
  blocking collectives: 0 us -> 40.6 us
  local copies, waits for them, and re-layouts: 91.7 us -> 124 us
  waiting for transfers between devices: 122 us -> 95 us
  starting transfers between devices: 20 us -> 6.88 us
  other arithmetic: 8.98 us -> 14.2 us
    all_to_all x0 -> x1, blocking collectives: none -> 40.6 us  [local(): lax.all_to_all(jnp.concatenate([img_send, txt_send], axis=1), 'seq', 0, 0...]
    all_to_all x2 -> x0, waiting for transfers between devices: 28.7 us -> none  [the longest x1 28.7 us: local(): img_heads = lax.all_to_all(img_split, 'seq', 3, 1, tiled=True)]
    reshape x4 -> x10, local copies, waits for them, and re-layouts: 11.6 us -> 32.6 us  [the longest x2 13.3 us: local(): qkv_image.reshape(prompts, img_rows, 3, nseq, width)]
    slice x1 -> x4, local copies, waits for them, and re-layouts: 0.95 us -> 14.9 us  [the longest x2 14.7 us: rows_of(): picked = part[:, :, :, which]]
    all_to_all x2 -> x0, starting transfers between devices: 13.1 us -> none  [the longest x1 7.18 us: local(): img_heads = lax.all_to_all(img_split, 'seq', 3, 1, tiled=True)]
    all_to_all x4 -> x1, local copies, waits for them, and re-layouts: 5.83 us -> 0.51 us  [local(): lax.all_to_all(jnp.concatenate([img_send, txt_send], axis=1), 'seq', 0, 0...]
    all_to_all x0 -> x2, other arithmetic: none -> 5.19 us  [local(): lax.all_to_all(jnp.concatenate([img_send, txt_send], axis=1), 'seq', 0, 0...]
    transpose x0 -> x5, local copies, waits for them, and re-layouts: none -> 4.62 us  [rows_of(): return jnp.transpose(picked, (1, 0, 2, 3)).reshape(prompts, -1, width)]
  transfers between devices with their start and end apart: 5 -> 3, of which waited for: 3 -> 3; matrix products, arithmetic and copies ran while one was open for 16% -> 5% of each run, Pallas kernels for 0% -> 0%
where the time goes in v8:
time: 339 us; the launch traced here: 336 us
  local copies, waits for them, and re-layouts  124 us (37%)
  waiting for transfers between devices  95 us (28%)
  blocking collectives  40.6 us (12%)
  Pallas kernels  24.3 us (7%)
  matrix products  15.9 us (5%)
  between operations  15.1 us (4%)
  other arithmetic  14.2 us (4%)
  starting transfers between devices  6.88 us (2%)
    all_gather x1, waiting for transfers between devices, local(): gathered = lax.all_gather(local_all, all_axes, axis=0, tiled=False)  91 us
    unnamed x35, local copies, waits for them, and re-layouts  51 us
    all_to_all x1, blocking collectives, local(): lax.all_to_all(jnp.concatenate([img_send, txt_send], axis=1), 'seq', 0, 0...  40.6 us
    pallas_call x1, Pallas kernels, attend(): pl.pallas_call(attend_kernel, grid=(batch, rows // block), in_specs=[pl.B...  24.3 us
    slice x2, local copies, waits for them, and re-layouts, rows_of(): picked = part[:, :, :, which]  14.7 us
    reshape x2, local copies, waits for them, and re-layouts, local(): qkv_image.reshape(prompts, img_rows, 3, nseq, width)  13.3 us
    dot_general x1, matrix products, local(): jnp.einsum('prd,de->pre', image_in, full_img, preferred_element_type=jnp....  7.69 us
    reshape x1, local copies, waits for them, and re-layouts, local(): img_send = jnp.transpose(qkv_image.reshape(prompts, img_rows, 3, nseq, wi...  7.58 us
  transfers between devices with their start and end apart: 3, of which 3 were waited for; matrix products, arithmetic and copies ran while one was open for 5% of the time, Pallas kernels for 0%

profile of v8, /device:TPU:0, one launch (start us, length us, event | category | flops | bytes accessed | tf_op | source)
XLA Modules:
  0.0 336.3 jit_solution(8232280314843799793)
XLA Ops:
  17.1 91.0 %all-gather.4.cloned.1.call-done = bf16[128,12,6272]{2,1,0:T(8,128)(2,1)} async-done(((bf16[1,12,6272]{2,1,0:T(8,128)(2,1)}), bf16[128,12,6272]{2,1,0:T(8,128)(2,1)}) %all-gather.4.cloned.1.call-update) | async-done | bytes 19267600 | tf_op jit(solution)/shard_map/all_gather | solution.py:114
  108.1 26.4 %reshape.177 = bf16[1536,6272]{1,0:T(8,128)(2,1)} reshape(bf16[128,12,6272]{2,1,0:T(8,128)(2,1)} %all-gather.4.cloned.1.call-done) | data formatting | bytes 38535168
  134.5 4.0 %fusion.13 = bf16[6,12,2048]{2,1,0:T(8,128)(2,1)S(1)} fusion(bf16[1536,6272]{1,0:T(8,128)(2,1)} %reshape.177, bf16[1,6,12,1536]{3,2,1,0:T(8,128)(2,1)S(1)} %copy-done.2, f32[6,1536]{1,0:T(8,128)S(1)} %get-tuple-element.18, f32[6,1536]{1,0:T(8,128)S(1)} %get-tuple-element.19, f32[6,12]{1,0:T(8,128)S(1)} %add_rsqrt_fusion.1, ...), kind=kOutput, calls=%fused_computation.23 | convolution fusion | flops 453795840 | bytes 6881856 | tf_op jit(solution)/shard_map/prd,de->pre/dot_general | solution.py:129
  140.6 7.7 %fusion.2 = bf16[6,64,3072]{2,1,0:T(8,128)(2,1)S(1)} fusion(bf16[1536,6272]{1,0:T(8,128)(2,1)} %reshape.177, bf16[1,6,64,1536]{3,2,1,0:T(8,128)(2,1)S(1)} %copy-done, f32[6,1536]{1,0:T(8,128)} %get-tuple-element.23, f32[6,1536]{1,0:T(8,128)} %get-tuple-element.22, f32[6,64]{1,0:T(8,128)S(1)} %add_rsqrt_fusion.2, f32[6,64]{1,0:T(8,128)S(1)} %broadcast_multiply_fusion.2), kind=kOutput, calls=%fused_computation.5 | convolution fusion | flops 3628597248 | bytes 13077504 | tf_op jit(solution)/shard_map/prd,de->pre/dot_general | solution.py:126
  148.3 4.8 %reshape.149 = bf16[6,64,3,16,64]{4,3,2,1,0:T(8,128)(2,1)} reshape(bf16[6,64,3072]{2,1,0:T(8,128)(2,1)S(1)} %fusion.2) | data formatting | bytes 4718592 | tf_op jit(solution)/shard_map/reshape | solution.py:135
  153.1 8.6 %copy.116 = bf16[6,64,3,16,64]{4,2,1,0,3:T(4,128)(2,1)} copy(bf16[6,64,3,16,64]{4,3,2,1,0:T(8,128)(2,1)} %reshape.149) | data formatting | bytes 4718592 | tf_op jit(solution)/shard_map/reshape | solution.py:135
  161.7 7.6 %reshape.150 = bf16[16,73728]{1,0:T(8,128)(2,1)} reshape(bf16[16,6,64,3,64]{4,3,2,1,0:T(4,128)(2,1)} %bitcast.132) | data formatting | bytes 4718592 | tf_op jit(solution)/shard_map/reshape | solution.py:136
  171.6 3.3 reduce.4
  174.9 3.6 %reshape.183 = bf16[16,2,41472]{2,1,0:T(2,128)(2,1)S(1)} reshape(bf16[16,82944]{1,0:T(8,128)(2,1)} %reduce.4) | data formatting | bytes 5308416
  178.5 40.6 %all_to_all.27 = bf16[16,2,41472]{2,1,0:T(2,128)(2,1)} all-to-all(bf16[16,2,41472]{2,1,0:T(2,128)(2,1)S(1)} %reshape.183), channel_id=1, replica_groups=mesh['guid'=2,'xlo'=2,'core'=2,'seq'=16] {'seq'}, dimensions={0} | all-to-all | bytes 5308416 | tf_op jit(solution)/shard_map/all_to_all | solution.py:141
  219.2 10.8 %reshape.184 = bf16[16,1,82944]{2,1,0:T(2,128)(2,1)} reshape(bf16[16,2,41472]{2,1,0:T(2,128)(2,1)} %all_to_all.27) | data formatting | bytes 5308416
  229.9 3.4 copy.117
  233.5 7.4 %reshape.153 = bf16[16,6,64,3,64]{4,3,2,1,0:T(4,128)(2,1)} reshape(bf16[16,73728]{1,0:T(8,128)(2,1)S(1)} %slice.82) | data formatting | bytes 4718592 | tf_op jit(solution)/shard_map/reshape | solution.py:144
  240.9 13.9 %fusion.42 = (bf16[16,6,64,1,64]{4,3,2,1,0:T(2,128)(2,1)S(1)}, bf16[16,6,64,1,64]{4,3,2,1,0:T(2,128)(2,1)S(1)}, bf16[16,6,64,1,64]{4,3,2,1,0:T(2,128)(2,1)S(1)}) fusion(bf16[16,6,64,3,64]{4,3,2,1,0:T(4,128)(2,1)} %reshape.153), kind=kLoop, calls=%fused_computation.75 | loop fusion | bytes 4718592 | tf_op jit(solution)/shard_map/slice | solution.py:148
  262.4 24.3 %shard_map.122 = bf16[6,1024,64]{2,1,0:T(8,128)(2,1)} custom-call(s32[6]{0:T(128)} %bitcast.146, bf16[6,1024,64]{2,1,0:T(8,128)(2,1)} %bitcast.140, bf16[6,1024,64]{2,1,0:T(8,128)(2,1)} %bitcast.141, bf16[6,1024,64]{2,1,0:T(8,128)(2,1)} %bitcast.142, bf16[6,192,64]{2,1,0:T(8,128)(2,1)} %reshape.158.kt_ref, bf16[6,192,64]{2,1,0:T(8,128)(2,1)} %reshape.159.vt_ref), custom_call_target="tpu_custom_call" | custom-call | flops 1912602624 | bytes 3440640 | tf_op jit(solution)/shard_map/pallas_call | solution.py:62
  286.7 2.5 copy.123
  291.4 4.5 %all-to-all-start.1 = ((bf16[16,2,12288]{2,1,0:T(2,128)(2,1)}), bf16[16,2,12288]{2,1,0:T(2,128)(2,1)}, u32[]{:S(2)}, u32[]{:S(2)}) async-start(bf16[16,2,12288]{2,1,0:T(2,128)(2,1)} %reshape.185), calls=%async_computation.1 | async-start | bytes 1572864 | tf_op jit(solution)/shard_map/all_to_all | solution.py:163
  299.2 5.5 %reshape.161 = bf16[128,9,1536]{2,1,0:T(8,128)(2,1)} reshape(bf16[1536,1152]{1,0:T(8,128)(2,1)S(1)} %slice-done) | data formatting | bytes 7077888 | tf_op jit(solution)/shard_map/reshape | solution.py:118
  304.6 2.4 slice_reduce_fusion
  309.5 3.5 %reshape.186 = bf16[1024,1,6,64]{3,2,1,0:T(8,128)(2,1)S(1)} reshape(bf16[16,2,12288]{2,1,0:T(2,128)(2,1)} %all-to-all-done.1) | data formatting | bytes 1572864
  315.1 2.7 dot_general.16
  317.8 3.4 fusion.46
  323.1 2.3 collective-permute-start
  326.2 2.6 collective-permute-done
  (77 shorter events, 34.6 us)
Async XLA Ops:
  7.2 8.0 %copy-start = (bf16[1,6,64,1536]{3,2,1,0:T(8,128)(2,1)S(1)}, bf16[1,6,64,1536]{3,2,1,0:T(8,128)(2,1)}, u32[]{:S(2)}) copy-start(bf16[1,6,64,1536]{3,2,1,0:T(8,128)(2,1)} %param.11) | copy-start | bytes 3538948
  7.2 8.5 %copy-start.10 = (f32[1,6,2,1536]{3,2,1,0:T(2,128)S(1)}, f32[1,6,2,1536]{3,2,1,0:T(2,128)}, u32[]{:S(2)}) copy-start(f32[1,6,2,1536]{3,2,1,0:T(2,128)} %param.14) | copy-start | bytes 221188
  7.2 8.6 %copy-start.5 = (f32[1,6,5,1536]{3,0,2,1:T(1,128)S(1)}, f32[1,6,5,1536]{3,0,2,1:T(1,128)}, u32[]{:S(2)}) copy-start(f32[1,6,5,1536]{3,0,2,1:T(1,128)} %param.13) | copy-start | bytes 552964
  7.2 100.9 %all-gather.4.cloned.1.call-start = ((), (), s32[]{:S(2)}) async-start(), calls=%async_computation.2 | async-start | bytes 25890816 | tf_op jit(solution)/shard_map/all_gather | solution.py:114
  17.1 117.4 %copy-start.2 = (bf16[1,6,12,1536]{3,2,1,0:T(8,128)(2,1)S(1)}, bf16[1,6,12,1536]{3,2,1,0:T(8,128)(2,1)}, u32[]{:S(2)}) copy-start(bf16[1,6,12,1536]{3,2,1,0:T(8,128)(2,1)} %param.12) | copy-start | bytes 663556
  161.7 7.6 %copy-start.3 = (bf16[16,9216]{1,0:T(8,128)(2,1)S(1)}, bf16[16,9216]{1,0:T(8,128)(2,1)}, u32[]{:S(2)}) copy-start(bf16[16,9216]{1,0:T(8,128)(2,1)} %reshape.152) | copy-start | bytes 884740
  289.2 6.7 %copy-start.8 = (f32[1,6,1,1536]{3,0,2,1:T(1,128)S(1)}, f32[1,6,1,1536]{3,0,2,1:T(1,128)}, u32[]{:S(2)}) copy-start(f32[1,6,1,1536]{3,0,2,1:T(1,128)} %get-tuple-element.11) | copy-start | bytes 110596
  289.2 7.3 %copy-start.6 = (f32[1,6,1,1536]{3,0,2,1:T(1,128)S(1)}, f32[1,6,1,1536]{3,0,2,1:T(1,128)}, u32[]{:S(2)}) copy-start(f32[1,6,1,1536]{3,0,2,1:T(1,128)} %get-tuple-element.9) | copy-start | bytes 110596
  289.2 7.3 %copy-start.7 = (f32[1,6,1,1536]{3,0,2,1:T(1,128)S(1)}, f32[1,6,1,1536]{3,0,2,1:T(1,128)}, u32[]{:S(2)}) copy-start(f32[1,6,1,1536]{3,0,2,1:T(1,128)} %get-tuple-element.12) | copy-start | bytes 110596
  291.4 18.1 %all-to-all-start.1 = ((bf16[16,2,12288]{2,1,0:T(2,128)(2,1)}), bf16[16,2,12288]{2,1,0:T(2,128)(2,1)}, u32[]{:S(2)}, u32[]{:S(2)}) async-start(bf16[16,2,12288]{2,1,0:T(2,128)(2,1)} %reshape.185), calls=%async_computation.1 | async-start | bytes 1572864 | tf_op jit(solution)/shard_map/all_to_all | solution.py:163
  297.2 2.0 slice-start
  312.9 4.9 %copy-start.1 = (bf16[1,6,64,1536]{3,2,1,0:T(8,128)(2,1)S(1)}, bf16[1,6,64,1536]{3,2,1,0:T(8,128)(2,1)}, u32[]{:S(2)}) copy-start(bf16[1,6,64,1536]{3,2,1,0:T(8,128)(2,1)} %param.11) | copy-start | bytes 3538948
  312.9 4.9 %copy-start.11 = (f32[1,6,1,1536]{3,1,2,0:T(8,128)S(1)}, f32[1,6,1,1536]{3,1,2,0:T(8,128)}, u32[]{:S(2)}) copy-start(f32[1,6,1,1536]{3,1,2,0:T(8,128)} %copy.122) | copy-start | bytes 110596
  321.2 1.0 copy-start.4
  321.2 1.0 copy-start.12
  321.2 1.0 copy-start.13
  321.2 7.6 %copy-start.9 = (f32[6,64,32]{1,2,0:T(8,128)S(1)}, f32[6,64,32]{1,2,0:T(8,128)}, u32[]{:S(2)}) copy-start(f32[6,64,32]{1,2,0:T(8,128)} %param.20) | copy-start | bytes 147460
  323.1 5.7 %collective-permute-start = (bf16[6,64,32]{1,2,0:T(8,128)(2,1)S(1)}, bf16[6,64,32]{1,2,0:T(8,128)(2,1)S(1)}, u32[]{:S(2)}, u32[]{:S(2)}) collective-permute-start(bf16[6,64,32]{1,2,0:T(8,128)(2,1)S(1)} %dynamic-slice_convert_fusion), channel_id=1, source_target_pairs={{0,64},{64,0},{1,65},{65,1},{2,66},{66,2},{3,67},{67,3},{4,68},{68... | collective-permute-start | bytes 73736 | tf_op jit(solution)/shard_map/ppermute | solution.py:20
Sparse Core Ops, SparseCore 0:
  11.5 96.5 all-gather.3

commit v9 on v7

--- a/solution.py
+++ b/solution.py
@@ -78,7 +78,7 @@
     )(lengths, q, k_img, v_img, k_txt, v_txt)
 
 
-def local(
+def block(
     img_hidden,
     txt_hidden,
     img_mod,
@@ -135,7 +135,6 @@
     txt_split = qkv_text.reshape(prompts, txt_rows, 2, nseq, per_dev * HD)
     txt_heads = lax.all_to_all(txt_split, "seq", 3, 1, tiled=True)
     all_img = img_heads.shape[1]
-    all_txt = txt_heads.shape[1]
 
     assert per_dev == 1
     lengths = text_lengths[0]
@@ -199,7 +198,7 @@
         P(),
     )
     return jax.shard_map(
-        local,
+        block,
         mesh=fine,
         in_specs=placed,
         out_specs=(P(req, "seq", "guid"), P(req, "seq", "guid")),

time: 301 us -> 301 us (level)
  no operation moved by 1% of the time
where the time goes in v9:
time: 301 us; the launch traced here: 298 us
  waiting for transfers between devices  122 us (41%)
  local copies, waits for them, and re-layouts  91.7 us (30%)
  Pallas kernels  24.3 us (8%)
  starting transfers between devices  20 us (7%)
  matrix products  15.9 us (5%)
  between operations  15.1 us (5%)
  other arithmetic  8.98 us (3%)
    all_gather x1, waiting for transfers between devices, block(): gathered = lax.all_gather(local_all, all_axes, axis=0, tiled=False)  91 us
    unnamed x36, local copies, waits for them, and re-layouts  50.4 us
    all_to_all x1, waiting for transfers between devices, block(): img_heads = lax.all_to_all(img_split, 'seq', 3, 1, tiled=True)  28.7 us
    pallas_call x1, Pallas kernels, attend(): pl.pallas_call(attend_kernel, grid=(batch, rows // block), in_specs=[pl.B...  24.3 us
    reshape x2, local copies, waits for them, and re-layouts, block(): img_split = qkv_image.reshape(prompts, img_rows, 3, nseq, per_dev * HD)  10.5 us
    dot_general x1, matrix products, block(): jnp.einsum('prd,de->pre', image_in, full_img, preferred_element_type=jnp....  7.7 us
    all_to_all x1, starting transfers between devices, block(): img_heads = lax.all_to_all(img_split, 'seq', 3, 1, tiled=True)  7.18 us
  transfers between devices with their start and end apart: 5, of which 3 were waited for; matrix products, arithmetic and copies ran while one was open for 16% of the time, Pallas kernels for 0%

profile of v9, /device:TPU:0, one launch (start us, length us, event | category | flops | bytes accessed | tf_op | source)
XLA Modules:
  0.0 298.4 jit_solution(14510468621192711525)
XLA Ops:
  17.0 91.0 %all-gather.4.cloned.1.call-done = bf16[128,12,6272]{2,1,0:T(8,128)(2,1)} async-done(((bf16[1,12,6272]{2,1,0:T(8,128)(2,1)}), bf16[128,12,6272]{2,1,0:T(8,128)(2,1)}) %all-gather.4.cloned.1.call-update) | async-done | bytes 19267600 | tf_op jit(solution)/shard_map/all_gather | solution.py:114
  108.1 26.5 %reshape.139 = bf16[1536,6272]{1,0:T(8,128)(2,1)} reshape(bf16[128,12,6272]{2,1,0:T(8,128)(2,1)} %all-gather.4.cloned.1.call-done) | data formatting | bytes 38535168
  134.5 4.0 %fusion.13 = bf16[6,12,2048]{2,1,0:T(8,128)(2,1)S(1)} fusion(bf16[1536,6272]{1,0:T(8,128)(2,1)} %reshape.139, bf16[1,6,12,1536]{3,2,1,0:T(8,128)(2,1)S(1)} %copy-done.2, f32[6,1536]{1,0:T(8,128)S(1)} %get-tuple-element.22, f32[6,1536]{1,0:T(8,128)S(1)} %get-tuple-element.23, f32[6,12]{1,0:T(8,128)S(1)} %add_rsqrt_fusion.1, ...), kind=kOutput, calls=%fused_computation.20 | convolution fusion | flops 453795840 | bytes 6881856 | tf_op jit(solution)/shard_map/prd,de->pre/dot_general | solution.py:129
  140.7 5.9 %all-to-all-start.1 = ((bf16[16,2,4608]{2,1,0:T(2,128)(2,1)}), bf16[16,2,4608]{2,1,0:T(2,128)(2,1)}, u32[]{:S(2)}, u32[]{:S(2)}) async-start(bf16[16,2,4608]{2,1,0:T(2,128)(2,1)} %reshape.147), calls=%async_computation.1 | async-start | bytes 589824 | tf_op jit(solution)/shard_map/all_to_all | solution.py:136
  146.6 7.7 %fusion.2 = bf16[6,64,3072]{2,1,0:T(8,128)(2,1)S(1)} fusion(bf16[1536,6272]{1,0:T(8,128)(2,1)} %reshape.139, bf16[1,6,64,1536]{3,2,1,0:T(8,128)(2,1)S(1)} %copy-done, f32[6,1536]{1,0:T(8,128)} %get-tuple-element.21, f32[6,1536]{1,0:T(8,128)} %get-tuple-element.20, f32[6,64]{1,0:T(8,128)S(1)} %add_rsqrt_fusion.2, f32[6,64]{1,0:T(8,128)S(1)} %broadcast_multiply_fusion.2), kind=kOutput, calls=%fused_computation.4 | convolution fusion | flops 3628597248 | bytes 13077504 | tf_op jit(solution)/shard_map/prd,de->pre/dot_general | solution.py:126
  154.3 4.8 %reshape.120 = bf16[6,64,3,16,64]{4,3,2,1,0:T(8,128)(2,1)} reshape(bf16[6,64,3072]{2,1,0:T(8,128)(2,1)S(1)} %fusion.2) | data formatting | bytes 4718592 | tf_op jit(solution)/shard_map/reshape | solution.py:133
  159.1 5.7 %copy.75 = bf16[6,64,3,16,64]{4,1,0,2,3:T(8,128)(2,1)} copy(bf16[6,64,3,16,64]{4,3,2,1,0:T(8,128)(2,1)} %reshape.120) | data formatting | bytes 4718592 | tf_op jit(solution)/shard_map/reshape | solution.py:133
  164.8 7.9 %reshape.145 = bf16[16,2,36864]{2,1,0:T(2,128)(2,1)} reshape(bf16[16,3,6,64,64]{4,3,2,1,0:T(8,128)(2,1)} %bitcast.126) | data formatting | bytes 4718592
  172.7 7.2 %all-to-all-start = ((bf16[16,2,36864]{2,1,0:T(2,128)(2,1)}), bf16[16,2,36864]{2,1,0:T(2,128)(2,1)S(1)}, u32[]{:S(2)}, u32[]{:S(2)}) async-start(bf16[16,2,36864]{2,1,0:T(2,128)(2,1)} %reshape.145), calls=%async_computation | async-start | bytes 4718592 | tf_op jit(solution)/shard_map/all_to_all | solution.py:134
  184.5 28.7 %all-to-all-done = bf16[16,2,36864]{2,1,0:T(2,128)(2,1)S(1)} async-done(((bf16[16,2,36864]{2,1,0:T(2,128)(2,1)}), bf16[16,2,36864]{2,1,0:T(2,128)(2,1)S(1)}, u32[]{:S(2)}, u32[]{:S(2)}) %all-to-all-start) | async-done | bytes 2359328 | tf_op jit(solution)/shard_map/all_to_all | solution.py:134
  213.3 5.2 %reshape.146 = bf16[16,3,6,64,64]{4,3,2,1,0:T(8,128)(2,1)} reshape(bf16[16,2,36864]{2,1,0:T(2,128)(2,1)S(1)} %all-to-all-done) | data formatting | bytes 4718592
  218.5 3.4 %bitcast_bitcast_fusion = bf16[6,16,64,3,1,64]{5,2,0,3,1,4:T(8,128)(2,1)S(1)} fusion(bf16[16,3,6,64,64]{4,3,2,1,0:T(8,128)(2,1)} %reshape.146), kind=kLoop, calls=%fused_computation.78 | loop fusion | bytes 4718592 | tf_op jit(solution)/shard_map/all_to_all | solution.py:134
  223.5 2.2 slice_bitcast_fusion.14
  225.8 24.3 %shard_map.122 = bf16[6,1024,64]{2,1,0:T(8,128)(2,1)} custom-call(s32[6]{0:T(128)} %bitcast.136, bf16[6,1024,64]{2,1,0:T(8,128)(2,1)} %get-tuple-element.6.q_ref, bf16[6,1024,64]{2,1,0:T(8,128)(2,1)} %get-tuple-element.5.ki_ref, bf16[6,1024,64]{2,1,0:T(8,128)(2,1)} %get-tuple-element.4.vi_ref, bf16[6,192,64]{2,1,0:T(8,128)(2,1)} %bitcast.133, ...), custom_call_target="tpu_custom_call" | custom-call | flops 1912602624 | bytes 3440640 | tf_op jit(solution)/shard_map/pallas_call | solution.py:62
  250.1 2.5 copy.76
  252.6 2.2 reshape.149
  254.8 4.5 %all-to-all-start.2 = ((bf16[16,2,12288]{2,1,0:T(2,128)(2,1)}), bf16[16,2,12288]{2,1,0:T(2,128)(2,1)}, u32[]{:S(2)}, u32[]{:S(2)}) async-start(bf16[16,2,12288]{2,1,0:T(2,128)(2,1)} %reshape.149), calls=%async_computation.2 | async-start | bytes 1572864 | tf_op jit(solution)/shard_map/all_to_all | solution.py:150
  262.6 5.5 %reshape.123 = bf16[128,9,1536]{2,1,0:T(8,128)(2,1)} reshape(bf16[1536,1152]{1,0:T(8,128)(2,1)S(1)} %slice-done) | data formatting | bytes 7077888 | tf_op jit(solution)/shard_map/reshape | solution.py:118
  268.0 2.4 slice_reduce_fusion
  271.5 3.5 %reshape.150 = bf16[1024,1,6,64]{3,2,1,0:T(8,128)(2,1)S(1)} reshape(bf16[16,2,12288]{2,1,0:T(2,128)(2,1)} %all-to-all-done.2) | data formatting | bytes 1572864
  277.1 2.7 dot_general.16
  279.9 3.4 %fusion.45 = (f32[6,64]{1,0:T(8,128)S(1)}, f32[6,64,1536]{2,1,0:T(8,128)S(1)}) fusion(bf16[6,64,1024]{2,1,0:T(8,128)(2,1)S(1)} %dot_general.16, bf16[128,9,1536]{2,1,0:T(8,128)(2,1)} %reshape.123, f32[6,1536]{1,0:T(8,128)S(1)} %bitcast.135, bf16[1,6,64,1536]{3,2,1,0:T(8,128)(2,1)S(1)} %copy-done.1), kind=kOutput, calls=%fused_computation.77 | convolution fusion | flops 1210318464 | bytes 7509504 | tf_op jit(solution)/shard_map/dot_general | solution.py:153
  285.1 2.3 collective-permute-start
  288.2 2.6 collective-permute-done
  (69 shorter events, 27.2 us)
Async XLA Ops:
  7.2 8.0 %copy-start = (bf16[1,6,64,1536]{3,2,1,0:T(8,128)(2,1)S(1)}, bf16[1,6,64,1536]{3,2,1,0:T(8,128)(2,1)}, u32[]{:S(2)}) copy-start(bf16[1,6,64,1536]{3,2,1,0:T(8,128)(2,1)} %param.11) | copy-start | bytes 3538948
  7.2 8.5 %copy-start.9 = (f32[1,6,2,1536]{3,2,1,0:T(2,128)S(1)}, f32[1,6,2,1536]{3,2,1,0:T(2,128)}, u32[]{:S(2)}) copy-start(f32[1,6,2,1536]{3,2,1,0:T(2,128)} %param.14) | copy-start | bytes 221188
  7.2 8.5 %copy-start.4 = (f32[1,6,5,1536]{3,0,2,1:T(1,128)S(1)}, f32[1,6,5,1536]{3,0,2,1:T(1,128)}, u32[]{:S(2)}) copy-start(f32[1,6,5,1536]{3,0,2,1:T(1,128)} %param.13) | copy-start | bytes 552964
  7.2 100.9 %all-gather.4.cloned.1.call-start = ((), (), s32[]{:S(2)}) async-start(), calls=%async_computation.3 | async-start | bytes 25890816 | tf_op jit(solution)/shard_map/all_gather | solution.py:114
  17.0 117.5 %copy-start.2 = (bf16[1,6,12,1536]{3,2,1,0:T(8,128)(2,1)S(1)}, bf16[1,6,12,1536]{3,2,1,0:T(8,128)(2,1)}, u32[]{:S(2)}) copy-start(bf16[1,6,12,1536]{3,2,1,0:T(8,128)(2,1)} %param.12) | copy-start | bytes 663556
  140.7 32.0 %all-to-all-start.1 = ((bf16[16,2,4608]{2,1,0:T(2,128)(2,1)}), bf16[16,2,4608]{2,1,0:T(2,128)(2,1)}, u32[]{:S(2)}, u32[]{:S(2)}) async-start(bf16[16,2,4608]{2,1,0:T(2,128)(2,1)} %reshape.147), calls=%async_computation.1 | async-start | bytes 589824 | tf_op jit(solution)/shard_map/all_to_all | solution.py:136
  172.7 40.6 %all-to-all-start = ((bf16[16,2,36864]{2,1,0:T(2,128)(2,1)}), bf16[16,2,36864]{2,1,0:T(2,128)(2,1)S(1)}, u32[]{:S(2)}, u32[]{:S(2)}) async-start(bf16[16,2,36864]{2,1,0:T(2,128)(2,1)} %reshape.145), calls=%async_computation | async-start | bytes 4718592 | tf_op jit(solution)/shard_map/all_to_all | solution.py:134
  252.6 6.7 %copy-start.7 = (f32[1,6,1,1536]{3,0,2,1:T(1,128)S(1)}, f32[1,6,1,1536]{3,0,2,1:T(1,128)}, u32[]{:S(2)}) copy-start(f32[1,6,1,1536]{3,0,2,1:T(1,128)} %get-tuple-element.11) | copy-start | bytes 110596
  252.6 7.4 %copy-start.5 = (f32[1,6,1,1536]{3,0,2,1:T(1,128)S(1)}, f32[1,6,1,1536]{3,0,2,1:T(1,128)}, u32[]{:S(2)}) copy-start(f32[1,6,1,1536]{3,0,2,1:T(1,128)} %get-tuple-element.9) | copy-start | bytes 110596
  252.6 7.3 %copy-start.6 = (f32[1,6,1,1536]{3,0,2,1:T(1,128)S(1)}, f32[1,6,1,1536]{3,0,2,1:T(1,128)}, u32[]{:S(2)}) copy-start(f32[1,6,1,1536]{3,0,2,1:T(1,128)} %get-tuple-element.12) | copy-start | bytes 110596
  254.8 16.7 %all-to-all-start.2 = ((bf16[16,2,12288]{2,1,0:T(2,128)(2,1)}), bf16[16,2,12288]{2,1,0:T(2,128)(2,1)}, u32[]{:S(2)}, u32[]{:S(2)}) async-start(bf16[16,2,12288]{2,1,0:T(2,128)(2,1)} %reshape.149), calls=%async_computation.2 | async-start | bytes 1572864 | tf_op jit(solution)/shard_map/all_to_all | solution.py:150
  260.6 2.0 slice-start
  274.9 4.9 %copy-start.1 = (bf16[1,6,64,1536]{3,2,1,0:T(8,128)(2,1)S(1)}, bf16[1,6,64,1536]{3,2,1,0:T(8,128)(2,1)}, u32[]{:S(2)}) copy-start(bf16[1,6,64,1536]{3,2,1,0:T(8,128)(2,1)} %param.11) | copy-start | bytes 3538948
  275.0 4.9 %copy-start.10 = (f32[1,6,1,1536]{3,1,2,0:T(8,128)S(1)}, f32[1,6,1,1536]{3,1,2,0:T(8,128)}, u32[]{:S(2)}) copy-start(f32[1,6,1,1536]{3,1,2,0:T(8,128)} %copy.74) | copy-start | bytes 110596
  283.2 1.0 copy-start.3
  283.2 1.0 copy-start.11
  283.2 1.0 copy-start.12
  283.3 7.6 %copy-start.8 = (f32[6,64,32]{1,2,0:T(8,128)S(1)}, f32[6,64,32]{1,2,0:T(8,128)}, u32[]{:S(2)}) copy-start(f32[6,64,32]{1,2,0:T(8,128)} %param.20) | copy-start | bytes 147460
  285.1 5.7 %collective-permute-start = (bf16[6,64,32]{1,2,0:T(8,128)(2,1)S(1)}, bf16[6,64,32]{1,2,0:T(8,128)(2,1)S(1)}, u32[]{:S(2)}, u32[]{:S(2)}) collective-permute-start(bf16[6,64,32]{1,2,0:T(8,128)(2,1)S(1)} %dynamic-slice_convert_fusion), channel_id=1, source_target_pairs={{0,64},{64,0},{1,65},{65,1},{2,66},{66,2},{3,67},{67,3},{4,68},{68... | collective-permute-start | bytes 73736 | tf_op jit(solution)/shard_map/ppermute | solution.py:20
Sparse Core Ops, SparseCore 0:
  11.5 96.5 all-gather.3

commit v10 on v9

--- a/solution.py
+++ b/solution.py
@@ -35,9 +35,12 @@
 
 def attend_kernel(len_ref, q_ref, ki_ref, vi_ref, kt_ref, vt_ref, o_ref):
     length = len_ref[pl.program_id(0)]
-    q = q_ref[0]
+    width = q_ref.shape[-1]
+    q = q_ref[...].reshape(-1, width)
+    k_img = ki_ref[...].reshape(-1, width)
+    v_img = vi_ref[...].reshape(-1, width)
     dims = (((1,), (1,)), ((), ()))
-    s_img = lax.dot_general(q, ki_ref[0], dims, preferred_element_type=jnp.float32) * 0.125
+    s_img = lax.dot_general(q, k_img, dims, preferred_element_type=jnp.float32) * 0.125
     s_txt = lax.dot_general(q, kt_ref[0], dims, preferred_element_type=jnp.float32) * 0.125
     col = lax.broadcasted_iota(jnp.int32, s_txt.shape, 1)
     s_txt = jnp.where(col < length, s_txt, -1e30)
@@ -48,34 +51,36 @@
     e_txt = jnp.exp(s_txt - highest)
     totals = jnp.sum(e_img, axis=1, keepdims=True) + jnp.sum(e_txt, axis=1, keepdims=True)
     acc = jnp.dot(
-        e_img.astype(jnp.bfloat16), vi_ref[0], preferred_element_type=jnp.float32
+        e_img.astype(jnp.bfloat16), v_img, preferred_element_type=jnp.float32
     ) + jnp.dot(e_txt.astype(jnp.bfloat16), vt_ref[0], preferred_element_type=jnp.float32)
     o_ref[0] = (acc / totals).astype(o_ref.dtype)
 
 
-def attend(lengths, q, k_img, v_img, k_txt, v_txt, block=256):
-    batch, rows, width = q.shape
-    n_img = k_img.shape[1]
+def attend(lengths, img_parts, k_txt, v_txt, block=256):
+    sources, batch, _, src_rows, width = img_parts.shape
+    rows = sources * src_rows
     n_txt = k_txt.shape[1]
-    flops = 4 * batch * rows * (n_img + n_txt) * width
-    moved = 2 * (q.size * 2 + k_img.size * 2 + k_txt.size * 2)
+    per_block = block // src_rows
+    flops = 4 * batch * rows * (rows + n_txt) * width
+    moved = 2 * (img_parts.size + k_txt.size * 2 + batch * rows * width)
+    whole = (sources, 1, 1, src_rows, width)
     return pl.pallas_call(
         attend_kernel,
         grid=(batch, rows // block),
         in_specs=[
             pl.BlockSpec(memory_space=pltpu.SMEM),
-            pl.BlockSpec((1, block, width), lambda b, i: (b, i, 0)),
-            pl.BlockSpec((1, n_img, width), lambda b, i: (b, 0, 0)),
-            pl.BlockSpec((1, n_img, width), lambda b, i: (b, 0, 0)),
+            pl.BlockSpec((per_block, 1, 1, src_rows, width), lambda b, i: (i, b, 0, 0, 0)),
+            pl.BlockSpec(whole, lambda b, i: (0, b, 1, 0, 0)),
+            pl.BlockSpec(whole, lambda b, i: (0, b, 2, 0, 0)),
             pl.BlockSpec((1, n_txt, width), lambda b, i: (b, 0, 0)),
             pl.BlockSpec((1, n_txt, width), lambda b, i: (b, 0, 0)),
         ],
         out_specs=pl.BlockSpec((1, block, width), lambda b, i: (b, i, 0)),
-        out_shape=jax.ShapeDtypeStruct(q.shape, jnp.bfloat16),
+        out_shape=jax.ShapeDtypeStruct((batch, rows, width), jnp.bfloat16),
         cost_estimate=pl.CostEstimate(
-            flops=flops, transcendentals=batch * rows * (n_img + n_txt), bytes_accessed=moved
+            flops=flops, transcendentals=batch * rows * (rows + n_txt), bytes_accessed=moved
         ),
-    )(lengths, q, k_img, v_img, k_txt, v_txt)
+    )(lengths, img_parts, img_parts, img_parts, k_txt, v_txt)
 
 
 def block(
@@ -138,14 +143,10 @@
 
     assert per_dev == 1
     lengths = text_lengths[0]
-    mixture = attend(
-        lengths,
-        img_heads[:, :, 0, 0],
-        img_heads[:, :, 1, 0],
-        img_heads[:, :, 2, 0],
-        txt_heads[:, :, 0, 0],
-        txt_heads[:, :, 1, 0],
-    )
+    img_parts = jnp.transpose(
+        img_heads.reshape(prompts, nseq, img_rows, 3, HD), (1, 0, 3, 2, 4)
+    )
+    mixture = attend(lengths, img_parts, txt_heads[:, :, 0, 0], txt_heads[:, :, 1, 0])
     head_out = mixture.reshape(prompts, all_img, 1, per_dev * HD)
     token_out = lax.all_to_all(head_out, "seq", 1, 2, tiled=True)
     attended = token_out.reshape(prompts * img_rows, attn_width)

time: 301 us -> 299 us (level)
    transpose x0 -> x1, local copies, waits for them, and re-layouts: none -> 6.04 us  [block(): jnp.transpose(img_heads.reshape(prompts, nseq, img_rows, 3, HD), (1, 0, 3...]
    all_to_all x2 -> x0, local copies, waits for them, and re-layouts: 5.02 us -> none  [block(): img_heads = lax.all_to_all(img_split, 'seq', 3, 1, tiled=True)]
where the time goes in v10:
time: 299 us; the launch traced here: 297 us
  waiting for transfers between devices  122 us (41%)
  local copies, waits for them, and re-layouts  90.5 us (30%)
  Pallas kernels  24.3 us (8%)
  starting transfers between devices  19.9 us (7%)
  matrix products  15.9 us (5%)
  between operations  15.1 us (5%)
  other arithmetic  8.98 us (3%)
    all_gather x1, waiting for transfers between devices, block(): gathered = lax.all_gather(local_all, all_axes, axis=0, tiled=False)  91 us
    unnamed x36, local copies, waits for them, and re-layouts  50.4 us
    all_to_all x1, waiting for transfers between devices, block(): img_heads = lax.all_to_all(img_split, 'seq', 3, 1, tiled=True)  28.8 us
    pallas_call x1, Pallas kernels, attend(): pl.pallas_call(attend_kernel, grid=(batch, rows // block), in_specs=[pl.B...  24.3 us
    reshape x2, local copies, waits for them, and re-layouts, block(): img_split = qkv_image.reshape(prompts, img_rows, 3, nseq, per_dev * HD)  10.5 us
    dot_general x1, matrix products, block(): jnp.einsum('prd,de->pre', image_in, full_img, preferred_element_type=jnp....  7.7 us
    all_to_all x1, starting transfers between devices, block(): img_heads = lax.all_to_all(img_split, 'seq', 3, 1, tiled=True)  7.18 us
    transpose x1, local copies, waits for them, and re-layouts, block(): jnp.transpose(img_heads.reshape(prompts, nseq, img_rows, 3, HD), (1, 0, 3...  6.04 us
  transfers between devices with their start and end apart: 5, of which 3 were waited for; matrix products, arithmetic and copies ran while one was open for 16% of the time, Pallas kernels for 0%

profile of v10, /device:TPU:0, one launch (start us, length us, event | category | flops | bytes accessed | tf_op | source)
XLA Modules:
  0.0 297.2 jit_solution(7663063820553035191)
XLA Ops:
  17.0 91.0 %all-gather.4.cloned.1.call-done = bf16[128,12,6272]{2,1,0:T(8,128)(2,1)} async-done(((bf16[1,12,6272]{2,1,0:T(8,128)(2,1)}), bf16[128,12,6272]{2,1,0:T(8,128)(2,1)}) %all-gather.4.cloned.1.call-update) | async-done | bytes 19267600 | tf_op jit(solution)/shard_map/all_gather | solution.py:119
  108.1 26.4 %reshape.144 = bf16[1536,6272]{1,0:T(8,128)(2,1)} reshape(bf16[128,12,6272]{2,1,0:T(8,128)(2,1)} %all-gather.4.cloned.1.call-done) | data formatting | bytes 38535168
  134.5 4.0 %fusion.13 = bf16[6,12,2048]{2,1,0:T(8,128)(2,1)S(1)} fusion(bf16[1536,6272]{1,0:T(8,128)(2,1)} %reshape.144, bf16[1,6,12,1536]{3,2,1,0:T(8,128)(2,1)S(1)} %copy-done.2, f32[6,1536]{1,0:T(8,128)S(1)} %get-tuple-element.19, f32[6,1536]{1,0:T(8,128)S(1)} %get-tuple-element.20, f32[6,12]{1,0:T(8,128)S(1)} %add_rsqrt_fusion.1, ...), kind=kOutput, calls=%fused_computation.20 | convolution fusion | flops 453795840 | bytes 6881856 | tf_op jit(solution)/shard_map/prd,de->pre/dot_general | solution.py:134
  140.6 5.9 %all-to-all-start.1 = ((bf16[16,2,4608]{2,1,0:T(2,128)(2,1)}), bf16[16,2,4608]{2,1,0:T(2,128)(2,1)}, u32[]{:S(2)}, u32[]{:S(2)}) async-start(bf16[16,2,4608]{2,1,0:T(2,128)(2,1)} %reshape.152), calls=%async_computation.1 | async-start | bytes 589824 | tf_op jit(solution)/shard_map/all_to_all | solution.py:141
  146.5 7.7 %fusion.2 = bf16[6,64,3072]{2,1,0:T(8,128)(2,1)S(1)} fusion(bf16[1536,6272]{1,0:T(8,128)(2,1)} %reshape.144, bf16[1,6,64,1536]{3,2,1,0:T(8,128)(2,1)S(1)} %copy-done, f32[6,1536]{1,0:T(8,128)} %get-tuple-element.18, f32[6,1536]{1,0:T(8,128)} %get-tuple-element.17, f32[6,64]{1,0:T(8,128)S(1)} %add_rsqrt_fusion.2, f32[6,64]{1,0:T(8,128)S(1)} %broadcast_multiply_fusion.2), kind=kOutput, calls=%fused_computation.4 | convolution fusion | flops 3628597248 | bytes 13077504 | tf_op jit(solution)/shard_map/prd,de->pre/dot_general | solution.py:131
  154.3 4.8 %reshape.124 = bf16[6,64,3,16,64]{4,3,2,1,0:T(8,128)(2,1)} reshape(bf16[6,64,3072]{2,1,0:T(8,128)(2,1)S(1)} %fusion.2) | data formatting | bytes 4718592 | tf_op jit(solution)/shard_map/reshape | solution.py:138
  159.0 5.7 %copy.73 = bf16[6,64,3,16,64]{4,1,2,0,3:T(8,128)(2,1)} copy(bf16[6,64,3,16,64]{4,3,2,1,0:T(8,128)(2,1)} %reshape.124) | data formatting | bytes 4718592 | tf_op jit(solution)/shard_map/reshape | solution.py:138
  164.8 7.8 %reshape.150 = bf16[16,2,36864]{2,1,0:T(2,128)(2,1)} reshape(bf16[16,6,3,64,64]{4,3,2,1,0:T(8,128)(2,1)} %bitcast.122) | data formatting | bytes 4718592
  172.6 7.2 %all-to-all-start = ((bf16[16,2,36864]{2,1,0:T(2,128)(2,1)}), bf16[16,2,36864]{2,1,0:T(2,128)(2,1)S(1)}, u32[]{:S(2)}, u32[]{:S(2)}) async-start(bf16[16,2,36864]{2,1,0:T(2,128)(2,1)} %reshape.150), calls=%async_computation | async-start | bytes 4718592 | tf_op jit(solution)/shard_map/all_to_all | solution.py:139
  184.5 28.8 %all-to-all-done = bf16[16,2,36864]{2,1,0:T(2,128)(2,1)S(1)} async-done(((bf16[16,2,36864]{2,1,0:T(2,128)(2,1)}), bf16[16,2,36864]{2,1,0:T(2,128)(2,1)S(1)}, u32[]{:S(2)}, u32[]{:S(2)}) %all-to-all-start) | async-done | bytes 2359328 | tf_op jit(solution)/shard_map/all_to_all | solution.py:139
  213.3 5.2 %reshape.151 = bf16[16,6,3,64,64]{4,3,2,1,0:T(8,128)(2,1)} reshape(bf16[16,2,36864]{2,1,0:T(2,128)(2,1)S(1)} %all-to-all-done) | data formatting | bytes 4718592
  218.5 6.0 %bitcast_bitcast_fusion.q_ref.ki_ref.vi_ref = bf16[16,6,3,64,64]{4,3,2,1,0:T(8,128)(2,1)} fusion(bf16[16,6,3,64,64]{4,3,2,1,0:T(8,128)(2,1)} %reshape.151), kind=kLoop, calls=%fused_computation.75 | loop fusion | bytes 4718592 | tf_op jit(solution)/shard_map/transpose | solution.py:146
  224.5 24.3 %shard_map.122 = bf16[6,1024,64]{2,1,0:T(8,128)(2,1)} custom-call(s32[6]{0:T(128)} %bitcast.132, bf16[16,6,3,64,64]{4,3,2,1,0:T(8,128)(2,1)} %bitcast_bitcast_fusion.q_ref.ki_ref.vi_ref, bf16[16,6,3,64,64]{4,3,2,1,0:T(8,128)(2,1)} %bitcast_bitcast_fusion.q_ref.ki_ref.vi_ref, bf16[16,6,3,64,64]{4,3,2,1,0:T(8,128)(2,1)} %bitcast_bitcast_fusion.q_ref.ki_ref.vi_ref, ...), custom_call_target="tpu_custom_call" | custom-call | flops 1912602624 | bytes 3440640 | tf_op jit(solution)/shard_map/pallas_call | solution.py:67
  248.8 2.5 copy.74
  251.4 2.2 reshape.154
  253.5 4.5 %all-to-all-start.2 = ((bf16[16,2,12288]{2,1,0:T(2,128)(2,1)}), bf16[16,2,12288]{2,1,0:T(2,128)(2,1)}, u32[]{:S(2)}, u32[]{:S(2)}) async-start(bf16[16,2,12288]{2,1,0:T(2,128)(2,1)} %reshape.154), calls=%async_computation.2 | async-start | bytes 1572864 | tf_op jit(solution)/shard_map/all_to_all | solution.py:151
  261.3 5.5 %reshape.128 = bf16[128,9,1536]{2,1,0:T(8,128)(2,1)} reshape(bf16[1536,1152]{1,0:T(8,128)(2,1)S(1)} %slice-done) | data formatting | bytes 7077888 | tf_op jit(solution)/shard_map/reshape | solution.py:123
  266.8 2.4 slice_reduce_fusion
  270.3 3.5 %reshape.155 = bf16[1024,1,6,64]{3,2,1,0:T(8,128)(2,1)S(1)} reshape(bf16[16,2,12288]{2,1,0:T(2,128)(2,1)} %all-to-all-done.2) | data formatting | bytes 1572864
  273.7 2.2 copy.69
  275.9 2.7 dot_general.16
  278.7 3.4 %fusion.45 = (f32[6,64]{1,0:T(8,128)S(1)}, f32[6,64,1536]{2,1,0:T(8,128)S(1)}) fusion(bf16[6,64,1024]{2,1,0:T(8,128)(2,1)S(1)} %dot_general.16, bf16[128,9,1536]{2,1,0:T(8,128)(2,1)} %reshape.128, f32[6,1536]{1,0:T(8,128)S(1)} %bitcast.131, bf16[1,6,64,1536]{3,2,1,0:T(8,128)(2,1)S(1)} %copy-done.1), kind=kOutput, calls=%fused_computation.74 | convolution fusion | flops 1210318464 | bytes 7509504 | tf_op jit(solution)/shard_map/dot_general | solution.py:154
  283.9 2.3 collective-permute-start
  287.0 2.6 collective-permute-done
  (67 shorter events, 23.5 us)
Async XLA Ops:
  7.2 8.0 %copy-start = (bf16[1,6,64,1536]{3,2,1,0:T(8,128)(2,1)S(1)}, bf16[1,6,64,1536]{3,2,1,0:T(8,128)(2,1)}, u32[]{:S(2)}) copy-start(bf16[1,6,64,1536]{3,2,1,0:T(8,128)(2,1)} %param.11) | copy-start | bytes 3538948
  7.2 8.5 %copy-start.9 = (f32[1,6,2,1536]{3,2,1,0:T(2,128)S(1)}, f32[1,6,2,1536]{3,2,1,0:T(2,128)}, u32[]{:S(2)}) copy-start(f32[1,6,2,1536]{3,2,1,0:T(2,128)} %param.14) | copy-start | bytes 221188
  7.2 8.5 %copy-start.4 = (f32[1,6,5,1536]{3,0,2,1:T(1,128)S(1)}, f32[1,6,5,1536]{3,0,2,1:T(1,128)}, u32[]{:S(2)}) copy-start(f32[1,6,5,1536]{3,0,2,1:T(1,128)} %param.13) | copy-start | bytes 552964
  7.2 100.9 %all-gather.4.cloned.1.call-start = ((), (), s32[]{:S(2)}) async-start(), calls=%async_computation.3 | async-start | bytes 25890816 | tf_op jit(solution)/shard_map/all_gather | solution.py:119
  17.0 117.5 %copy-start.2 = (bf16[1,6,12,1536]{3,2,1,0:T(8,128)(2,1)S(1)}, bf16[1,6,12,1536]{3,2,1,0:T(8,128)(2,1)}, u32[]{:S(2)}) copy-start(bf16[1,6,12,1536]{3,2,1,0:T(8,128)(2,1)} %param.12) | copy-start | bytes 663556
  140.6 32.0 %all-to-all-start.1 = ((bf16[16,2,4608]{2,1,0:T(2,128)(2,1)}), bf16[16,2,4608]{2,1,0:T(2,128)(2,1)}, u32[]{:S(2)}, u32[]{:S(2)}) async-start(bf16[16,2,4608]{2,1,0:T(2,128)(2,1)} %reshape.152), calls=%async_computation.1 | async-start | bytes 589824 | tf_op jit(solution)/shard_map/all_to_all | solution.py:141
  172.6 40.6 %all-to-all-start = ((bf16[16,2,36864]{2,1,0:T(2,128)(2,1)}), bf16[16,2,36864]{2,1,0:T(2,128)(2,1)S(1)}, u32[]{:S(2)}, u32[]{:S(2)}) async-start(bf16[16,2,36864]{2,1,0:T(2,128)(2,1)} %reshape.150), calls=%async_computation | async-start | bytes 4718592 | tf_op jit(solution)/shard_map/all_to_all | solution.py:139
  251.3 6.7 %copy-start.7 = (f32[1,6,1,1536]{3,0,2,1:T(1,128)S(1)}, f32[1,6,1,1536]{3,0,2,1:T(1,128)}, u32[]{:S(2)}) copy-start(f32[1,6,1,1536]{3,0,2,1:T(1,128)} %get-tuple-element.8) | copy-start | bytes 110596
  251.3 7.4 %copy-start.5 = (f32[1,6,1,1536]{3,0,2,1:T(1,128)S(1)}, f32[1,6,1,1536]{3,0,2,1:T(1,128)}, u32[]{:S(2)}) copy-start(f32[1,6,1,1536]{3,0,2,1:T(1,128)} %get-tuple-element.6) | copy-start | bytes 110596
  251.3 7.3 %copy-start.6 = (f32[1,6,1,1536]{3,0,2,1:T(1,128)S(1)}, f32[1,6,1,1536]{3,0,2,1:T(1,128)}, u32[]{:S(2)}) copy-start(f32[1,6,1,1536]{3,0,2,1:T(1,128)} %get-tuple-element.9) | copy-start | bytes 110596
  253.5 16.7 %all-to-all-start.2 = ((bf16[16,2,12288]{2,1,0:T(2,128)(2,1)}), bf16[16,2,12288]{2,1,0:T(2,128)(2,1)}, u32[]{:S(2)}, u32[]{:S(2)}) async-start(bf16[16,2,12288]{2,1,0:T(2,128)(2,1)} %reshape.154), calls=%async_computation.2 | async-start | bytes 1572864 | tf_op jit(solution)/shard_map/all_to_all | solution.py:151
  259.3 2.0 slice-start
  273.7 4.9 %copy-start.1 = (bf16[1,6,64,1536]{3,2,1,0:T(8,128)(2,1)S(1)}, bf16[1,6,64,1536]{3,2,1,0:T(8,128)(2,1)}, u32[]{:S(2)}) copy-start(bf16[1,6,64,1536]{3,2,1,0:T(8,128)(2,1)} %param.11) | copy-start | bytes 3538948
  273.7 4.9 %copy-start.10 = (f32[1,6,1,1536]{3,1,2,0:T(8,128)S(1)}, f32[1,6,1,1536]{3,1,2,0:T(8,128)}, u32[]{:S(2)}) copy-start(f32[1,6,1,1536]{3,1,2,0:T(8,128)} %copy.72) | copy-start | bytes 110596
  282.0 1.0 copy-start.3
  282.0 1.0 copy-start.11
  282.0 1.0 copy-start.12
  282.1 7.6 %copy-start.8 = (f32[6,64,32]{1,2,0:T(8,128)S(1)}, f32[6,64,32]{1,2,0:T(8,128)}, u32[]{:S(2)}) copy-start(f32[6,64,32]{1,2,0:T(8,128)} %param.20) | copy-start | bytes 147460
  283.9 5.7 %collective-permute-start = (bf16[6,64,32]{1,2,0:T(8,128)(2,1)S(1)}, bf16[6,64,32]{1,2,0:T(8,128)(2,1)S(1)}, u32[]{:S(2)}, u32[]{:S(2)}) collective-permute-start(bf16[6,64,32]{1,2,0:T(8,128)(2,1)S(1)} %dynamic-slice_convert_fusion), channel_id=1, source_target_pairs={{0,64},{64,0},{1,65},{65,1},{2,66},{66,2},{3,67},{67,3},{4,68},{68... | collective-permute-start | bytes 73736 | tf_op jit(solution)/shard_map/ppermute | solution.py:20
Sparse Core Ops, SparseCore 0:
  11.5 96.5 all-gather.3

commit v11 on v10

--- a/solution.py
+++ b/solution.py
@@ -135,17 +135,16 @@
         "prd,de->pre", text_in, full_txt, preferred_element_type=jnp.float32
     ).astype(jnp.bfloat16)
 
-    img_split = qkv_image.reshape(prompts, img_rows, 3, nseq, per_dev * HD)
-    img_heads = lax.all_to_all(img_split, "seq", 3, 1, tiled=True)
+    img_split = jnp.transpose(
+        qkv_image.reshape(prompts, img_rows, 3, nseq, per_dev * HD), (3, 0, 2, 1, 4)
+    )
+    img_parts = lax.all_to_all(img_split, "seq", 0, 0, tiled=True)
     txt_split = qkv_text.reshape(prompts, txt_rows, 2, nseq, per_dev * HD)
     txt_heads = lax.all_to_all(txt_split, "seq", 3, 1, tiled=True)
-    all_img = img_heads.shape[1]
+    all_img = nseq * img_rows
 
     assert per_dev == 1
     lengths = text_lengths[0]
-    img_parts = jnp.transpose(
-        img_heads.reshape(prompts, nseq, img_rows, 3, HD), (1, 0, 3, 2, 4)
-    )
     mixture = attend(lengths, img_parts, txt_heads[:, :, 0, 0], txt_heads[:, :, 1, 0])
     head_out = mixture.reshape(prompts, all_img, 1, per_dev * HD)
     token_out = lax.all_to_all(head_out, "seq", 1, 2, tiled=True)

time: 299 us -> 293 us (0.980)
  local copies, waits for them, and re-layouts: 90.5 us -> 84.5 us
    transpose x1 -> x0, local copies, waits for them, and re-layouts: 6.04 us -> none  [block(): jnp.transpose(img_heads.reshape(prompts, nseq, img_rows, 3, HD), (1, 0, 3...]
where the time goes in v11:
time: 293 us; the launch traced here: 291 us
  waiting for transfers between devices  122 us (42%)
  local copies, waits for them, and re-layouts  84.5 us (29%)
  Pallas kernels  24.3 us (8%)
  starting transfers between devices  19.7 us (7%)
  matrix products  15.9 us (5%)
  between operations  15.1 us (5%)
  other arithmetic  8.98 us (3%)
    all_gather x1, waiting for transfers between devices, block(): gathered = lax.all_gather(local_all, all_axes, axis=0, tiled=False)  91 us
    unnamed x36, local copies, waits for them, and re-layouts  50.4 us
    all_to_all x1, waiting for transfers between devices, block(): img_parts = lax.all_to_all(img_split, 'seq', 0, 0, tiled=True)  28.8 us
    pallas_call x1, Pallas kernels, attend(): pl.pallas_call(attend_kernel, grid=(batch, rows // block), in_specs=[pl.B...  24.3 us
    reshape x2, local copies, waits for them, and re-layouts, block(): qkv_image.reshape(prompts, img_rows, 3, nseq, per_dev * HD)  10.5 us
    dot_general x1, matrix products, block(): jnp.einsum('prd,de->pre', image_in, full_img, preferred_element_type=jnp....  7.7 us
    all_to_all x1, starting transfers between devices, block(): img_parts = lax.all_to_all(img_split, 'seq', 0, 0, tiled=True)  7.18 us
    all_to_all x1, starting transfers between devices, block(): txt_heads = lax.all_to_all(txt_split, 'seq', 3, 1, tiled=True)  5.89 us
  transfers between devices with their start and end apart: 5, of which 3 were waited for; matrix products, arithmetic and copies ran while one was open for 16% of the time, Pallas kernels for 0%

profile of v11, /device:TPU:0, one launch (start us, length us, event | category | flops | bytes accessed | tf_op | source)
XLA Modules:
  0.0 290.9 jit_solution(11339176672572164289)
XLA Ops:
  17.0 91.0 %all-gather.4.cloned.1.call-done = bf16[128,12,6272]{2,1,0:T(8,128)(2,1)} async-done(((bf16[1,12,6272]{2,1,0:T(8,128)(2,1)}), bf16[128,12,6272]{2,1,0:T(8,128)(2,1)}) %all-gather.4.cloned.1.call-update) | async-done | bytes 19267600 | tf_op jit(solution)/shard_map/all_gather | solution.py:119
  108.1 26.4 %reshape.139 = bf16[1536,6272]{1,0:T(8,128)(2,1)} reshape(bf16[128,12,6272]{2,1,0:T(8,128)(2,1)} %all-gather.4.cloned.1.call-done) | data formatting | bytes 38535168
  134.5 4.0 %fusion.13 = bf16[6,12,2048]{2,1,0:T(8,128)(2,1)S(1)} fusion(bf16[1536,6272]{1,0:T(8,128)(2,1)} %reshape.139, bf16[1,6,12,1536]{3,2,1,0:T(8,128)(2,1)S(1)} %copy-done.2, f32[6,1536]{1,0:T(8,128)S(1)} %get-tuple-element.19, f32[6,1536]{1,0:T(8,128)S(1)} %get-tuple-element.20, f32[6,12]{1,0:T(8,128)S(1)} %add_rsqrt_fusion.1, ...), kind=kOutput, calls=%fused_computation.21 | convolution fusion | flops 453795840 | bytes 6881856 | tf_op jit(solution)/shard_map/prd,de->pre/dot_general | solution.py:134
  140.6 5.9 %all-to-all-start.1 = ((bf16[16,2,4608]{2,1,0:T(2,128)(2,1)}), bf16[16,2,4608]{2,1,0:T(2,128)(2,1)}, u32[]{:S(2)}, u32[]{:S(2)}) async-start(bf16[16,2,4608]{2,1,0:T(2,128)(2,1)} %reshape.147), calls=%async_computation.1 | async-start | bytes 589824 | tf_op jit(solution)/shard_map/all_to_all | solution.py:143
  146.5 7.7 %fusion.2 = bf16[6,64,3072]{2,1,0:T(8,128)(2,1)S(1)} fusion(bf16[1536,6272]{1,0:T(8,128)(2,1)} %reshape.139, bf16[1,6,64,1536]{3,2,1,0:T(8,128)(2,1)S(1)} %copy-done, f32[6,1536]{1,0:T(8,128)} %get-tuple-element.18, f32[6,1536]{1,0:T(8,128)} %get-tuple-element.17, f32[6,64]{1,0:T(8,128)S(1)} %add_rsqrt_fusion.2, f32[6,64]{1,0:T(8,128)S(1)} %broadcast_multiply_fusion.2), kind=kOutput, calls=%fused_computation.5 | convolution fusion | flops 3628597248 | bytes 13077504 | tf_op jit(solution)/shard_map/prd,de->pre/dot_general | solution.py:131
  154.3 4.8 %reshape.120 = bf16[6,64,3,16,64]{4,3,2,1,0:T(8,128)(2,1)} reshape(bf16[6,64,3072]{2,1,0:T(8,128)(2,1)S(1)} %fusion.2) | data formatting | bytes 4718592 | tf_op jit(solution)/shard_map/reshape | solution.py:139
  159.0 5.7 %copy.69 = bf16[6,64,3,16,64]{4,1,2,0,3:T(8,128)(2,1)} copy(bf16[6,64,3,16,64]{4,3,2,1,0:T(8,128)(2,1)} %reshape.120) | data formatting | bytes 4718592 | tf_op jit(solution)/shard_map/reshape | solution.py:139
  164.8 7.8 %reshape.145 = bf16[16,2,36864]{2,1,0:T(2,128)(2,1)} reshape(bf16[16,6,3,64,64]{4,3,2,1,0:T(8,128)(2,1)} %bitcast.112) | data formatting | bytes 4718592
  172.6 7.2 %all-to-all-start = ((bf16[16,2,36864]{2,1,0:T(2,128)(2,1)}), bf16[16,2,36864]{2,1,0:T(2,128)(2,1)S(1)}, u32[]{:S(2)}, u32[]{:S(2)}) async-start(bf16[16,2,36864]{2,1,0:T(2,128)(2,1)} %reshape.145), calls=%async_computation | async-start | bytes 4718592 | tf_op jit(solution)/shard_map/all_to_all | solution.py:141
  184.5 28.8 %all-to-all-done = bf16[16,2,36864]{2,1,0:T(2,128)(2,1)S(1)} async-done(((bf16[16,2,36864]{2,1,0:T(2,128)(2,1)}), bf16[16,2,36864]{2,1,0:T(2,128)(2,1)S(1)}, u32[]{:S(2)}, u32[]{:S(2)}) %all-to-all-start) | async-done | bytes 2359328 | tf_op jit(solution)/shard_map/all_to_all | solution.py:141
  213.3 5.2 %reshape.146.q_ref.ki_ref.vi_ref = bf16[16,6,3,64,64]{4,3,2,1,0:T(8,128)(2,1)} reshape(bf16[16,2,36864]{2,1,0:T(2,128)(2,1)S(1)} %all-to-all-done) | data formatting | bytes 4718592
  218.5 24.3 %shard_map.122 = bf16[6,1024,64]{2,1,0:T(8,128)(2,1)} custom-call(s32[6]{0:T(128)} %bitcast.122, bf16[16,6,3,64,64]{4,3,2,1,0:T(8,128)(2,1)} %reshape.146.q_ref.ki_ref.vi_ref, bf16[16,6,3,64,64]{4,3,2,1,0:T(8,128)(2,1)} %reshape.146.q_ref.ki_ref.vi_ref, bf16[16,6,3,64,64]{4,3,2,1,0:T(8,128)(2,1)} %reshape.146.q_ref.ki_ref.vi_ref, ...), custom_call_target="tpu_custom_call" | custom-call | flops 1912602624 | bytes 3440640 | tf_op jit(solution)/shard_map/pallas_call | solution.py:67
  242.8 2.5 copy.74
  245.3 2.2 reshape.149
  247.5 4.3 %all-to-all-start.2 = ((bf16[16,2,12288]{2,1,0:T(2,128)(2,1)}), bf16[16,2,12288]{2,1,0:T(2,128)(2,1)}, u32[]{:S(2)}, u32[]{:S(2)}) async-start(bf16[16,2,12288]{2,1,0:T(2,128)(2,1)} %reshape.149), calls=%async_computation.2 | async-start | bytes 1572864 | tf_op jit(solution)/shard_map/all_to_all | solution.py:150
  253.0 2.0 slice-done
  255.0 5.5 %reshape.123 = bf16[128,9,1536]{2,1,0:T(8,128)(2,1)} reshape(bf16[1536,1152]{1,0:T(8,128)(2,1)S(1)} %slice-done) | data formatting | bytes 7077888 | tf_op jit(solution)/shard_map/reshape | solution.py:123
  260.5 2.4 slice_reduce_fusion
  264.0 3.5 %reshape.150 = bf16[1024,1,6,64]{3,2,1,0:T(8,128)(2,1)S(1)} reshape(bf16[16,2,12288]{2,1,0:T(2,128)(2,1)} %all-to-all-done.2) | data formatting | bytes 1572864
  267.5 2.2 copy.70
  269.6 2.7 dot_general.16
  272.4 3.4 %fusion.45 = (f32[6,64]{1,0:T(8,128)S(1)}, f32[6,64,1536]{2,1,0:T(8,128)S(1)}) fusion(bf16[6,64,1024]{2,1,0:T(8,128)(2,1)S(1)} %dot_general.16, bf16[128,9,1536]{2,1,0:T(8,128)(2,1)} %reshape.123, f32[6,1536]{1,0:T(8,128)S(1)} %bitcast.121, bf16[1,6,64,1536]{3,2,1,0:T(8,128)(2,1)S(1)} %copy-done.1), kind=kOutput, calls=%fused_computation.75 | convolution fusion | flops 1210318464 | bytes 7509504 | tf_op jit(solution)/shard_map/dot_general | solution.py:153
  277.7 2.3 collective-permute-start
  280.7 2.6 collective-permute-done
  (66 shorter events, 21.5 us)
Async XLA Ops:
  7.2 8.0 %copy-start = (bf16[1,6,64,1536]{3,2,1,0:T(8,128)(2,1)S(1)}, bf16[1,6,64,1536]{3,2,1,0:T(8,128)(2,1)}, u32[]{:S(2)}) copy-start(bf16[1,6,64,1536]{3,2,1,0:T(8,128)(2,1)} %param.11) | copy-start | bytes 3538948
  7.2 8.5 %copy-start.9 = (f32[1,6,2,1536]{3,2,1,0:T(2,128)S(1)}, f32[1,6,2,1536]{3,2,1,0:T(2,128)}, u32[]{:S(2)}) copy-start(f32[1,6,2,1536]{3,2,1,0:T(2,128)} %param.14) | copy-start | bytes 221188
  7.2 8.5 %copy-start.4 = (f32[1,6,5,1536]{3,0,2,1:T(1,128)S(1)}, f32[1,6,5,1536]{3,0,2,1:T(1,128)}, u32[]{:S(2)}) copy-start(f32[1,6,5,1536]{3,0,2,1:T(1,128)} %param.13) | copy-start | bytes 552964
  7.2 100.9 %all-gather.4.cloned.1.call-start = ((), (), s32[]{:S(2)}) async-start(), calls=%async_computation.3 | async-start | bytes 25890816 | tf_op jit(solution)/shard_map/all_gather | solution.py:119
  17.0 117.5 %copy-start.2 = (bf16[1,6,12,1536]{3,2,1,0:T(8,128)(2,1)S(1)}, bf16[1,6,12,1536]{3,2,1,0:T(8,128)(2,1)}, u32[]{:S(2)}) copy-start(bf16[1,6,12,1536]{3,2,1,0:T(8,128)(2,1)} %param.12) | copy-start | bytes 663556
  140.6 32.0 %all-to-all-start.1 = ((bf16[16,2,4608]{2,1,0:T(2,128)(2,1)}), bf16[16,2,4608]{2,1,0:T(2,128)(2,1)}, u32[]{:S(2)}, u32[]{:S(2)}) async-start(bf16[16,2,4608]{2,1,0:T(2,128)(2,1)} %reshape.147), calls=%async_computation.1 | async-start | bytes 589824 | tf_op jit(solution)/shard_map/all_to_all | solution.py:143
  172.6 40.6 %all-to-all-start = ((bf16[16,2,36864]{2,1,0:T(2,128)(2,1)}), bf16[16,2,36864]{2,1,0:T(2,128)(2,1)S(1)}, u32[]{:S(2)}, u32[]{:S(2)}) async-start(bf16[16,2,36864]{2,1,0:T(2,128)(2,1)} %reshape.145), calls=%async_computation | async-start | bytes 4718592 | tf_op jit(solution)/shard_map/all_to_all | solution.py:141
  245.3 6.5 %copy-start.7 = (f32[1,6,1,1536]{3,0,2,1:T(1,128)S(1)}, f32[1,6,1,1536]{3,0,2,1:T(1,128)}, u32[]{:S(2)}) copy-start(f32[1,6,1,1536]{3,0,2,1:T(1,128)} %get-tuple-element.8) | copy-start | bytes 110596
  245.3 7.1 %copy-start.5 = (f32[1,6,1,1536]{3,0,2,1:T(1,128)S(1)}, f32[1,6,1,1536]{3,0,2,1:T(1,128)}, u32[]{:S(2)}) copy-start(f32[1,6,1,1536]{3,0,2,1:T(1,128)} %get-tuple-element.6) | copy-start | bytes 110596
  245.3 7.1 %copy-start.6 = (f32[1,6,1,1536]{3,0,2,1:T(1,128)S(1)}, f32[1,6,1,1536]{3,0,2,1:T(1,128)}, u32[]{:S(2)}) copy-start(f32[1,6,1,1536]{3,0,2,1:T(1,128)} %get-tuple-element.9) | copy-start | bytes 110596
  247.5 16.5 %all-to-all-start.2 = ((bf16[16,2,12288]{2,1,0:T(2,128)(2,1)}), bf16[16,2,12288]{2,1,0:T(2,128)(2,1)}, u32[]{:S(2)}, u32[]{:S(2)}) async-start(bf16[16,2,12288]{2,1,0:T(2,128)(2,1)} %reshape.149), calls=%async_computation.2 | async-start | bytes 1572864 | tf_op jit(solution)/shard_map/all_to_all | solution.py:150
  253.0 2.0 slice-start
  267.4 4.9 %copy-start.1 = (bf16[1,6,64,1536]{3,2,1,0:T(8,128)(2,1)S(1)}, bf16[1,6,64,1536]{3,2,1,0:T(8,128)(2,1)}, u32[]{:S(2)}) copy-start(bf16[1,6,64,1536]{3,2,1,0:T(8,128)(2,1)} %param.11) | copy-start | bytes 3538948
  267.4 4.9 %copy-start.10 = (f32[1,6,1,1536]{3,1,2,0:T(8,128)S(1)}, f32[1,6,1,1536]{3,1,2,0:T(8,128)}, u32[]{:S(2)}) copy-start(f32[1,6,1,1536]{3,1,2,0:T(8,128)} %copy.73) | copy-start | bytes 110596
  275.7 1.0 copy-start.3
  275.7 1.0 copy-start.11
  275.8 1.0 copy-start.12
  275.8 7.6 %copy-start.8 = (f32[6,64,32]{1,2,0:T(8,128)S(1)}, f32[6,64,32]{1,2,0:T(8,128)}, u32[]{:S(2)}) copy-start(f32[6,64,32]{1,2,0:T(8,128)} %param.20) | copy-start | bytes 147460
  277.7 5.7 %collective-permute-start = (bf16[6,64,32]{1,2,0:T(8,128)(2,1)S(1)}, bf16[6,64,32]{1,2,0:T(8,128)(2,1)S(1)}, u32[]{:S(2)}, u32[]{:S(2)}) collective-permute-start(bf16[6,64,32]{1,2,0:T(8,128)(2,1)S(1)} %dynamic-slice_convert_fusion), channel_id=1, source_target_pairs={{0,64},{64,0},{1,65},{65,1},{2,66},{66,2},{3,67},{67,3},{4,68},{68... | collective-permute-start | bytes 73736 | tf_op jit(solution)/shard_map/ppermute | solution.py:20
Sparse Core Ops, SparseCore 0:
  11.5 96.5 all-gather.3

commit v12 on v11

--- a/solution.py
+++ b/solution.py
@@ -53,7 +53,7 @@
     acc = jnp.dot(
         e_img.astype(jnp.bfloat16), v_img, preferred_element_type=jnp.float32
     ) + jnp.dot(e_txt.astype(jnp.bfloat16), vt_ref[0], preferred_element_type=jnp.float32)
-    o_ref[0] = (acc / totals).astype(o_ref.dtype)
+    o_ref[:, 0] = (acc / totals).astype(o_ref.dtype).reshape(o_ref.shape[0], -1, width)
 
 
 def attend(lengths, img_parts, k_txt, v_txt, block=256):
@@ -75,8 +75,8 @@
             pl.BlockSpec((1, n_txt, width), lambda b, i: (b, 0, 0)),
             pl.BlockSpec((1, n_txt, width), lambda b, i: (b, 0, 0)),
         ],
-        out_specs=pl.BlockSpec((1, block, width), lambda b, i: (b, i, 0)),
-        out_shape=jax.ShapeDtypeStruct((batch, rows, width), jnp.bfloat16),
+        out_specs=pl.BlockSpec((per_block, 1, src_rows, width), lambda b, i: (i, b, 0, 0)),
+        out_shape=jax.ShapeDtypeStruct((sources, batch, src_rows, width), jnp.bfloat16),
         cost_estimate=pl.CostEstimate(
             flops=flops, transcendentals=batch * rows * (rows + n_txt), bytes_accessed=moved
         ),
@@ -98,7 +98,6 @@
 ):
     all_axes = ("guid", "xlo", "core", "seq")
     prompts = img_hidden.shape[1]
-    img_rows = img_hidden.shape[2]
     txt_rows = txt_hidden.shape[2]
     model_width = img_hidden.shape[3]
     nseq = lax.axis_size("seq")
@@ -128,32 +127,31 @@
     text_in = modulate(txt_hidden[0], txt_mod[0, :, 0], txt_mod[0, :, 1])
     head_count = attn_width // HD
     per_dev = head_count // nseq
-    qkv_image = jnp.einsum(
-        "prd,de->pre", image_in, full_img, preferred_element_type=jnp.float32
+    img_split = jnp.einsum(
+        "prd,dthe->hptre",
+        image_in,
+        full_img.reshape(-1, 3, nseq, per_dev * HD),
+        preferred_element_type=jnp.float32,
     ).astype(jnp.bfloat16)
     qkv_text = jnp.einsum(
         "prd,de->pre", text_in, full_txt, preferred_element_type=jnp.float32
     ).astype(jnp.bfloat16)
 
-    img_split = jnp.transpose(
-        qkv_image.reshape(prompts, img_rows, 3, nseq, per_dev * HD), (3, 0, 2, 1, 4)
-    )
     img_parts = lax.all_to_all(img_split, "seq", 0, 0, tiled=True)
     txt_split = qkv_text.reshape(prompts, txt_rows, 2, nseq, per_dev * HD)
     txt_heads = lax.all_to_all(txt_split, "seq", 3, 1, tiled=True)
-    all_img = nseq * img_rows
 
     assert per_dev == 1
     lengths = text_lengths[0]
     mixture = attend(lengths, img_parts, txt_heads[:, :, 0, 0], txt_heads[:, :, 1, 0])
-    head_out = mixture.reshape(prompts, all_img, 1, per_dev * HD)
-    token_out = lax.all_to_all(head_out, "seq", 1, 2, tiled=True)
-    attended = token_out.reshape(prompts * img_rows, attn_width)
-
-    projected = jnp.dot(attended, full_out, preferred_element_type=jnp.float32)
-    residual = img_hidden[0].astype(jnp.float32) + img_mod[0, :, 2][:, None, :] * projected.reshape(
-        prompts, img_rows, model_width
-    )
+    head_parts = lax.all_to_all(mixture, "seq", 0, 0, tiled=True)
+    projected = jnp.einsum(
+        "hprd,hdc->prc",
+        head_parts,
+        full_out.reshape(nseq, per_dev * HD, model_width),
+        preferred_element_type=jnp.float32,
+    )
+    residual = img_hidden[0].astype(jnp.float32) + img_mod[0, :, 2][:, None, :] * projected
     final_in = modulate(residual, img_mod[0, :, 3], img_mod[0, :, 4])
     guid_index = lax.axis_index("guid")
     half_width = latent.shape[2]

time: 293 us -> 302 us (1.031)
  local copies, waits for them, and re-layouts: 84.5 us -> 89.8 us
  matrix products: 15.9 us -> 19.2 us
    slice x0 -> x4, local copies, waits for them, and re-layouts: none -> 21 us  [the longest x2 21 us: block(): full_img = full_all[:, :img_width]]
    reshape x3 -> x0, local copies, waits for them, and re-layouts: 13 us -> none  [the longest x2 10.5 us: block(): qkv_image.reshape(prompts, img_rows, 3, nseq, per_dev * HD)]
    unnamed x36 -> x31, local copies, waits for them, and re-layouts: 50.4 us -> 54.7 us
    dot_general x2, matrix products: 11.1 us -> 14.4 us  [the longest x1 11.1 us: block(): jnp.einsum('prd,dthe->hptre', image_in, full_img.reshape(-1, 3, nseq, per...]
  transfers between devices with their start and end apart: 5 -> 5, of which waited for: 3 -> 3; matrix products, arithmetic and copies ran while one was open for 16% -> 12% of each run, Pallas kernels for 0% -> 0%
where the time goes in v12:
time: 302 us; the launch traced here: 300 us
  waiting for transfers between devices  123 us (41%)
  local copies, waits for them, and re-layouts  89.8 us (30%)
  Pallas kernels  24.4 us (8%)
  starting transfers between devices  19.7 us (7%)
  matrix products  19.2 us (6%)
  between operations  15 us (5%)
  other arithmetic  8.34 us (3%)
    all_gather x1, waiting for transfers between devices, block(): gathered = lax.all_gather(local_all, all_axes, axis=0, tiled=False)  91 us
    unnamed x31, local copies, waits for them, and re-layouts  54.7 us
    all_to_all x1, waiting for transfers between devices, block(): img_parts = lax.all_to_all(img_split, 'seq', 0, 0, tiled=True)  29.8 us
    pallas_call x1, Pallas kernels, attend(): pl.pallas_call(attend_kernel, grid=(batch, rows // block), in_specs=[pl.B...  24.4 us
    slice x2, local copies, waits for them, and re-layouts, block(): full_img = full_all[:, :img_width]  21 us
    dot_general x1, matrix products, block(): jnp.einsum('prd,dthe->hptre', image_in, full_img.reshape(-1, 3, nseq, per...  11.1 us
    all_to_all x1, starting transfers between devices, block(): img_parts = lax.all_to_all(img_split, 'seq', 0, 0, tiled=True)  7.22 us
  transfers between devices with their start and end apart: 5, of which 3 were waited for; matrix products, arithmetic and copies ran while one was open for 12% of the time, Pallas kernels for 0%

profile of v12, /device:TPU:0, one launch (start us, length us, event | category | flops | bytes accessed | tf_op | source)
XLA Modules:
  0.0 299.9 jit_solution(12750986947343736677)
XLA Ops:
  9.7 1.6 maximum_bitcast_fusion
  12.5 1.2 fusion.25
  13.6 1.5 convert_reduce_fusion
  17.1 91.0 %all-gather.4.cloned.1.call-done = bf16[128,12,6272]{2,1,0:T(8,128)(2,1)} async-done(((bf16[1,12,6272]{2,1,0:T(8,128)(2,1)}), bf16[128,12,6272]{2,1,0:T(8,128)(2,1)}) %all-gather.4.cloned.1.call-update) | async-done | bytes 19267600 | tf_op jit(solution)/shard_map/all_gather | solution.py:118
  108.1 26.4 %reshape.127 = bf16[1536,6272]{1,0:T(8,128)(2,1)} reshape(bf16[128,12,6272]{2,1,0:T(8,128)(2,1)} %all-gather.4.cloned.1.call-done) | data formatting | bytes 38535168
  134.5 8.2 %slice.60 = bf16[1536,3072]{1,0:T(8,128)(2,1)} slice(bf16[1536,6272]{1,0:T(8,128)(2,1)} %reshape.127), slice={[0:1536], [0:3072]} | slice | bytes 18874368 | tf_op jit(solution)/shard_map/slice | solution.py:120
  142.7 12.8 %copy.27 = bf16[1536,3072]{0,1:T(8,128)(2,1)} copy(bf16[1536,3072]{1,0:T(8,128)(2,1)} %slice.60) | data formatting | bytes 18874368 | tf_op jit(solution)/shard_map/slice | solution.py:120
  155.5 4.0 %fusion.14 = bf16[6,12,2048]{2,1,0:T(8,128)(2,1)S(1)} fusion(bf16[1536,6272]{1,0:T(8,128)(2,1)} %reshape.127, bf16[1,6,12,1536]{3,2,1,0:T(8,128)(2,1)S(1)} %copy-done.2, f32[6,1536]{1,0:T(8,128)S(1)} %get-tuple-element.19, f32[6,1536]{1,0:T(8,128)S(1)} %get-tuple-element.20, f32[6,12]{1,0:T(8,128)S(1)} %add_rsqrt_fusion.1, ...), kind=kOutput, calls=%fused_computation.20 | convolution fusion | flops 453795840 | bytes 6881856 | tf_op jit(solution)/shard_map/prd,de->pre/dot_general | solution.py:136
  161.6 5.8 %all-to-all-start.1 = ((bf16[16,2,4608]{2,1,0:T(2,128)(2,1)}), bf16[16,2,4608]{2,1,0:T(2,128)(2,1)S(1)}, u32[]{:S(2)}, u32[]{:S(2)}) async-start(bf16[16,2,4608]{2,1,0:T(2,128)(2,1)} %reshape.137), calls=%async_computation.1 | async-start | bytes 589824 | tf_op jit(solution)/shard_map/all_to_all | solution.py:142
  167.4 11.1 %convert_bitcast_fusion = bf16[16,6,3,64,64]{4,3,2,1,0:T(8,128)(2,1)} fusion(bf16[1536,3,16,64,1]{0,3,2,1,4:T(8,128)(2,1)} %bitcast.96, bf16[1,6,64,1536]{3,2,1,0:T(8,128)(2,1)S(1)} %copy-done.1, f32[6,1536]{1,0:T(8,128)S(1)} %get-tuple-element.18, f32[6,1536]{1,0:T(8,128)S(1)} %get-tuple-element.16, f32[6,64]{1,0:T(8,128)S(1)} %add_rsqrt_fusion.2, ...), kind=kOutput, calls=%fused_computation.4 | convolution fusion | flops 3628597248 | bytes 13052928 | tf_op jit(solution)/shard_map/prd,dthe->hptre/dot_general | solution.py:130
  178.5 7.8 %reshape.135 = bf16[16,2,36864]{2,1,0:T(2,128)(2,1)} reshape(bf16[16,6,3,64,64]{4,3,2,1,0:T(8,128)(2,1)} %convert_bitcast_fusion) | data formatting | bytes 4718592
  186.4 7.2 %all-to-all-start = ((bf16[16,2,36864]{2,1,0:T(2,128)(2,1)}), bf16[16,2,36864]{2,1,0:T(2,128)(2,1)S(1)}, u32[]{:S(2)}, u32[]{:S(2)}) async-start(bf16[16,2,36864]{2,1,0:T(2,128)(2,1)} %reshape.135), calls=%async_computation | async-start | bytes 4718592 | tf_op jit(solution)/shard_map/all_to_all | solution.py:140
  197.3 29.8 %all-to-all-done = bf16[16,2,36864]{2,1,0:T(2,128)(2,1)S(1)} async-done(((bf16[16,2,36864]{2,1,0:T(2,128)(2,1)}), bf16[16,2,36864]{2,1,0:T(2,128)(2,1)S(1)}, u32[]{:S(2)}, u32[]{:S(2)}) %all-to-all-start) | async-done | bytes 2359328 | tf_op jit(solution)/shard_map/all_to_all | solution.py:140
  227.0 5.3 %reshape.136.q_ref.ki_ref.vi_ref = bf16[16,6,3,64,64]{4,3,2,1,0:T(8,128)(2,1)} reshape(bf16[16,2,36864]{2,1,0:T(2,128)(2,1)S(1)} %all-to-all-done) | data formatting | bytes 4718592
  232.3 24.4 %shard_map.122 = bf16[16,6,64,64]{3,2,1,0:T(8,128)(2,1)} custom-call(s32[6]{0:T(128)} %bitcast.102, bf16[16,6,3,64,64]{4,3,2,1,0:T(8,128)(2,1)} %reshape.136.q_ref.ki_ref.vi_ref, bf16[16,6,3,64,64]{4,3,2,1,0:T(8,128)(2,1)} %reshape.136.q_ref.ki_ref.vi_ref, bf16[16,6,3,64,64]{4,3,2,1,0:T(8,128)(2,1)} %reshape.136.q_ref.ki_ref.vi_ref, ...), custom_call_target="tpu_custom_call" | custom-call | flops 1912602624 | bytes 3440640 | tf_op jit(solution)/shard_map/pallas_call | solution.py:67
  256.7 3.8 %reshape.139 = bf16[16,2,12288]{2,1,0:T(2,128)(2,1)} reshape(bf16[16,6,64,64]{3,2,1,0:T(8,128)(2,1)} %shard_map.122) | data formatting | bytes 1572864
  260.5 4.3 %all-to-all-start.2 = ((bf16[16,2,12288]{2,1,0:T(2,128)(2,1)}), bf16[16,2,12288]{2,1,0:T(2,128)(2,1)}, u32[]{:S(2)}, u32[]{:S(2)}) async-start(bf16[16,2,12288]{2,1,0:T(2,128)(2,1)} %reshape.139), calls=%async_computation.2 | async-start | bytes 1572864 | tf_op jit(solution)/shard_map/all_to_all | solution.py:147
  265.4 2.0 slice-done
  267.4 5.5 %reshape.112 = bf16[128,9,1536]{2,1,0:T(8,128)(2,1)} reshape(bf16[1536,1152]{1,0:T(8,128)(2,1)S(1)} %slice-done) | data formatting | bytes 7077888 | tf_op jit(solution)/shard_map/reshape | solution.py:122
  272.9 2.8 copy-done
  277.7 3.8 %reshape.140 = bf16[16,6,64,64]{3,2,1,0:T(8,128)(2,1)} reshape(bf16[16,2,12288]{2,1,0:T(2,128)(2,1)} %all-to-all-done.2) | data formatting | bytes 1572864
  281.5 3.3 %fusion.47 = (f32[6,64]{1,0:T(8,128)S(1)}, f32[6,64,1536]{2,1,0:T(8,128)S(1)}) fusion(bf16[16,6,64,64]{3,2,1,0:T(8,128)(2,1)} %reshape.140, bf16[16,64,1536,1]{2,1,3,0:T(8,128)(2,1)S(1)} %bitcast.95, f32[6,1536]{1,0:T(8,128)S(1)} %bitcast.101, bf16[1,6,64,1536]{3,2,1,0:T(8,128)(2,1)} %param.11), kind=kOutput, calls=%fused_computation.74 | convolution fusion | flops 1210318464 | bytes 7509504 | tf_op jit(solution)/shard_map/hprd,hdc->prc/dot_general | solution.py:148
  286.7 2.3 collective-permute-start
  289.8 2.6 collective-permute-done
  (59 shorter events, 16.5 us)
Async XLA Ops:
  7.2 8.0 %copy-start.1 = (bf16[1,6,64,1536]{3,2,1,0:T(8,128)(2,1)S(1)}, bf16[1,6,64,1536]{3,2,1,0:T(8,128)(2,1)}, u32[]{:S(2)}) copy-start(bf16[1,6,64,1536]{3,2,1,0:T(8,128)(2,1)} %param.11) | copy-start | bytes 3538948
  7.2 8.5 %copy-start.6 = (f32[1,6,2,1536]{3,2,1,0:T(2,128)S(1)}, f32[1,6,2,1536]{3,2,1,0:T(2,128)}, u32[]{:S(2)}) copy-start(f32[1,6,2,1536]{3,2,1,0:T(2,128)} %param.14) | copy-start | bytes 221188
  7.2 8.5 %copy-start.4 = (f32[1,6,5,1536]{3,0,2,1:T(1,128)S(1)}, f32[1,6,5,1536]{3,0,2,1:T(1,128)}, u32[]{:S(2)}) copy-start(f32[1,6,5,1536]{3,0,2,1:T(1,128)} %param.13) | copy-start | bytes 552964
  7.2 100.9 %all-gather.4.cloned.1.call-start = ((), (), s32[]{:S(2)}) async-start(), calls=%async_computation.3 | async-start | bytes 25890816 | tf_op jit(solution)/shard_map/all_gather | solution.py:118
  142.7 12.8 %copy-start.2 = (bf16[1,6,12,1536]{3,2,1,0:T(8,128)(2,1)S(1)}, bf16[1,6,12,1536]{3,2,1,0:T(8,128)(2,1)}, u32[]{:S(2)}) copy-start(bf16[1,6,12,1536]{3,2,1,0:T(8,128)(2,1)} %param.12) | copy-start | bytes 663556
  161.6 24.8 %all-to-all-start.1 = ((bf16[16,2,4608]{2,1,0:T(2,128)(2,1)}), bf16[16,2,4608]{2,1,0:T(2,128)(2,1)S(1)}, u32[]{:S(2)}, u32[]{:S(2)}) async-start(bf16[16,2,4608]{2,1,0:T(2,128)(2,1)} %reshape.137), calls=%async_computation.1 | async-start | bytes 589824 | tf_op jit(solution)/shard_map/all_to_all | solution.py:142
  186.4 40.7 %all-to-all-start = ((bf16[16,2,36864]{2,1,0:T(2,128)(2,1)}), bf16[16,2,36864]{2,1,0:T(2,128)(2,1)S(1)}, u32[]{:S(2)}, u32[]{:S(2)}) async-start(bf16[16,2,36864]{2,1,0:T(2,128)(2,1)} %reshape.135), calls=%async_computation | async-start | bytes 4718592 | tf_op jit(solution)/shard_map/all_to_all | solution.py:140
  260.5 17.2 %all-to-all-start.2 = ((bf16[16,2,12288]{2,1,0:T(2,128)(2,1)}), bf16[16,2,12288]{2,1,0:T(2,128)(2,1)}, u32[]{:S(2)}, u32[]{:S(2)}) async-start(bf16[16,2,12288]{2,1,0:T(2,128)(2,1)} %reshape.139), calls=%async_computation.2 | async-start | bytes 1572864 | tf_op jit(solution)/shard_map/all_to_all | solution.py:147
  265.4 2.0 slice-start
  272.9 2.8 copy-start
  275.7 5.8 %slice-start.1 = ((bf16[128,9,1536]{2,1,0:T(8,128)(2,1)}), bf16[128,8,1536]{2,1,0:T(8,128)(2,1)S(1)}, s32[]{:S(2)}) async-start(bf16[128,9,1536]{2,1,0:T(8,128)(2,1)} %reshape.112), calls=%async_computation.5 | async-start | bytes 6291456 | tf_op jit(solution)/shard_map/slice | solution.py:123
  275.7 5.8 %copy-start.9 = (f32[1,6,1,1536]{3,1,2,0:T(8,128)S(1)}, f32[1,6,1,1536]{3,1,2,0:T(8,128)}, u32[]{:S(2)}) copy-start(f32[1,6,1,1536]{3,1,2,0:T(8,128)} %copy.78) | copy-start | bytes 110596
  284.8 1.0 copy-start.3
  284.8 1.0 copy-start.7
  284.8 1.0 copy-start.8
  284.8 7.6 %copy-start.5 = (f32[6,64,32]{1,2,0:T(8,128)S(1)}, f32[6,64,32]{1,2,0:T(8,128)}, u32[]{:S(2)}) copy-start(f32[6,64,32]{1,2,0:T(8,128)} %param.20) | copy-start | bytes 147460
  286.7 5.7 %collective-permute-start = (bf16[6,64,32]{1,2,0:T(8,128)(2,1)S(1)}, bf16[6,64,32]{1,2,0:T(8,128)(2,1)S(1)}, u32[]{:S(2)}, u32[]{:S(2)}) collective-permute-start(bf16[6,64,32]{1,2,0:T(8,128)(2,1)S(1)} %dynamic-slice_convert_fusion), channel_id=1, source_target_pairs={{0,64},{64,0},{1,65},{65,1},{2,66},{66,2},{3,67},{67,3},{4,68},{68... | collective-permute-start | bytes 73736 | tf_op jit(solution)/shard_map/ppermute | solution.py:20
Sparse Core Ops, SparseCore 0:
  11.5 96.5 all-gather.3

commit v13 on v12

--- a/solution.py
+++ b/solution.py
@@ -56,7 +56,7 @@
     o_ref[:, 0] = (acc / totals).astype(o_ref.dtype).reshape(o_ref.shape[0], -1, width)
 
 
-def attend(lengths, img_parts, k_txt, v_txt, block=256):
+def attend(lengths, img_parts, k_txt, v_txt, block=1024):
     sources, batch, _, src_rows, width = img_parts.shape
     rows = sources * src_rows
     n_txt = k_txt.shape[1]
@@ -98,6 +98,7 @@
 ):
     all_axes = ("guid", "xlo", "core", "seq")
     prompts = img_hidden.shape[1]
+    img_rows = img_hidden.shape[2]
     txt_rows = txt_hidden.shape[2]
     model_width = img_hidden.shape[3]
     nseq = lax.axis_size("seq")
@@ -127,16 +128,16 @@
     text_in = modulate(txt_hidden[0], txt_mod[0, :, 0], txt_mod[0, :, 1])
     head_count = attn_width // HD
     per_dev = head_count // nseq
-    img_split = jnp.einsum(
-        "prd,dthe->hptre",
-        image_in,
-        full_img.reshape(-1, 3, nseq, per_dev * HD),
-        preferred_element_type=jnp.float32,
+    qkv_image = jnp.einsum(
+        "prd,de->pre", image_in, full_img, preferred_element_type=jnp.float32
     ).astype(jnp.bfloat16)
     qkv_text = jnp.einsum(
         "prd,de->pre", text_in, full_txt, preferred_element_type=jnp.float32
     ).astype(jnp.bfloat16)
 
+    img_split = jnp.transpose(
+        qkv_image.reshape(prompts, img_rows, 3, nseq, per_dev * HD), (3, 0, 2, 1, 4)
+    )
     img_parts = lax.all_to_all(img_split, "seq", 0, 0, tiled=True)
     txt_split = qkv_text.reshape(prompts, txt_rows, 2, nseq, per_dev * HD)
     txt_heads = lax.all_to_all(txt_split, "seq", 3, 1, tiled=True)

time: 302 us -> 287 us (0.950)
  local copies, waits for them, and re-layouts: 89.8 us -> 80.5 us
  matrix products: 19.2 us -> 15.9 us
    slice x2 -> x0, local copies, waits for them, and re-layouts: 21 us -> none  [block(): full_img = full_all[:, :img_width]]
    reshape x0 -> x2, local copies, waits for them, and re-layouts: none -> 10.5 us  [block(): qkv_image.reshape(prompts, img_rows, 3, nseq, per_dev * HD)]
    dot_general x1, matrix products: 11.1 us -> 7.69 us  [block(): jnp.einsum('prd,de->pre', image_in, full_img, preferred_element_type=jnp....]
    unnamed x31 -> x36, local copies, waits for them, and re-layouts: 54.7 us -> 55.2 us
  transfers between devices with their start and end apart: 5 -> 5, of which waited for: 3 -> 3; matrix products, arithmetic and copies ran while one was open for 12% -> 16% of each run, Pallas kernels for 0% -> 0%
where the time goes in v13:
time: 287 us; the launch traced here: 285 us
  waiting for transfers between devices  122 us (43%)
  local copies, waits for them, and re-layouts  80.5 us (28%)
  Pallas kernels  22.3 us (8%)
  starting transfers between devices  19.7 us (7%)
  matrix products  15.9 us (6%)
  between operations  15 us (5%)
  other arithmetic  8.99 us (3%)
    all_gather x1, waiting for transfers between devices, block(): gathered = lax.all_gather(local_all, all_axes, axis=0, tiled=False)  91 us
    unnamed x36, local copies, waits for them, and re-layouts  55.2 us
    all_to_all x1, waiting for transfers between devices, block(): img_parts = lax.all_to_all(img_split, 'seq', 0, 0, tiled=True)  28.7 us
    pallas_call x1, Pallas kernels, attend(): pl.pallas_call(attend_kernel, grid=(batch, rows // block), in_specs=[pl.B...  22.3 us
    reshape x2, local copies, waits for them, and re-layouts, block(): qkv_image.reshape(prompts, img_rows, 3, nseq, per_dev * HD)  10.5 us
    dot_general x1, matrix products, block(): jnp.einsum('prd,de->pre', image_in, full_img, preferred_element_type=jnp....  7.69 us
    all_to_all x1, starting transfers between devices, block(): img_parts = lax.all_to_all(img_split, 'seq', 0, 0, tiled=True)  7.18 us
    all_to_all x1, starting transfers between devices, block(): txt_heads = lax.all_to_all(txt_split, 'seq', 3, 1, tiled=True)  5.89 us
  transfers between devices with their start and end apart: 5, of which 3 were waited for; matrix products, arithmetic and copies ran while one was open for 16% of the time, Pallas kernels for 0%

profile of v13, /device:TPU:0, one launch (start us, length us, event | category | flops | bytes accessed | tf_op | source)
XLA Modules:
  0.0 284.8 jit_solution(9442636198580202247)
XLA Ops:
  9.7 1.6 maximum_bitcast_fusion
  13.6 1.5 convert_reduce_fusion
  17.1 91.0 %all-gather.4.cloned.1.call-done = bf16[128,12,6272]{2,1,0:T(8,128)(2,1)} async-done(((bf16[1,12,6272]{2,1,0:T(8,128)(2,1)}), bf16[128,12,6272]{2,1,0:T(8,128)(2,1)}) %all-gather.4.cloned.1.call-update) | async-done | bytes 19267600 | tf_op jit(solution)/shard_map/all_gather | solution.py:119
  108.1 26.4 %reshape.126 = bf16[1536,6272]{1,0:T(8,128)(2,1)} reshape(bf16[128,12,6272]{2,1,0:T(8,128)(2,1)} %all-gather.4.cloned.1.call-done) | data formatting | bytes 38535168
  134.5 4.0 %fusion.12 = bf16[6,12,2048]{2,1,0:T(8,128)(2,1)S(1)} fusion(bf16[1536,6272]{1,0:T(8,128)(2,1)} %reshape.126, bf16[1,6,12,1536]{3,2,1,0:T(8,128)(2,1)S(1)} %copy-done.2, f32[6,1536]{1,0:T(8,128)S(1)} %get-tuple-element.19, f32[6,1536]{1,0:T(8,128)S(1)} %get-tuple-element.20, f32[6,12]{1,0:T(8,128)S(1)} %add_rsqrt_fusion.1, ...), kind=kOutput, calls=%fused_computation.20 | convolution fusion | flops 453795840 | bytes 6881856 | tf_op jit(solution)/shard_map/prd,de->pre/dot_general | solution.py:134
  140.7 5.9 %all-to-all-start.1 = ((bf16[16,2,4608]{2,1,0:T(2,128)(2,1)}), bf16[16,2,4608]{2,1,0:T(2,128)(2,1)}, u32[]{:S(2)}, u32[]{:S(2)}) async-start(bf16[16,2,4608]{2,1,0:T(2,128)(2,1)} %reshape.135), calls=%async_computation.1 | async-start | bytes 589824 | tf_op jit(solution)/shard_map/all_to_all | solution.py:143
  146.6 7.7 %fusion.2 = bf16[6,64,3072]{2,1,0:T(8,128)(2,1)S(1)} fusion(bf16[1536,6272]{1,0:T(8,128)(2,1)} %reshape.126, bf16[1,6,64,1536]{3,2,1,0:T(8,128)(2,1)S(1)} %copy-done.1, f32[6,1536]{1,0:T(8,128)} %get-tuple-element.18, f32[6,1536]{1,0:T(8,128)} %get-tuple-element.17, f32[6,64]{1,0:T(8,128)S(1)} %add_rsqrt_fusion.2, f32[6,64]{1,0:T(8,128)S(1)} %broadcast_multiply_fusion.2), kind=kOutput, calls=%fused_computation.5 | convolution fusion | flops 3628597248 | bytes 13077504 | tf_op jit(solution)/shard_map/prd,de->pre/dot_general | solution.py:131
  154.3 4.8 %reshape.109 = bf16[6,64,3,16,64]{4,3,2,1,0:T(8,128)(2,1)} reshape(bf16[6,64,3072]{2,1,0:T(8,128)(2,1)S(1)} %fusion.2) | data formatting | bytes 4718592 | tf_op jit(solution)/shard_map/reshape | solution.py:139
  159.1 5.7 %copy.66 = bf16[6,64,3,16,64]{4,1,2,0,3:T(8,128)(2,1)} copy(bf16[6,64,3,16,64]{4,3,2,1,0:T(8,128)(2,1)} %reshape.109) | data formatting | bytes 4718592 | tf_op jit(solution)/shard_map/reshape | solution.py:139
  164.8 7.8 %reshape.133 = bf16[16,2,36864]{2,1,0:T(2,128)(2,1)} reshape(bf16[16,6,3,64,64]{4,3,2,1,0:T(8,128)(2,1)} %bitcast.100) | data formatting | bytes 4718592
  172.7 7.2 %all-to-all-start = ((bf16[16,2,36864]{2,1,0:T(2,128)(2,1)}), bf16[16,2,36864]{2,1,0:T(2,128)(2,1)S(1)}, u32[]{:S(2)}, u32[]{:S(2)}) async-start(bf16[16,2,36864]{2,1,0:T(2,128)(2,1)} %reshape.133), calls=%async_computation | async-start | bytes 4718592 | tf_op jit(solution)/shard_map/all_to_all | solution.py:141
  179.9 1.4 reshape.136
  184.5 28.7 %all-to-all-done = bf16[16,2,36864]{2,1,0:T(2,128)(2,1)S(1)} async-done(((bf16[16,2,36864]{2,1,0:T(2,128)(2,1)}), bf16[16,2,36864]{2,1,0:T(2,128)(2,1)S(1)}, u32[]{:S(2)}, u32[]{:S(2)}) %all-to-all-start) | async-done | bytes 2359328 | tf_op jit(solution)/shard_map/all_to_all | solution.py:141
  213.3 5.2 %reshape.134.q_ref.ki_ref.vi_ref = bf16[16,6,3,64,64]{4,3,2,1,0:T(8,128)(2,1)} reshape(bf16[16,2,36864]{2,1,0:T(2,128)(2,1)S(1)} %all-to-all-done) | data formatting | bytes 4718592
  218.5 22.3 %shard_map.122 = bf16[16,6,64,64]{3,2,1,0:T(8,128)(2,1)} custom-call(s32[6]{0:T(128)} %bitcast.107, bf16[16,6,3,64,64]{4,3,2,1,0:T(8,128)(2,1)} %reshape.134.q_ref.ki_ref.vi_ref, bf16[16,6,3,64,64]{4,3,2,1,0:T(8,128)(2,1)} %reshape.134.q_ref.ki_ref.vi_ref, bf16[16,6,3,64,64]{4,3,2,1,0:T(8,128)(2,1)} %reshape.134.q_ref.ki_ref.vi_ref, ...), custom_call_target="tpu_custom_call" | custom-call | flops 1912602624 | bytes 3440640 | tf_op jit(solution)/shard_map/pallas_call | solution.py:67
  240.9 3.9 %reshape.137 = bf16[16,2,12288]{2,1,0:T(2,128)(2,1)} reshape(bf16[16,6,64,64]{3,2,1,0:T(8,128)(2,1)} %shard_map.122) | data formatting | bytes 1572864
  244.7 4.3 %all-to-all-start.2 = ((bf16[16,2,12288]{2,1,0:T(2,128)(2,1)}), bf16[16,2,12288]{2,1,0:T(2,128)(2,1)}, u32[]{:S(2)}, u32[]{:S(2)}) async-start(bf16[16,2,12288]{2,1,0:T(2,128)(2,1)} %reshape.137), calls=%async_computation.2 | async-start | bytes 1572864 | tf_op jit(solution)/shard_map/all_to_all | solution.py:148
  250.3 2.0 slice-done
  252.3 5.5 %reshape.111 = bf16[128,9,1536]{2,1,0:T(8,128)(2,1)} reshape(bf16[1536,1152]{1,0:T(8,128)(2,1)S(1)} %slice-done) | data formatting | bytes 7077888 | tf_op jit(solution)/shard_map/reshape | solution.py:123
  257.8 2.8 copy-done
  262.6 3.8 %reshape.138 = bf16[16,6,64,64]{3,2,1,0:T(8,128)(2,1)} reshape(bf16[16,2,12288]{2,1,0:T(2,128)(2,1)} %all-to-all-done.2) | data formatting | bytes 1572864
  266.4 3.3 %fusion.44 = (f32[6,64]{1,0:T(8,128)S(1)}, f32[6,64,1536]{2,1,0:T(8,128)S(1)}) fusion(bf16[16,6,64,64]{3,2,1,0:T(8,128)(2,1)} %reshape.138, bf16[16,64,1536,1]{2,1,3,0:T(8,128)(2,1)S(1)} %bitcast.101, f32[6,1536]{1,0:T(8,128)S(1)} %bitcast.106, bf16[1,6,64,1536]{3,2,1,0:T(8,128)(2,1)} %param.11), kind=kOutput, calls=%fused_computation.73 | convolution fusion | flops 1210318464 | bytes 7509504 | tf_op jit(solution)/shard_map/hprd,hdc->prc/dot_general | solution.py:149
  271.6 2.3 collective-permute-start
  274.7 2.6 collective-permute-done
  (65 shorter events, 18.0 us)
Async XLA Ops:
  7.2 8.0 %copy-start.1 = (bf16[1,6,64,1536]{3,2,1,0:T(8,128)(2,1)S(1)}, bf16[1,6,64,1536]{3,2,1,0:T(8,128)(2,1)}, u32[]{:S(2)}) copy-start(bf16[1,6,64,1536]{3,2,1,0:T(8,128)(2,1)} %param.11) | copy-start | bytes 3538948
  7.2 8.5 %copy-start.9 = (f32[1,6,2,1536]{3,2,1,0:T(2,128)S(1)}, f32[1,6,2,1536]{3,2,1,0:T(2,128)}, u32[]{:S(2)}) copy-start(f32[1,6,2,1536]{3,2,1,0:T(2,128)} %param.14) | copy-start | bytes 221188
  7.2 8.5 %copy-start.4 = (f32[1,6,5,1536]{3,0,2,1:T(1,128)S(1)}, f32[1,6,5,1536]{3,0,2,1:T(1,128)}, u32[]{:S(2)}) copy-start(f32[1,6,5,1536]{3,0,2,1:T(1,128)} %param.13) | copy-start | bytes 552964
  7.2 100.9 %all-gather.4.cloned.1.call-start = ((), (), s32[]{:S(2)}) async-start(), calls=%async_computation.3 | async-start | bytes 25890816 | tf_op jit(solution)/shard_map/all_gather | solution.py:119
  17.0 117.5 %copy-start.2 = (bf16[1,6,12,1536]{3,2,1,0:T(8,128)(2,1)S(1)}, bf16[1,6,12,1536]{3,2,1,0:T(8,128)(2,1)}, u32[]{:S(2)}) copy-start(bf16[1,6,12,1536]{3,2,1,0:T(8,128)(2,1)} %param.12) | copy-start | bytes 663556
  140.7 32.0 %all-to-all-start.1 = ((bf16[16,2,4608]{2,1,0:T(2,128)(2,1)}), bf16[16,2,4608]{2,1,0:T(2,128)(2,1)}, u32[]{:S(2)}, u32[]{:S(2)}) async-start(bf16[16,2,4608]{2,1,0:T(2,128)(2,1)} %reshape.135), calls=%async_computation.1 | async-start | bytes 589824 | tf_op jit(solution)/shard_map/all_to_all | solution.py:143
  172.7 40.6 %all-to-all-start = ((bf16[16,2,36864]{2,1,0:T(2,128)(2,1)}), bf16[16,2,36864]{2,1,0:T(2,128)(2,1)S(1)}, u32[]{:S(2)}, u32[]{:S(2)}) async-start(bf16[16,2,36864]{2,1,0:T(2,128)(2,1)} %reshape.133), calls=%async_computation | async-start | bytes 4718592 | tf_op jit(solution)/shard_map/all_to_all | solution.py:141
  240.8 8.2 %copy-start.7 = (f32[1,6,1,1536]{3,0,2,1:T(1,128)S(1)}, f32[1,6,1,1536]{3,0,2,1:T(1,128)}, u32[]{:S(2)}) copy-start(f32[1,6,1,1536]{3,0,2,1:T(1,128)} %get-tuple-element.8) | copy-start | bytes 110596
  240.9 8.8 %copy-start.5 = (f32[1,6,1,1536]{3,0,2,1:T(1,128)S(1)}, f32[1,6,1,1536]{3,0,2,1:T(1,128)}, u32[]{:S(2)}) copy-start(f32[1,6,1,1536]{3,0,2,1:T(1,128)} %get-tuple-element.6) | copy-start | bytes 110596
  240.9 8.8 %copy-start.6 = (f32[1,6,1,1536]{3,0,2,1:T(1,128)S(1)}, f32[1,6,1,1536]{3,0,2,1:T(1,128)}, u32[]{:S(2)}) copy-start(f32[1,6,1,1536]{3,0,2,1:T(1,128)} %get-tuple-element.9) | copy-start | bytes 110596
  244.7 17.9 %all-to-all-start.2 = ((bf16[16,2,12288]{2,1,0:T(2,128)(2,1)}), bf16[16,2,12288]{2,1,0:T(2,128)(2,1)}, u32[]{:S(2)}, u32[]{:S(2)}) async-start(bf16[16,2,12288]{2,1,0:T(2,128)(2,1)} %reshape.137), calls=%async_computation.2 | async-start | bytes 1572864 | tf_op jit(solution)/shard_map/all_to_all | solution.py:148
  250.3 2.0 slice-start
  257.8 2.8 copy-start
  260.6 5.8 %slice-start.1 = ((bf16[128,9,1536]{2,1,0:T(8,128)(2,1)}), bf16[128,8,1536]{2,1,0:T(8,128)(2,1)S(1)}, s32[]{:S(2)}) async-start(bf16[128,9,1536]{2,1,0:T(8,128)(2,1)} %reshape.111), calls=%async_computation.5 | async-start | bytes 6291456 | tf_op jit(solution)/shard_map/slice | solution.py:124
  260.6 5.8 %copy-start.10 = (f32[1,6,1,1536]{3,1,2,0:T(8,128)S(1)}, f32[1,6,1,1536]{3,1,2,0:T(8,128)}, u32[]{:S(2)}) copy-start(f32[1,6,1,1536]{3,1,2,0:T(8,128)} %copy.69) | copy-start | bytes 110596
  269.7 1.0 copy-start.3
  269.7 1.0 copy-start.11
  269.7 1.0 copy-start.12
  269.7 7.6 %copy-start.8 = (f32[6,64,32]{1,2,0:T(8,128)S(1)}, f32[6,64,32]{1,2,0:T(8,128)}, u32[]{:S(2)}) copy-start(f32[6,64,32]{1,2,0:T(8,128)} %param.20) | copy-start | bytes 147460
  271.6 5.7 %collective-permute-start = (bf16[6,64,32]{1,2,0:T(8,128)(2,1)S(1)}, bf16[6,64,32]{1,2,0:T(8,128)(2,1)S(1)}, u32[]{:S(2)}, u32[]{:S(2)}) collective-permute-start(bf16[6,64,32]{1,2,0:T(8,128)(2,1)S(1)} %dynamic-slice_convert_fusion), channel_id=1, source_target_pairs={{0,64},{64,0},{1,65},{65,1},{2,66},{66,2},{3,67},{67,3},{4,68},{68... | collective-permute-start | bytes 73736 | tf_op jit(solution)/shard_map/ppermute | solution.py:20
Sparse Core Ops, SparseCore 0:
  11.5 96.5 all-gather.3
